TPU v7x, 256 devices: a whole 4x4x8 slice. The times are simulated.
256 devices in a mesh: orbit: 16 (over z, core), space: 16 (over x, y).
Axes of the slice: x: 4, y: 4, z: 8, core: 2. Of those that a mesh axis runs over, the one named last changes fastest.
Arguments:
- queries: bfloat16 [16, 32, 64, 2240], P('orbit', 'space'), may hold values from -6 to 6
- keys_in: bfloat16 [16, 32, 64, 2240], P('orbit', 'space'), may hold values from -6 to 6
- values: bfloat16 [16, 32, 64, 2240], P('orbit', 'space'), may hold values from -6 to 6
- conv_weight: bfloat16 [3, 3, 2240], replicated, may hold values from -2 to 2
- grad_out: bfloat16 [16, 32, 64, 2240], P('orbit', 'space'), may hold values from -6 to 6
Outputs:
- attended: bfloat16 [16, 32, 64, 2240], P('orbit', 'space')
- grad_query: bfloat16 [16, 32, 64, 2240], P('orbit', 'space')
- grad_key: bfloat16 [16, 32, 64, 2240], P('orbit', 'space')
- grad_value: bfloat16 [16, 32, 64, 2240], P('orbit', 'space')
All inputs are finite; a program needn't handle non-finite values.
Results may differ from a plain program's by a relative error of at most 0.0079.
Values may be sent and summed in bfloat16 or wider, within the bound.
No kernel may reach another device: no remote copies, remote signals or barrier semaphores. Data moves between devices by JAX's collectives and lax.ppermute only.
A program may use at most 128 MiB of HBM per device.

v0:
```python
import jax
import jax.numpy as jnp
from jax import lax
from jax.sharding import PartitionSpec as P

HEADS = 20
HD = 112


def prefix(part, axis, combine, identity, reverse):
    count = lax.axis_size(axis)
    place = lax.axis_index(axis)
    ahead = count - 1 - place if reverse else place
    gathered = jax.tree.map(lambda a: lax.all_gather(a, axis), part)
    state = jax.tree.map(lambda a, e: jnp.zeros_like(a) + jnp.asarray(e, a.dtype), part, identity)

    def one(turn, state):
        source = count - 1 - turn if reverse else turn
        return combine(
            state, jax.tree.map(lambda a: lax.dynamic_index_in_dim(a, source, 0, False), gathered)
        )

    return lax.fori_loop(0, ahead, one, state)


def padded(cells, sides, width):
    for axis, dim in sides:
        count = lax.axis_size(axis)
        ends = count - 1
        head = lax.slice_in_dim(cells, 0, width, axis=dim)
        tail = lax.slice_in_dim(cells, cells.shape[dim] - width, cells.shape[dim], axis=dim)
        cells = jnp.concatenate(
            [
                lax.ppermute(tail, axis, [(i, (i + 1) % count) for i in range(ends)]),
                cells,
                lax.ppermute(head, axis, [((i + 1) % count, i) for i in range(ends)]),
            ],
            axis=dim,
        )
    return cells


def add_pair(earlier, later):
    return (earlier[0] + later[0], earlier[1] + later[1])


def running(source_field, reverse):
    if reverse:
        return jnp.flip(jnp.cumsum(jnp.flip(source_field, 0), 0), 0)
    return jnp.cumsum(source_field, 0)


def scan_before(totals, reverse):
    identity = (jnp.zeros_like(totals[0]), jnp.zeros_like(totals[1]))
    return prefix(totals, "orbit", add_pair, identity, reverse)


def finish(flat_state, flat_norm, before, reverse, counts):
    state_sum = before[0][None] + running(flat_state, reverse)
    norm_sum = before[1][None] + running(flat_norm, reverse)
    if counts is not None:
        state_sum = state_sum / counts[:, None]
        norm_sum = norm_sum / counts[:, None]
    return (state_sum.astype(jnp.bfloat16), norm_sum.astype(jnp.bfloat16))


def spread_states(state_part, norm_part, reverse, counts):
    view_count = state_part.shape[0]
    flat_state = state_part.reshape(view_count, -1)
    flat_norm = norm_part.reshape(view_count, -1)
    whole_state, whole_norm = lax.psum((flat_state, flat_norm), "space")
    totals = (jnp.sum(whole_state, 0), jnp.sum(whole_norm, 0))
    before = scan_before(totals, reverse)
    state_b, norm_b = finish(whole_state, whole_norm, before, reverse, counts)
    return (state_b.reshape(state_part.shape), norm_b.reshape(norm_part.shape))


def on_device(queries, keys_in, values, conv_weight, grad_out):
    view_count, row_count, col_count, feature_width = queries.shape
    token_count = row_count * col_count
    value_rows, grad_rows = (
        padded(values, (("space", 1),), 1),
        padded(grad_out, (("space", 1),), 1),
    )
    heads_shape = (view_count, token_count, HEADS, HD)
    query_feat = jax.nn.relu(queries).reshape(heads_shape)
    key_feat = jax.nn.relu(keys_in).reshape(heads_shape)
    value_heads = values.reshape(heads_shape)
    grad_heads = grad_out.reshape(heads_shape)
    global_view = lax.axis_index("orbit") * view_count + jnp.arange(view_count)
    counts = (global_view.astype(jnp.float32) + 1.0) * float(
        row_count * lax.axis_size("space") * col_count
    )
    state_part = jnp.einsum(
        "vthd,vthe->vhde", key_feat, value_heads, preferred_element_type=jnp.float32
    )
    norm_part = jnp.sum(key_feat, axis=1, dtype=jnp.float32)
    state_b, norm_b = spread_states(state_part, norm_part, False, counts)
    numerator = jnp.einsum(
        "vthd,vhde->vthe", query_feat, state_b, preferred_element_type=jnp.float32
    )
    denominator = (
        jnp.einsum("vthd,vhd->vth", query_feat, norm_b, preferred_element_type=jnp.float32) + 1.0
    )
    weight_wide = conv_weight.astype(jnp.float32)
    value_pad = jnp.pad(value_rows, ((0, 0), (0, 0), (1, 1), (0, 0)))
    grad_pad = jnp.pad(grad_rows, ((0, 0), (0, 0), (1, 1), (0, 0)))
    conv_term = jnp.zeros(queries.shape, jnp.float32)
    conv_grad = jnp.zeros(queries.shape, jnp.float32)
    for row_step in range(3):
        for col_step in range(3):
            conv_term = conv_term + weight_wide[row_step, col_step] * value_pad[
                :, row_step : row_step + row_count, col_step : col_step + col_count
            ].astype(jnp.float32)
            conv_grad = conv_grad + weight_wide[row_step, col_step] * grad_pad[
                :, 2 - row_step : 2 - row_step + row_count, 2 - col_step : 2 - col_step + col_count
            ].astype(jnp.float32)
    attention = numerator / denominator[..., None]
    attended = (attention.reshape(queries.shape) + conv_term).astype(jnp.bfloat16)
    grad_wide = grad_heads.astype(jnp.float32)
    numerator_grad = (grad_wide / denominator[..., None]).astype(jnp.bfloat16)
    denominator_grad = (-jnp.sum(grad_wide * numerator, -1) / (denominator * denominator)).astype(
        jnp.bfloat16
    )
    query_grad = jnp.einsum(
        "vthe,vhde->vthd", numerator_grad, state_b, preferred_element_type=jnp.float32
    )
    query_grad = (
        query_grad
        + denominator_grad.astype(jnp.float32)[..., None] * norm_b.astype(jnp.float32)[:, None]
    )
    grad_query = (
        jnp.where(queries.reshape(heads_shape) > 0, query_grad, 0.0)
        .astype(jnp.bfloat16)
        .reshape(queries.shape)
    )
    state_grad = jnp.einsum(
        "vthd,vthe->vhde", query_feat, numerator_grad, preferred_element_type=jnp.float32
    )
    norm_grad = jnp.einsum(
        "vthd,vth->vhd", query_feat, denominator_grad, preferred_element_type=jnp.float32
    )
    back_state, back_norm = spread_states(
        state_grad / counts[:, None, None, None], norm_grad / counts[:, None, None], True, None
    )
    key_grad = jnp.einsum(
        "vthe,vhde->vthd", value_heads, back_state, preferred_element_type=jnp.float32
    )
    key_grad = key_grad + back_norm.astype(jnp.float32)[:, None]
    grad_key = (
        jnp.where(keys_in.reshape(heads_shape) > 0, key_grad, 0.0)
        .astype(jnp.bfloat16)
        .reshape(queries.shape)
    )
    value_grad = (
        jnp.einsum(
            "vthd,vhde->vthe", key_feat, back_state, preferred_element_type=jnp.float32
        ).reshape(queries.shape)
        + conv_grad
    )
    grad_value = value_grad.astype(jnp.bfloat16)
    return (attended, grad_query, grad_key, grad_value)


def solution(mesh):
    placed = (
        P("orbit", "space", None, None),
        P("orbit", "space", None, None),
        P("orbit", "space", None, None),
        P(),
        P("orbit", "space", None, None),
    )
    return jax.shard_map(
        on_device,
        mesh=mesh,
        in_specs=placed,
        out_specs=(
            P("orbit", "space", None, None),
            P("orbit", "space", None, None),
            P("orbit", "space", None, None),
            P("orbit", "space", None, None),
        ),
        check_vma=False,
    )
```

profile of v0, /device:TPU:0, one launch (start us, length us, event | category | flops | bytes accessed | tf_op | source)
XLA Modules:
  0.0 655.8 jit_solution(9873634601114750085)
XLA Ops:
  11.4 2.7 reshape.250
  14.2 98.7 %all-reduce.5.cloned.1.call-done = f32[1,250880]{1,0:T(1,128)} async-done(((f32[1,250880]{1,0:T(1,128)}), f32[1,250880]{1,0:T(1,128)}) %all-reduce.5.cloned.1.call-update) | async-done | bytes 1003536 | tf_op jit(solution)/shard_map/psum | solution.py:71
  113.1 39.3 %psum.29 = f32[1,2240]{1,0:T(1,128)S(1)} all-reduce(f32[1,2240]{1,0:T(1,128)S(1)} %reshape.251), channel_id=1, replica_groups=mesh['orbit'=16,'space'=16] {'space'}, use_global_device_ids=true, to_apply=%region_2.3 | all-reduce | flops 2240 | bytes 17920 | tf_op jit(solution)/shard_map/psum | solution.py:71
  152.5 19.1 %all-gather.1 = f32[16,1,2240]{2,1,0:T(1,128)S(1)} all-gather(f32[1,1,2240]{2,1,0:T(1,128)S(1)} %bitcast.124), channel_id=1, replica_groups=mesh['orbit'=16,'space'=16] {'orbit'}, dimensions={0}, use_global_device_ids=true | all-gather | bytes 152320 | tf_op jit(solution)/shard_map/all_gather | solution.py:14
  173.6 1.9 reshape.262
  175.5 31.2 %all-gather.7.cloned.1.call-done = f32[16,1,250880]{2,1,0:T(1,128)} async-done(((f32[1,1,250880]{2,1,0:T(1,128)}), f32[16,1,250880]{2,1,0:T(1,128)}) %all-gather.7.cloned.1.call-update) | async-done | bytes 16056336 | tf_op jit(solution)/shard_map/all_gather | solution.py:14
  206.7 12.4 %copy.85 = f32[16,1,250880]{2,0,1:T(8,128)} copy(f32[16,1,250880]{2,1,0:T(1,128)} %all-gather.7.cloned.1.call-done) | data formatting | bytes 32112640
  219.2 11.0 %while.26 = (s32[]{:T(128)}, f32[250880]{0:T(1024)S(1)}, f32[2240]{0:T(1024)S(1)}, s32[]{:T(128)}, f32[16,250880]{1,0:T(8,128)}, /*index=5*/f32[16,2240]{1,0:T(8,128)}, s32[]{:T(128)}, s32[]{:T(128)}, s32[]{:T(128)}) while((s32[]{:T(128)}, f32[250880]{0:T(1024)S(1)}, f32[2240]{0:T(1024)S(1)}, s32[]{:T(128)}, f32[16,250880]{1,0:T(8,128)}, ...), condition=%wide.region_4.5_spmd, body=%wide.region_3.4_spmd.sunk | while | flops 253125 | bytes 5062535 | solution.py:23
  231.4 2.8 divide_convert_fusion
  234.2 2.3 copy.49
  236.5 2.5 convolution_divide_fusion
  239.0 4.0 reshape.257
  243.0 168.2 %all-reduce.7.cloned.1.call-done = f32[1,250880]{1,0:T(1,128)} async-done(((f32[1,250880]{1,0:T(1,128)}), f32[1,250880]{1,0:T(1,128)}) %all-reduce.7.cloned.1.call-update) | async-done | bytes 1003536 | tf_op jit(solution)/shard_map/psum | solution.py:71
  412.0 3.7 collective-permute-start.2
  417.9 5.3 collective-permute-start
  426.2 1.9 reshape.263
  428.1 2.9 copy.50
  437.6 2.5 select_maximum_fusion.2
  440.8 12.2 %convert_reduce_fusion.2 = bf16[250880]{0:T(1024)(128)(2,1)} fusion(f32[1,250880]{1,0:T(1,128)S(1)} %bitcast.117, f32[1,250880]{1,0:T(1,128)} %all-reduce.5.cloned.1.call-done, f32[]{:T(128)S(6)} %mul.179), kind=kLoop, calls=%fused_computation.32 | loop fusion | flops 752640 | bytes 2508804 | tf_op jit(solution)/shard_map/convert_element_type | solution.py:64
  453.1 1.7 reshape.252
  454.8 2.9 multiply_reduce_fusion
  458.3 41.1 %psum.31 = f32[1,2240]{1,0:T(1,128)S(1)} all-reduce(f32[1,2240]{1,0:T(1,128)S(1)} %reshape.258), channel_id=1, replica_groups=mesh['orbit'=16,'space'=16] {'space'}, use_global_device_ids=true, to_apply=%region_7.8 | all-reduce | flops 2240 | bytes 17920 | tf_op jit(solution)/shard_map/psum | solution.py:71
  499.4 17.9 %all-gather.3 = f32[16,1,2240]{2,1,0:T(1,128)S(1)} all-gather(f32[1,1,2240]{2,1,0:T(1,128)S(1)} %bitcast.125), channel_id=1, replica_groups=mesh['orbit'=16,'space'=16] {'orbit'}, dimensions={0}, use_global_device_ids=true | all-gather | bytes 152320 | tf_op jit(solution)/shard_map/all_gather | solution.py:14
  518.0 2.9 copy.47
  520.8 2.7 reshape.255
  523.6 2.3 fusion.8
  528.9 4.8 add_convert_fusion.1
  533.8 12.4 %copy.84 = f32[16,1,250880]{2,0,1:T(8,128)} copy(f32[16,1,250880]{2,1,0:T(1,128)} %all-gather.9.cloned.1.call-done) | data formatting | bytes 32112640
  546.3 73.9 %while.27 = (s32[]{:T(128)}, f32[250880]{0:T(1024)S(1)}, f32[2240]{0:T(1024)S(1)}, s32[]{:T(128)}, f32[16,250880]{1,0:T(8,128)}, /*index=5*/f32[16,2240]{1,0:T(8,128)}, s32[]{:T(128)}, s32[]{:T(128)}, s32[]{:T(128)}, s32[]{:T(128)}) while((s32[]{:T(128)}, f32[250880]{0:T(1024)S(1)}, f32[2240]{0:T(1024)S(1)}, s32[]{:T(128)}, ...), condition=%wide.region_9.10_spmd, body=%wide.region_8.9_spmd.sunk | while | flops 253126 | bytes 5062555 | solution.py:23
  546.3 3.7 constant_dynamic-slice_fusion.5
  551.2 3.7 constant_dynamic-slice_fusion.5
  556.2 3.7 constant_dynamic-slice_fusion.5
  561.1 3.7 constant_dynamic-slice_fusion.5
  566.0 3.7 constant_dynamic-slice_fusion.5
  570.9 3.7 constant_dynamic-slice_fusion.5
  575.9 3.7 constant_dynamic-slice_fusion.5
  580.8 3.7 constant_dynamic-slice_fusion.5
  585.7 3.7 constant_dynamic-slice_fusion.5
  590.7 3.7 constant_dynamic-slice_fusion.5
  595.6 3.7 constant_dynamic-slice_fusion.5
  600.5 3.7 constant_dynamic-slice_fusion.5
  605.4 3.7 constant_dynamic-slice_fusion.5
  610.4 3.7 constant_dynamic-slice_fusion.5
  615.3 3.7 constant_dynamic-slice_fusion.5
  620.2 12.3 %convert_reduce_fusion.1 = bf16[250880]{0:T(1024)(128)(2,1)} fusion(f32[1,250880]{1,0:T(1,128)S(1)} %bitcast.116, f32[1,250880]{1,0:T(1,128)} %all-reduce.7.cloned.1.call-done), kind=kLoop, calls=%fused_computation.31 | loop fusion | flops 501760 | bytes 2508800 | tf_op jit(solution)/shard_map/convert_element_type | solution.py:64
  635.6 2.9 copy.60
  638.5 2.8 reshape.261
  645.7 3.3 add_convert_fusion
  (176 shorter events, 49.9 us)
Async XLA Ops:
  7.2 105.7 %all-reduce.5.cloned.1.call-start = ((), (), s32[]{:S(2)}) async-start(), calls=%async_computation | async-start | bytes 2007040 | tf_op jit(solution)/shard_map/psum | solution.py:71
  8.3 1.3 copy-start.1
  9.6 1.3 copy-start.3
  11.0 3.1 copy-start.9
  14.1 98.9 %copy-start.2 = (bf16[1,2,64,2240]{3,2,1,0:T(8,128)(2,1)S(1)}, bf16[1,2,64,2240]{3,2,1,0:T(8,128)(2,1)}, u32[]{:S(2)}) copy-start(bf16[1,2,64,2240]{3,2,1,0:T(8,128)(2,1)} %param.10) | copy-start | bytes 1720324
  14.1 158.1 %copy-start.7 = (bf16[1,2,64,2240]{3,2,1,0:T(8,128)(2,1)S(1)}, bf16[1,2,64,2240]{3,2,1,0:T(8,128)(2,1)}, u32[]{:S(2)}) copy-start(bf16[1,2,64,2240]{3,2,1,0:T(8,128)(2,1)} %param.9) | copy-start | bytes 1720324
  14.1 192.6 %all-gather.7.cloned.1.call-start = ((), (), s32[]{:S(2)}) async-start(), calls=%async_computation.2 | async-start | bytes 17059840 | tf_op jit(solution)/shard_map/all_gather | solution.py:14
  112.9 298.3 %all-reduce.7.cloned.1.call-start = ((), (), s32[]{:S(2)}) async-start(), calls=%async_computation.1 | async-start | bytes 2007040 | tf_op jit(solution)/shard_map/psum | solution.py:71
  172.3 1.3 copy-start
  173.6 62.9 %copy-start.5 = (bf16[128,20,112]{0,2,1:T(8,128)(2,1)}, bf16[128,20,112]{0,2,1:T(8,128)(2,1)S(1)}, u32[]{:S(2)}) copy-start(bf16[128,20,112]{0,2,1:T(8,128)(2,1)S(1)} %copy.46) | copy-start | bytes 1720324
  230.7 0.6 copy-start.27
  231.3 2.9 copy-start.32
  243.0 290.8 %all-gather.9.cloned.1.call-start = ((), (), s32[]{:S(2)}) async-start(), calls=%async_computation.3 | async-start | bytes 17059840 | tf_op jit(solution)/shard_map/all_gather | solution.py:14
  412.0 13.2 %copy-start.8 = (bf16[1,2,64,2240]{3,2,1,0:T(8,128)(2,1)S(1)}, bf16[1,2,64,2240]{3,2,1,0:T(8,128)(2,1)}, u32[]{:S(2)}) copy-start(bf16[1,2,64,2240]{3,2,1,0:T(8,128)(2,1)} %param.9) | copy-start | bytes 1720324
  412.0 24.1 %collective-permute-start.2 = (bf16[1,1,64,2240]{3,2,1,0:T(8,128)(2,1)}, bf16[1,1,64,2240]{3,2,1,0:T(8,128)(2,1)}, u32[]{:S(2)}, u32[]{:S(2)}) collective-permute-start(bf16[1,1,64,2240]{3,2,1,0:T(8,128)(2,1)} %get-tuple-element.164), channel_id=1, source_target_pairs={{0,1},{1,2},{2,3},{3,4},{4,5},{5,6},{6,7},{7,8},{8,9},{9,10},{10,1... | collective-permute-start | bytes 860168 | tf_op jit(solution)/shard_map/ppermute | solution.py:34
  415.7 20.5 %collective-permute-start.3 = (bf16[1,1,64,2240]{3,2,1,0:T(8,128)(2,1)}, bf16[1,1,64,2240]{3,2,1,0:T(8,128)(2,1)}, u32[]{:S(2)}, u32[]{:S(2)}) collective-permute-start(bf16[1,1,64,2240]{3,2,1,0:T(8,128)(2,1)} %get-tuple-element.165), channel_id=1, source_target_pairs={{1,0},{2,1},{3,2},{4,3},{5,4},{6,5},{7,6},{8,7},{9,8},{10,9},{11,1... | collective-permute-start | bytes 860168 | tf_op jit(solution)/shard_map/ppermute | solution.py:36
  417.9 19.8 %collective-permute-start = (bf16[1,1,64,2240]{3,2,1,0:T(8,128)(2,1)}, bf16[1,1,64,2240]{3,2,1,0:T(8,128)(2,1)}, u32[]{:S(2)}, u32[]{:S(2)}) collective-permute-start(bf16[1,1,64,2240]{3,2,1,0:T(8,128)(2,1)} %get-tuple-element.166), channel_id=1, source_target_pairs={{0,1},{1,2},{2,3},{3,4},{4,5},{5,6},{6,7},{7,8},{8,9},{9,10},{10,1... | collective-permute-start | bytes 860168 | tf_op jit(solution)/shard_map/ppermute | solution.py:34
  423.1 14.5 %collective-permute-start.1 = (bf16[1,1,64,2240]{3,2,1,0:T(8,128)(2,1)}, bf16[1,1,64,2240]{3,2,1,0:T(8,128)(2,1)}, u32[]{:S(2)}, u32[]{:S(2)}) collective-permute-start(bf16[1,1,64,2240]{3,2,1,0:T(8,128)(2,1)} %get-tuple-element.167), channel_id=1, source_target_pairs={{1,0},{2,1},{3,2},{4,3},{5,4},{6,5},{7,6},{8,7},{9,8},{10,9},{11,1... | collective-permute-start | bytes 860168 | tf_op jit(solution)/shard_map/ppermute | solution.py:36
  428.1 2.9 copy-start.31
  428.1 2.9 copy-start.12
  431.0 2.2 copy-start.11
  454.8 2.9 copy-start.28
  454.8 2.9 copy-start.6
  499.4 18.6 %copy-start.29 = (f32[1,2240]{1,0:T(1,128)}, f32[1,2240]{1,0:T(1,128)S(1)}, u32[]{:S(2)}) copy-start(f32[1,2240]{1,0:T(1,128)S(1)} %psum.31) | copy-start | bytes 26884
  520.8 2.7 copy-start.33
  520.8 2.8 copy-start.14
  525.9 3.0 copy-start.15
  525.9 3.0 copy-start.17
  525.9 3.0 copy-start.19
  525.9 3.0 copy-start.21
  525.9 3.0 copy-start.23
  525.9 3.0 copy-start.25
  620.2 14.0 %copy-start.4 = (bf16[128,20,112]{0,2,1:T(8,128)(2,1)S(1)}, bf16[128,20,112]{0,2,1:T(8,128)(2,1)}, u32[]{:S(2)}) copy-start(bf16[128,20,112]{0,2,1:T(8,128)(2,1)} %copy-done.3) | copy-start | bytes 1720324
  638.5 2.8 copy-start.30
  638.5 2.9 copy-start.10
  638.5 2.9 copy-start.13
  642.6 3.0 copy-start.16
  642.6 3.0 copy-start.18
  642.6 3.0 copy-start.20
  642.6 3.0 copy-start.22
  642.6 3.0 copy-start.24
  642.7 3.0 copy-start.26
Sparse Core Ops, SparseCore 0:
  14.2 98.5 all-reduce.4
  114.7 91.9 all-gather.6
  243.1 168.0 all-reduce.6
  412.9 91.1 all-gather.8
where the time goes:
time: 664 us; the launch traced here: 656 us
  waiting for transfers between devices  298 us (45%)
  local copies, waits for them, and re-layouts  145 us (22%)
  blocking collectives  117 us (18%)
  other arithmetic  45.8 us (7%)
  between operations  14.6 us (2%)
  loops' own time  11.7 us (2%)
  starting transfers between devices  11.6 us (2%)
  matrix products  11.5 us (2%)
    psum x2, waiting for transfers between devices, spread_states(): whole_state, whole_norm = lax.psum((flat_state, flat_norm), 'space')  267 us
    psum x2, blocking collectives, spread_states(): whole_state, whole_norm = lax.psum((flat_state, flat_norm), 'space')  80.4 us
    dynamic_slice x30, local copies, waits for them, and re-layouts, one(): lax.dynamic_index_in_dim(a, source, 0, False)  69.9 us
    all_gather x2, blocking collectives, prefix(): gathered = jax.tree.map(lambda a: lax.all_gather(a, axis), part)  37 us
    all_gather x2, waiting for transfers between devices, prefix(): gathered = jax.tree.map(lambda a: lax.all_gather(a, axis), part)  31.2 us
    unnamed x72, local copies, waits for them, and re-layouts  27 us
    convert_element_type x3, other arithmetic, finish(): return (state_sum.astype(jnp.bfloat16), norm_sum.astype(jnp.bfloat16))  24.6 us
  transfers between devices with their start and end apart: 8, of which 3 were waited for; matrix products, arithmetic and copies ran while one was open for 9% of the time, Pallas kernels for 0%

commit v1 on v0

v1 whole, which is shorter than its diff:
```python
import jax
import jax.numpy as jnp
from jax import lax
from jax.sharding import PartitionSpec as P

HEADS = 20
HD = 112


def padded(cells, sides, width):
    for axis, dim in sides:
        count = lax.axis_size(axis)
        ends = count - 1
        head = lax.slice_in_dim(cells, 0, width, axis=dim)
        tail = lax.slice_in_dim(cells, cells.shape[dim] - width, cells.shape[dim], axis=dim)
        cells = jnp.concatenate(
            [
                lax.ppermute(tail, axis, [(i, (i + 1) % count) for i in range(ends)]),
                cells,
                lax.ppermute(head, axis, [((i + 1) % count, i) for i in range(ends)]),
            ],
            axis=dim,
        )
    return cells


def spread_states(state_part, norm_part, reverse, counts):
    space = lax.axis_size("space")
    orbit = lax.axis_size("orbit")
    place = lax.axis_index("orbit")
    flat = jnp.concatenate([state_part.reshape(-1), norm_part.reshape(-1)])
    total = flat.shape[0]
    chunk = -(-total // (space * 128)) * 128
    flat = jnp.pad(flat, (0, chunk * space - total))
    pieces = lax.all_to_all(flat.reshape(space, chunk), "space", 0, 0, tiled=True)
    whole = jnp.sum(pieces, axis=0)
    if not reverse:
        gathered = lax.all_gather(whole, "orbit")
        views = jnp.arange(orbit)
        keep = views <= place
        summed = jnp.sum(jnp.where(keep[:, None], gathered, 0.0), axis=0)
        summed = summed / counts
    else:
        whole = whole / counts
        gathered = lax.all_gather(whole, "orbit")
        views = jnp.arange(orbit)
        keep = views >= place
        summed = jnp.sum(jnp.where(keep[:, None], gathered, 0.0), axis=0)
    rounded = summed.astype(jnp.bfloat16)
    full = lax.all_gather(rounded, "space", tiled=True)[:total]
    size = state_part.size
    return full[:size].reshape(state_part.shape), full[size:].reshape(norm_part.shape)


def on_device(queries, keys_in, values, conv_weight, grad_out):
    view_count, row_count, col_count, feature_width = queries.shape
    token_count = row_count * col_count
    value_rows, grad_rows = (
        padded(values, (("space", 1),), 1),
        padded(grad_out, (("space", 1),), 1),
    )
    heads_shape = (token_count, HEADS, HD)
    query_feat = jax.nn.relu(queries).reshape(heads_shape)
    key_feat = jax.nn.relu(keys_in).reshape(heads_shape)
    value_heads = values.reshape(heads_shape)
    grad_heads = grad_out.reshape(heads_shape)
    place = lax.axis_index("orbit")
    count = (place.astype(jnp.float32) + 1.0) * float(
        row_count * lax.axis_size("space") * col_count
    )
    state_part = jnp.einsum(
        "thd,the->hde", key_feat, value_heads, preferred_element_type=jnp.float32
    )
    norm_part = jnp.sum(key_feat, axis=0, dtype=jnp.float32)
    state_b, norm_b = spread_states(state_part, norm_part, False, count)
    numerator = jnp.einsum(
        "thd,hde->the", query_feat, state_b, preferred_element_type=jnp.float32
    )
    denominator = (
        jnp.einsum("thd,hd->th", query_feat, norm_b, preferred_element_type=jnp.float32) + 1.0
    )
    weight_wide = conv_weight.astype(jnp.float32)
    value_pad = jnp.pad(value_rows, ((0, 0), (0, 0), (1, 1), (0, 0)))
    grad_pad = jnp.pad(grad_rows, ((0, 0), (0, 0), (1, 1), (0, 0)))
    conv_term = jnp.zeros(queries.shape, jnp.float32)
    conv_grad = jnp.zeros(queries.shape, jnp.float32)
    for row_step in range(3):
        for col_step in range(3):
            conv_term = conv_term + weight_wide[row_step, col_step] * value_pad[
                :, row_step : row_step + row_count, col_step : col_step + col_count
            ].astype(jnp.float32)
            conv_grad = conv_grad + weight_wide[row_step, col_step] * grad_pad[
                :, 2 - row_step : 2 - row_step + row_count, 2 - col_step : 2 - col_step + col_count
            ].astype(jnp.float32)
    attention = numerator / denominator[..., None]
    attended = (attention.reshape(queries.shape) + conv_term).astype(jnp.bfloat16)
    grad_wide = grad_heads.astype(jnp.float32)
    numerator_grad = (grad_wide / denominator[..., None]).astype(jnp.bfloat16)
    denominator_grad = (-jnp.sum(grad_wide * numerator, -1) / (denominator * denominator)).astype(
        jnp.bfloat16
    )
    query_grad = jnp.einsum(
        "the,hde->thd", numerator_grad, state_b, preferred_element_type=jnp.float32
    )
    query_grad = (
        query_grad
        + denominator_grad.astype(jnp.float32)[..., None] * norm_b.astype(jnp.float32)[None]
    )
    grad_query = (
        jnp.where(queries.reshape(heads_shape) > 0, query_grad, 0.0)
        .astype(jnp.bfloat16)
        .reshape(queries.shape)
    )
    state_grad = jnp.einsum(
        "thd,the->hde", query_feat, numerator_grad, preferred_element_type=jnp.float32
    )
    norm_grad = jnp.einsum(
        "thd,th->hd", query_feat, denominator_grad, preferred_element_type=jnp.float32
    )
    back_state, back_norm = spread_states(state_grad, norm_grad, True, count)
    key_grad = jnp.einsum(
        "the,hde->thd", value_heads, back_state, preferred_element_type=jnp.float32
    )
    key_grad = key_grad + back_norm.astype(jnp.float32)[None]
    grad_key = (
        jnp.where(keys_in.reshape(heads_shape) > 0, key_grad, 0.0)
        .astype(jnp.bfloat16)
        .reshape(queries.shape)
    )
    value_grad = (
        jnp.einsum(
            "thd,hde->the", key_feat, back_state, preferred_element_type=jnp.float32
        ).reshape(queries.shape)
        + conv_grad
    )
    grad_value = value_grad.astype(jnp.bfloat16)
    return (attended, grad_query, grad_key, grad_value)


def solution(mesh):
    placed = (
        P("orbit", "space", None, None),
        P("orbit", "space", None, None),
        P("orbit", "space", None, None),
        P(),
        P("orbit", "space", None, None),
    )
    return jax.shard_map(
        on_device,
        mesh=mesh,
        in_specs=placed,
        out_specs=(
            P("orbit", "space", None, None),
            P("orbit", "space", None, None),
            P("orbit", "space", None, None),
            P("orbit", "space", None, None),
        ),
        check_vma=False,
    )
```

time: 664 us -> 223 us (0.34)
  waiting for transfers between devices: 298 us -> 2.34 us
  local copies, waits for them, and re-layouts: 145 us -> 51.1 us
  blocking collectives: 117 us -> 94.2 us
  between operations: 14.6 us -> 1.05 us
  starting transfers between devices: 11.6 us -> 23.7 us
  loops' own time: 11.7 us -> 0 us
  other arithmetic: 45.8 us -> 34.8 us
    psum x2 -> x0, waiting for transfers between devices: 267 us -> none  [spread_states(): whole_state, whole_norm = lax.psum((flat_state, flat_norm), 'space')]
    psum x2 -> x0, blocking collectives: 80.4 us -> none  [spread_states(): whole_state, whole_norm = lax.psum((flat_state, flat_norm), 'space')]
    dynamic_slice x30 -> x0, local copies, waits for them, and re-layouts: 69.9 us -> none  [one(): lax.dynamic_index_in_dim(a, source, 0, False)]
    all_gather x2 -> x4, blocking collectives: 37 us -> 94.2 us  [the longest x2 53.8 us: spread_states(): full = lax.all_gather(rounded, 'space', tiled=True)[:total]]
    all_gather x2 -> x0, waiting for transfers between devices: 31.2 us -> none  [prefix(): gathered = jax.tree.map(lambda a: lax.all_gather(a, axis), part)]
    convert_element_type x6 -> x4, other arithmetic: 27.3 us -> 2.65 us  [the longest x1 1.33 us: on_device(): denominator_grad.astype(jnp.float32)[..., None]]
    unnamed x72 -> x52, local copies, waits for them, and re-layouts: 27 us -> 6.12 us
    another operation x2 -> x0, loops' own time: 11.7 us -> none  [prefix(): return lax.fori_loop(0, ahead, one, state)]
  transfers between devices with their start and end apart: 8 -> 6, of which waited for: 3 -> 1; matrix products, arithmetic and copies ran while one was open for 9% -> 13% of each run, Pallas kernels for 0% -> 0%
where the time goes in v1:
time: 223 us; the launch traced here: 220 us
  blocking collectives  94.2 us (42%)
  local copies, waits for them, and re-layouts  51.1 us (23%)
  other arithmetic  34.8 us (16%)
  starting transfers between devices  23.7 us (11%)
  matrix products  12.8 us (6%)
  waiting for transfers between devices  2.34 us (1%)
    all_gather x2, blocking collectives, spread_states(): full = lax.all_gather(rounded, 'space', tiled=True)[:total]  53.8 us
    all_gather x2, blocking collectives, spread_states(): gathered = lax.all_gather(whole, 'orbit')  40.4 us
    ppermute x2, starting transfers between devices, padded(): lax.ppermute(tail, axis, [(i, (i + 1) % count) for i in range(ends)])  10.5 us
    all_to_all x2, starting transfers between devices, spread_states(): lax.all_to_all(flat.reshape(space, chunk), 'space', 0, 0, tiled=True)  10.5 us
    all_gather x2, other arithmetic, spread_states(): full = lax.all_gather(rounded, 'space', tiled=True)[:total]  7.85 us
    unnamed x52, local copies, waits for them, and re-layouts  6.12 us
    reshape x3, local copies, waits for them, and re-layouts, spread_states(): flat = jnp.concatenate([state_part.reshape(-1), norm_part.reshape(-1)])  5.41 us
  transfers between devices with their start and end apart: 6, of which 1 were waited for; matrix products, arithmetic and copies ran while one was open for 13% of the time, Pallas kernels for 0%

profile of v1, /device:TPU:0, one launch (start us, length us, event | category | flops | bytes accessed | tf_op | source)
XLA Modules:
  0.0 220.0 jit_solution(818352391605206176)
XLA Ops:
  0.6 1.2 convert_reduce_fusion
  8.8 5.5 %all-to-all-start = ((f32[16,1,15872]{2,1,0:T(1,128)}), f32[16,1,15872]{2,1,0:T(1,128)}, u32[]{:S(2)}, u32[]{:S(2)}) async-start(f32[16,1,15872]{2,1,0:T(1,128)} %bitcast), calls=%async_computation | async-start | bytes 2031616 | tf_op jit(solution)/shard_map/all_to_all | solution.py:35
  15.2 1.3 collective-permute-start.1
  16.5 5.3 %collective-permute-start = (bf16[1,1,64,2240]{3,2,1,0:T(8,128)(2,1)}, bf16[1,1,64,2240]{3,2,1,0:T(8,128)(2,1)}, u32[]{:S(2)}, u32[]{:S(2)}) collective-permute-start(bf16[1,1,64,2240]{3,2,1,0:T(8,128)(2,1)} %get-tuple-element.23), channel_id=1, source_target_pairs={{0,1},{1,2},{2,3},{3,4},{4,5},{5,6},{6,7},{7,8},{8,9},{9,10},{10,1... | collective-permute-start | bytes 860168 | tf_op jit(solution)/shard_map/ppermute | solution.py:18
  22.7 1.4 collective-permute-start.3
  24.1 5.3 %collective-permute-start.2 = (bf16[1,1,64,2240]{3,2,1,0:T(8,128)(2,1)}, bf16[1,1,64,2240]{3,2,1,0:T(8,128)(2,1)}, u32[]{:S(2)}, u32[]{:S(2)}) collective-permute-start(bf16[1,1,64,2240]{3,2,1,0:T(8,128)(2,1)} %get-tuple-element.21), channel_id=1, source_target_pairs={{0,1},{1,2},{2,3},{3,4},{4,5},{5,6},{6,7},{7,8},{8,9},{9,10},{10,1... | collective-permute-start | bytes 860168 | tf_op jit(solution)/shard_map/ppermute | solution.py:18
  33.3 1.5 copy.78
  34.7 2.0 reshape.130
  36.8 1.2 copy.76
  39.0 1.3 copy.80
  43.2 1.5 select_maximum_fusion.2
  44.7 1.4 select_maximum_fusion
  46.1 2.5 %reduce_sum.55 = f32[15872]{0:T(1024)} reduce(f32[16,1,15872]{2,1,0:T(1,128)} %all-to-all-done, f32[]{:T(128)} %constant.17.clone.1), dimensions={0,1}, to_apply=%region_1.2 | reduce | flops 238080 | bytes 1079300 | tf_op jit(solution)/shard_map/reduce_sum | solution.py:36
  49.5 22.8 %all-gather.2 = f32[16,1,15872]{2,1,0:T(1,128)S(1)} all-gather(f32[1,1,15872]{2,1,0:T(1,128)S(1)} %reshape.143), channel_id=2, replica_groups=mesh['orbit'=16,'space'=16] {'orbit'}, dimensions={0}, use_global_device_ids=true | all-gather | bytes 1079296 | tf_op jit(solution)/shard_map/all_gather | solution.py:38
  72.6 30.2 %all-gather.3 = bf16[16,1,15872]{2,1,0:T(2,128)(2,1)} all-gather(bf16[1,1,15872]{2,1,0:T(2,128)(2,1)S(1)} %reshape.145), channel_id=1, replica_groups=mesh['orbit'=16,'space'=16] {'space'}, dimensions={0}, use_global_device_ids=true | all-gather | bytes 539648 | tf_op jit(solution)/shard_map/all_gather | solution.py:50
  102.8 4.8 %reduce.3 = bf16[16,15872]{1,0:T(8,128)(2,1)} reduce(bf16[16,1,15872]{2,1,0:T(2,128)(2,1)} %all-gather.3, bf16[]{:T(256)} %constant.32), dimensions={1}, to_apply=%all-gather.3.reduce_sub_computation | reduce | bytes 1015810 | tf_op jit(solution)/shard_map/all_gather | solution.py:50
  107.7 2.6 %reshape.146 = bf16[253952]{0:T(1024)(128)(2,1)} reshape(bf16[16,15872]{1,0:T(8,128)(2,1)} %reduce.3) | data formatting | bytes 1015808
  110.3 1.3 slice.160
  111.5 1.8 slice.159
  113.4 1.4 reshape.158
  114.8 1.4 reshape.131
  116.1 1.3 fusion.18
  118.7 2.5 %reshape.129 = bf16[20,112,112]{2,1,0:T(8,128)(2,1)} reshape(bf16[250880]{0:T(1024)(128)(2,1)} %slice.159) | data formatting | bytes 1003520 | tf_op jit(solution)/shard_map/reshape | solution.py:52
  121.2 3.0 %fusion.13 = f32[20,112,112]{2,1,0:T(8,128)} fusion(bf16[128,20,112]{0,2,1:T(8,128)(2,1)} %copy.76, f32[128,20,112]{0,2,1:T(8,128)} %copy.78, f32[128,20]{0,1:T(8,128)} %fusion.10), kind=kOutput, calls=%fused_computation.59 | convolution fusion | flops 64798720 | bytes 2734080 | tf_op jit(solution)/shard_map/thd,the->hde/dot_general | solution.py:114
  124.3 2.0 multiply_reduce_fusion
  126.2 2.9 %copy.77 = f32[128,20,112]{2,1,0:T(8,128)} copy(f32[128,20,112]{0,2,1:T(8,128)} %get-tuple-element.20) | data formatting | bytes 2293760 | tf_op jit(solution)/shard_map/div | solution.py:95
  129.1 2.7 %reshape.132 = f32[1,2,64,2240]{3,2,1,0:T(8,128)} reshape(f32[128,20,112]{2,1,0:T(8,128)} %copy.77) | data formatting | bytes 2293760 | tf_op jit(solution)/shard_map/reshape | solution.py:96
  131.8 1.3 convert_element_type.139
  133.1 1.3 fusion.14
  134.4 1.4 fusion.11
  136.5 1.4 reshape.135
  137.9 3.1 %reshape.134 = f32[250880]{0:T(1024)} reshape(f32[20,112,112]{2,1,0:T(8,128)} %fusion.13) | data formatting | bytes 2007040 | tf_op jit(solution)/shard_map/reshape | solution.py:31
  141.0 2.3 %select_maximum_fusion.4 = f32[253952]{0:T(1024)} fusion(f32[2240]{0:T(1024)} %reshape.135, f32[250880]{0:T(1024)} %reshape.134), kind=kLoop, calls=%fused_computation.23 | loop fusion | flops 1015808 | bytes 2028288 | tf_op jit(solution)/shard_map/concatenate | solution.py:31
  143.3 5.0 %all-to-all-start.1 = ((f32[16,1,15872]{2,1,0:T(1,128)}), f32[16,1,15872]{2,1,0:T(1,128)}, u32[]{:S(2)}, u32[]{:S(2)}) async-start(f32[16,1,15872]{2,1,0:T(1,128)} %bitcast.69), calls=%async_computation.1 | async-start | bytes 2031616 | tf_op jit(solution)/shard_map/all_to_all | solution.py:35
  148.2 2.8 %fusion.7 = bf16[128,20,112]{0,2,1:T(8,128)(2,1)} fusion(pred[128,20,112]{0,2,1:T(8,128)(4,1)} %copy.80, bf16[20,112,112]{2,1,0:T(8,128)(2,1)} %reshape.129, f32[20,112]{1,0:T(8,128)} %convert_element_type.139, f32[128,20]{0,1:T(8,128)} %get-tuple-element.17, f32[128,20,112]{0,2,1:T(8,128)} %copy.78, f32[128,20]{0,1:T(8,128)} %fusion.10), kind=kOutput, calls=%fused_computation.17 | convolution fusion | flops 65945600 | bytes 2538240 | tf_op jit(solution)/shard_map/the,hde->thd/dot_general | solution.py:102
  151.0 2.3 %copy.81 = bf16[128,20,112]{2,1,0:T(8,128)(2,1)} copy(bf16[128,20,112]{0,2,1:T(8,128)(2,1)} %fusion.7) | data formatting | bytes 1146880 | tf_op jit(solution)/shard_map/convert_element_type | solution.py:111
  153.3 2.4 %reshape.133 = bf16[1,2,64,2240]{3,2,1,0:T(8,128)(2,1)} reshape(bf16[128,20,112]{2,1,0:T(8,128)(2,1)} %copy.81) | data formatting | bytes 1146880 | tf_op jit(solution)/shard_map/reshape | solution.py:112
  155.7 3.3 %add_convert_fusion.1 = bf16[1,2,64,2240]{3,2,1,0:T(8,128)(2,1)} fusion(f32[1,2,64,2240]{3,2,1,0:T(8,128)} %reshape.132, bf16[1,2,64,2240]{3,2,1,0:T(8,128)(2,1)S(1)} %copy-done, bf16[1,4,66,2240]{3,2,1,0:T(8,128)(2,1)S(1)} %select_maximum_fusion.2, bf16[1,1,64,2240]{3,2,1,0:T(8,128)(2,1)} %collective-permute-done.1, ...), kind=kLoop, calls=%fused_computation.19 | loop fusion | flops 8601600 | bytes 6388480 | tf_op jit(solution)/shard_map/convert_element_type | solution.py:96
  159.0 2.3 %all-to-all-done.1 = f32[16,1,15872]{2,1,0:T(1,128)} async-done(((f32[16,1,15872]{2,1,0:T(1,128)}), f32[16,1,15872]{2,1,0:T(1,128)}, u32[]{:S(2)}, u32[]{:S(2)}) %all-to-all-start.1) | async-done | bytes 1015840 | tf_op jit(solution)/shard_map/all_to_all | solution.py:35
  161.4 1.8 reduce_sum.58
  163.3 17.6 %all-gather.4 = f32[16,1,15872]{2,1,0:T(1,128)S(1)} all-gather(f32[1,1,15872]{2,1,0:T(1,128)S(1)} %reshape.147), channel_id=3, replica_groups=mesh['orbit'=16,'space'=16] {'orbit'}, dimensions={0}, use_global_device_ids=true | all-gather | bytes 1079296 | tf_op jit(solution)/shard_map/all_gather | solution.py:45
  181.2 23.6 %all-gather.5 = bf16[16,1,15872]{2,1,0:T(2,128)(2,1)S(1)} all-gather(bf16[1,1,15872]{2,1,0:T(2,128)(2,1)S(1)} %reshape.149), channel_id=1, replica_groups=mesh['orbit'=16,'space'=16] {'space'}, dimensions={0}, use_global_device_ids=true | all-gather | bytes 539648 | tf_op jit(solution)/shard_map/all_gather | solution.py:50
  204.8 3.0 %reduce.13 = bf16[16,15872]{1,0:T(8,128)(2,1)S(1)} reduce(bf16[16,1,15872]{2,1,0:T(2,128)(2,1)S(1)} %all-gather.5, bf16[]{:T(256)} %constant.32), dimensions={1}, to_apply=%all-gather.5.reduce_sub_computation | reduce | bytes 1015810 | tf_op jit(solution)/shard_map/all_gather | solution.py:50
  209.7 1.4 convolution_bitcast_fusion
  212.0 1.4 reshape.137
  213.4 1.8 copy.89
  215.3 1.4 reshape.138
  216.7 3.3 %add_convert_fusion = bf16[1,2,64,2240]{3,2,1,0:T(8,128)(2,1)} fusion(f32[1,2,64,2240]{3,2,1,0:T(8,128)} %reshape.138, bf16[1,4,66,2240]{3,2,1,0:T(8,128)(2,1)S(1)} %select_maximum_fusion, bf16[1,2,64,2240]{3,2,1,0:T(8,128)(2,1)S(1)} %copy-done.3, bf16[1,1,64,2240]{3,2,1,0:T(8,128)(2,1)} %collective-permute-done.2, ...), kind=kLoop, calls=%fused_computation.18 | loop fusion | flops 8601600 | bytes 6388480 | tf_op jit(solution)/shard_map/convert_element_type | solution.py:136
  (89 shorter events, 22.5 us)
Async XLA Ops:
  2.9 1.3 copy-start
  4.3 1.3 copy-start.5
  5.6 0.8 copy-start.9
  8.8 13.0 %copy-start.1 = (bf16[1,2,64,2240]{3,2,1,0:T(8,128)(2,1)S(1)}, bf16[1,2,64,2240]{3,2,1,0:T(8,128)(2,1)}, u32[]{:S(2)}) copy-start(bf16[1,2,64,2240]{3,2,1,0:T(8,128)(2,1)} %param.9) | copy-start | bytes 1720324
  8.8 37.3 %all-to-all-start = ((f32[16,1,15872]{2,1,0:T(1,128)}), f32[16,1,15872]{2,1,0:T(1,128)}, u32[]{:S(2)}, u32[]{:S(2)}) async-start(f32[16,1,15872]{2,1,0:T(1,128)} %bitcast), calls=%async_computation | async-start | bytes 2031616 | tf_op jit(solution)/shard_map/all_to_all | solution.py:35
  14.4 15.0 %copy-start.8 = (bf16[1,2,64,2240]{3,2,1,0:T(8,128)(2,1)S(1)}, bf16[1,2,64,2240]{3,2,1,0:T(8,128)(2,1)}, u32[]{:S(2)}) copy-start(bf16[1,2,64,2240]{3,2,1,0:T(8,128)(2,1)} %param.5) | copy-start | bytes 1720324
  15.2 28.0 %collective-permute-start.1 = (bf16[1,1,64,2240]{3,2,1,0:T(8,128)(2,1)}, bf16[1,1,64,2240]{3,2,1,0:T(8,128)(2,1)}, u32[]{:S(2)}, u32[]{:S(2)}) collective-permute-start(bf16[1,1,64,2240]{3,2,1,0:T(8,128)(2,1)} %get-tuple-element.24), channel_id=1, source_target_pairs={{1,0},{2,1},{3,2},{4,3},{5,4},{6,5},{7,6},{8,7},{9,8},{10,9},{11,1... | collective-permute-start | bytes 860168 | tf_op jit(solution)/shard_map/ppermute | solution.py:20
  16.5 26.7 %collective-permute-start = (bf16[1,1,64,2240]{3,2,1,0:T(8,128)(2,1)}, bf16[1,1,64,2240]{3,2,1,0:T(8,128)(2,1)}, u32[]{:S(2)}, u32[]{:S(2)}) collective-permute-start(bf16[1,1,64,2240]{3,2,1,0:T(8,128)(2,1)} %get-tuple-element.23), channel_id=1, source_target_pairs={{0,1},{1,2},{2,3},{3,4},{4,5},{5,6},{6,7},{7,8},{8,9},{9,10},{10,1... | collective-permute-start | bytes 860168 | tf_op jit(solution)/shard_map/ppermute | solution.py:18
  22.7 8.4 %copy-start.4 = (bf16[1,2,64,2240]{3,2,1,0:T(8,128)(2,1)S(1)}, bf16[1,2,64,2240]{3,2,1,0:T(8,128)(2,1)}, u32[]{:S(2)}) copy-start(bf16[1,2,64,2240]{3,2,1,0:T(8,128)(2,1)} %param.6) | copy-start | bytes 1720324
  22.7 22.0 %collective-permute-start.3 = (bf16[1,1,64,2240]{3,2,1,0:T(8,128)(2,1)}, bf16[1,1,64,2240]{3,2,1,0:T(8,128)(2,1)}, u32[]{:S(2)}, u32[]{:S(2)}) collective-permute-start(bf16[1,1,64,2240]{3,2,1,0:T(8,128)(2,1)} %get-tuple-element.22), channel_id=1, source_target_pairs={{1,0},{2,1},{3,2},{4,3},{5,4},{6,5},{7,6},{8,7},{9,8},{10,9},{11,1... | collective-permute-start | bytes 860168 | tf_op jit(solution)/shard_map/ppermute | solution.py:20
  24.1 20.6 %collective-permute-start.2 = (bf16[1,1,64,2240]{3,2,1,0:T(8,128)(2,1)}, bf16[1,1,64,2240]{3,2,1,0:T(8,128)(2,1)}, u32[]{:S(2)}, u32[]{:S(2)}) collective-permute-start(bf16[1,1,64,2240]{3,2,1,0:T(8,128)(2,1)} %get-tuple-element.21), channel_id=1, source_target_pairs={{0,1},{1,2},{2,3},{3,4},{4,5},{5,6},{6,7},{7,8},{8,9},{9,10},{10,1... | collective-permute-start | bytes 860168 | tf_op jit(solution)/shard_map/ppermute | solution.py:18
  34.7 3.3 %copy-start.19 = (bf16[3,3,2240]{2,1,0:T(4,128)(2,1)S(1)}, bf16[3,3,2240]{2,1,0:T(4,128)(2,1)}, u32[]{:S(2)}) copy-start(bf16[3,3,2240]{2,1,0:T(4,128)(2,1)} %param.8) | copy-start | bytes 120964
  34.7 3.3 %copy-start.12 = (pred[1,2,64,2240]{3,2,1,0:T(8,128)(4,1)S(1)}, pred[1,2,64,2240]{3,2,1,0:T(8,128)(4,1)}, u32[]{:S(2)}) copy-start(pred[1,2,64,2240]{3,2,1,0:T(8,128)(4,1)} %broadcast_compare_fusion.1) | copy-start | bytes 860164
  36.8 3.5 %copy-start.11 = (pred[1,2,64,2240]{3,2,1,0:T(8,128)(4,1)S(1)}, pred[1,2,64,2240]{3,2,1,0:T(8,128)(4,1)}, u32[]{:S(2)}) copy-start(pred[1,2,64,2240]{3,2,1,0:T(8,128)(4,1)} %broadcast_compare_fusion) | copy-start | bytes 860164
  43.2 1.5 copy-start.2
  48.6 23.7 %copy-start.22 = (pred[16]{0:T(512)(128)(4,1)S(1)}, pred[16]{0:T(512)(128)(4,1)}, u32[]{:S(2)}) copy-start(pred[16]{0:T(512)(128)(4,1)} %iota_compare_fusion.4) | copy-start | bytes 52
  117.5 0.6 copy-start.18
  121.2 3.0 %copy-start.7 = (bf16[128,20,112]{0,2,1:T(8,128)(2,1)S(1)}, bf16[128,20,112]{0,2,1:T(8,128)(2,1)}, u32[]{:S(2)}) copy-start(bf16[128,20,112]{0,2,1:T(8,128)(2,1)} %copy.76) | copy-start | bytes 1720324
  121.2 3.0 %copy-start.13 = (f32[128,20,112]{0,2,1:T(8,128)S(1)}, f32[128,20,112]{0,2,1:T(8,128)}, u32[]{:S(2)}) copy-start(f32[128,20,112]{0,2,1:T(8,128)} %copy.78) | copy-start | bytes 3440644
  121.2 3.1 %copy-start.14 = (bf16[20,112,112]{2,1,0:T(8,128)(2,1)S(1)}, bf16[20,112,112]{2,1,0:T(8,128)(2,1)}, u32[]{:S(2)}) copy-start(bf16[20,112,112]{2,1,0:T(8,128)(2,1)} %reshape.129) | copy-start | bytes 1505284
  121.2 3.1 %copy-start.20 = (f32[128,20]{0,1:T(8,128)S(1)}, f32[128,20]{0,1:T(8,128)}, u32[]{:S(2)}) copy-start(f32[128,20]{0,1:T(8,128)} %fusion.10) | copy-start | bytes 30724
  143.3 18.1 %all-to-all-start.1 = ((f32[16,1,15872]{2,1,0:T(1,128)}), f32[16,1,15872]{2,1,0:T(1,128)}, u32[]{:S(2)}, u32[]{:S(2)}) async-start(f32[16,1,15872]{2,1,0:T(1,128)} %bitcast.69), calls=%async_computation.1 | async-start | bytes 2031616 | tf_op jit(solution)/shard_map/all_to_all | solution.py:35
  159.0 21.9 %copy-start.21 = (pred[16]{0:T(512)(128)(4,1)S(1)}, pred[16]{0:T(512)(128)(4,1)}, u32[]{:S(2)}) copy-start(pred[16]{0:T(512)(128)(4,1)} %iota_compare_fusion.3) | copy-start | bytes 52
  208.7 1.1 copy-start.6
  209.4 1.7 copy-start.10
  215.2 1.5 copy-start.3
  215.2 1.5 copy-start.15
  215.2 1.5 copy-start.16
  215.3 1.5 copy-start.17

commit v2 on v1

v2 whole, which is shorter than its diff:
```python
import jax
import jax.numpy as jnp
from jax import lax
from jax.experimental import pallas as pl
from jax.sharding import PartitionSpec as P

HEADS = 20
HD = 112


def padded_pair(cells, width):
    count = lax.axis_size("space")
    ends = count - 1
    rows = cells.shape[2]
    head = cells[:, :, :width]
    tail = cells[:, :, rows - width :]
    return jnp.concatenate(
        [
            lax.ppermute(tail, "space", [(i, (i + 1) % count) for i in range(ends)]),
            cells,
            lax.ppermute(head, "space", [((i + 1) % count, i) for i in range(ends)]),
        ],
        axis=2,
    )


def part_kernel(k_ref, v_ref, s_ref, n_ref):
    for h in range(HEADS):
        cols = slice(h * HD, (h + 1) * HD)
        kf = jnp.maximum(k_ref[:, cols], 0)
        vh = v_ref[:, cols]
        s_ref[h] = lax.dot_general(
            kf, vh, (((0,), (0,)), ((), ())), preferred_element_type=jnp.float32
        )
        n_ref[h : h + 1, :] = jnp.sum(kf.astype(jnp.float32), axis=0, keepdims=True)


def forward_kernel(q_ref, g_ref, c_ref, s_ref, n_ref, a_ref, gq_ref, sg_ref, ng_ref):
    for h in range(HEADS):
        cols = slice(h * HD, (h + 1) * HD)
        qh = q_ref[:, cols]
        qf = jnp.maximum(qh, 0)
        qw = qf.astype(jnp.float32)
        state = s_ref[h]
        norm = n_ref[h : h + 1, :].astype(jnp.float32)
        numerator = jnp.dot(qf, state, preferred_element_type=jnp.float32)
        denominator = jnp.sum(qw * norm, axis=1, keepdims=True) + 1.0
        a_ref[:, cols] = (numerator / denominator + c_ref[:, cols]).astype(jnp.bfloat16)
        gw = g_ref[:, cols].astype(jnp.float32)
        num_grad = (gw / denominator).astype(jnp.bfloat16)
        den_grad = (
            -jnp.sum(gw * numerator, axis=1, keepdims=True) / (denominator * denominator)
        ).astype(jnp.bfloat16).astype(jnp.float32)
        query_grad = lax.dot_general(
            num_grad, state, (((1,), (1,)), ((), ())), preferred_element_type=jnp.float32
        )
        query_grad = query_grad + den_grad * norm
        gq_ref[:, cols] = jnp.where(qh > 0, query_grad, 0.0).astype(jnp.bfloat16)
        sg_ref[h] = lax.dot_general(
            qf, num_grad, (((0,), (0,)), ((), ())), preferred_element_type=jnp.float32
        )
        ng_ref[h : h + 1, :] = jnp.sum(den_grad * qw, axis=0, keepdims=True)


def backward_kernel(k_ref, v_ref, c_ref, s_ref, n_ref, gk_ref, gv_ref):
    for h in range(HEADS):
        cols = slice(h * HD, (h + 1) * HD)
        kh = k_ref[:, cols]
        kf = jnp.maximum(kh, 0)
        vh = v_ref[:, cols]
        state = s_ref[h]
        norm = n_ref[h : h + 1, :].astype(jnp.float32)
        key_grad = lax.dot_general(
            vh, state, (((1,), (1,)), ((), ())), preferred_element_type=jnp.float32
        )
        gk_ref[:, cols] = jnp.where(kh > 0, key_grad + norm, 0.0).astype(jnp.bfloat16)
        value_grad = jnp.dot(kf, state, preferred_element_type=jnp.float32) + c_ref[:, cols]
        gv_ref[:, cols] = value_grad.astype(jnp.bfloat16)


def spread_states(state_part, norm_part, reverse, counts):
    space = lax.axis_size("space")
    orbit = lax.axis_size("orbit")
    place = lax.axis_index("orbit")
    flat = jnp.concatenate([state_part.reshape(-1), norm_part.reshape(-1)])
    total = flat.shape[0]
    chunk = -(-total // (space * 128)) * 128
    flat = jnp.pad(flat, (0, chunk * space - total))
    pieces = lax.all_to_all(flat.reshape(space, chunk), "space", 0, 0, tiled=True)
    whole = jnp.sum(pieces, axis=0)
    if not reverse:
        gathered = lax.all_gather(whole, "orbit")
        views = jnp.arange(orbit)
        keep = views <= place
        summed = jnp.sum(jnp.where(keep[:, None], gathered, 0.0), axis=0)
        summed = summed / counts
    else:
        whole = whole / counts
        gathered = lax.all_gather(whole, "orbit")
        views = jnp.arange(orbit)
        keep = views >= place
        summed = jnp.sum(jnp.where(keep[:, None], gathered, 0.0), axis=0)
    rounded = summed.astype(jnp.bfloat16)
    full = lax.all_gather(rounded, "space", tiled=True)[:total]
    size = state_part.size
    return full[:size].reshape(state_part.shape), full[size:].reshape(norm_part.shape)


def on_device(queries, keys_in, values, conv_weight, grad_out):
    view_count, row_count, col_count, feature_width = queries.shape
    token_count = view_count * row_count * col_count
    flat_shape = (token_count, feature_width)
    q2 = queries.reshape(flat_shape)
    k2 = keys_in.reshape(flat_shape)
    v2 = values.reshape(flat_shape)
    g2 = grad_out.reshape(flat_shape)
    place = lax.axis_index("orbit")
    count = (place.astype(jnp.float32) + 1.0) * float(
        row_count * lax.axis_size("space") * col_count
    )
    f32 = jnp.float32
    state_part, norm_part = pl.pallas_call(
        part_kernel,
        out_shape=(
            jax.ShapeDtypeStruct((HEADS, HD, HD), f32),
            jax.ShapeDtypeStruct((HEADS, HD), f32),
        ),
    )(k2, v2)
    state_b, norm_b = spread_states(state_part, norm_part, False, count)

    pair = padded_pair(jnp.stack([values, grad_out]), 1)
    pair = jnp.pad(pair, ((0, 0), (0, 0), (0, 0), (1, 1), (0, 0)))
    value_pad, grad_pad = pair[0], pair[1]
    weight_wide = conv_weight.astype(f32)
    conv_term = jnp.zeros(queries.shape, f32)
    conv_grad = jnp.zeros(queries.shape, f32)
    for row_step in range(3):
        for col_step in range(3):
            conv_term = conv_term + weight_wide[row_step, col_step] * value_pad[
                :, row_step : row_step + row_count, col_step : col_step + col_count
            ].astype(f32)
            conv_grad = conv_grad + weight_wide[row_step, col_step] * grad_pad[
                :, 2 - row_step : 2 - row_step + row_count, 2 - col_step : 2 - col_step + col_count
            ].astype(f32)

    bf = jnp.bfloat16
    attended, grad_query, state_grad, norm_grad = pl.pallas_call(
        forward_kernel,
        out_shape=(
            jax.ShapeDtypeStruct(flat_shape, bf),
            jax.ShapeDtypeStruct(flat_shape, bf),
            jax.ShapeDtypeStruct((HEADS, HD, HD), f32),
            jax.ShapeDtypeStruct((HEADS, HD), f32),
        ),
    )(q2, g2, conv_term.reshape(flat_shape), state_b, norm_b)
    back_state, back_norm = spread_states(state_grad, norm_grad, True, count)
    grad_key, grad_value = pl.pallas_call(
        backward_kernel,
        out_shape=(
            jax.ShapeDtypeStruct(flat_shape, bf),
            jax.ShapeDtypeStruct(flat_shape, bf),
        ),
    )(k2, v2, conv_grad.reshape(flat_shape), back_state, back_norm)
    shape = queries.shape
    return (
        attended.reshape(shape),
        grad_query.reshape(shape),
        grad_key.reshape(shape),
        grad_value.reshape(shape),
    )


def solution(mesh):
    placed = (
        P("orbit", "space", None, None),
        P("orbit", "space", None, None),
        P("orbit", "space", None, None),
        P(),
        P("orbit", "space", None, None),
    )
    return jax.shard_map(
        on_device,
        mesh=mesh,
        in_specs=placed,
        out_specs=(
            P("orbit", "space", None, None),
            P("orbit", "space", None, None),
            P("orbit", "space", None, None),
            P("orbit", "space", None, None),
        ),
        check_vma=False,
    )
```

time: 223 us -> 185 us (0.83)
  local copies, waits for them, and re-layouts: 51.1 us -> 11.4 us
  Pallas kernels: 0 us -> 26.3 us
  waiting for transfers between devices: 2.34 us -> 22.7 us
  other arithmetic: 34.8 us -> 18.7 us
  matrix products: 12.8 us -> 0 us
  starting transfers between devices: 23.7 us -> 16 us
  blocking collectives: 94.2 us -> 86.8 us
    pallas_call x0 -> x3, Pallas kernels: none -> 26.3 us  [the longest x1 14.1 us: on_device(): pl.pallas_call(forward_kernel, out_shape=(jax.ShapeDtypeStruct(flat_shape...]
    all_to_all x2, waiting for transfers between devices: 2.33 us -> 22.3 us  [spread_states(): lax.all_to_all(flat.reshape(space, chunk), 'space', 0, 0, tiled=True)]
    reshape x10 -> x0, local copies, waits for them, and re-layouts: 13.8 us -> none  [the longest x2 3.29 us: on_device(): query_feat = jax.nn.relu(queries).reshape(heads_shape)]
    dot_general x8 -> x0, matrix products: 12.8 us -> none  [the longest x1 3.04 us: on_device(): jnp.einsum('thd,the->hde', query_feat, numerator_grad, preferred_element_...]
    ppermute x4 -> x2, starting transfers between devices: 13.2 us -> 3.88 us  [the longest x1 2.6 us: padded_pair(): lax.ppermute(tail, 'space', [(i, (i + 1) % count) for i in range(ends)])]
    convert_element_type x6 -> x1, other arithmetic: 9.25 us -> 0.01 us  [on_device(): weight_wide = conv_weight.astype(f32)]
    all_gather x2, blocking collectives: 53.8 us -> 46.4 us  [spread_states(): full = lax.all_gather(rounded, 'space', tiled=True)[:total]]
    convert_element_type x5 -> x0, local copies, waits for them, and re-layouts: 5.03 us -> none  [the longest x1 2.31 us: on_device(): grad_query = jnp.where(queries.reshape(heads_shape) > 0, query_grad, 0.0)...]
  transfers between devices with their start and end apart: 6 -> 4, of which waited for: 1 -> 3; matrix products, arithmetic and copies ran while one was open for 13% -> 5% of each run, Pallas kernels for 0% -> 2%
where the time goes in v2:
time: 185 us; the launch traced here: 183 us
  blocking collectives  86.8 us (47%)
  Pallas kernels  26.3 us (14%)
  waiting for transfers between devices  22.7 us (12%)
  other arithmetic  18.7 us (10%)
  starting transfers between devices  16 us (9%)
  local copies, waits for them, and re-layouts  11.4 us (6%)
    all_gather x2, blocking collectives, spread_states(): full = lax.all_gather(rounded, 'space', tiled=True)[:total]  46.4 us
    all_gather x2, blocking collectives, spread_states(): gathered = lax.all_gather(whole, 'orbit')  40.4 us
    all_to_all x2, waiting for transfers between devices, spread_states(): lax.all_to_all(flat.reshape(space, chunk), 'space', 0, 0, tiled=True)  22.3 us
    pallas_call x1, Pallas kernels, on_device(): pl.pallas_call(forward_kernel, out_shape=(jax.ShapeDtypeStruct(flat_shape...  14.1 us
    all_to_all x2, starting transfers between devices, spread_states(): lax.all_to_all(flat.reshape(space, chunk), 'space', 0, 0, tiled=True)  12.1 us
    pallas_call x1, Pallas kernels, on_device(): pl.pallas_call(backward_kernel, out_shape=(jax.ShapeDtypeStruct(flat_shap...  8.38 us
    all_gather x2, other arithmetic, spread_states(): full = lax.all_gather(rounded, 'space', tiled=True)[:total]  6.08 us
    reshape x4, local copies, waits for them, and re-layouts, spread_states(): flat = jnp.concatenate([state_part.reshape(-1), norm_part.reshape(-1)])  4.7 us
  transfers between devices with their start and end apart: 4, of which 3 were waited for; matrix products, arithmetic and copies ran while one was open for 5% of the time, Pallas kernels for 2%

profile of v2, /device:TPU:0, one launch (start us, length us, event | category | flops | bytes accessed | tf_op | source)
XLA Modules:
  0.0 182.9 jit_solution(3505993943274852435)
XLA Ops:
  0.6 2.3 %fusion.6 = (bf16[2,1,1,64,2240]{4,3,2,1,0:T(8,128)(2,1)}, bf16[2,1,1,64,2240]{4,3,2,1,0:T(8,128)(2,1)}) fusion(bf16[1,1,2,64,2240]{4,3,2,1,0:T(8,128)(2,1)} %bitcast.26, bf16[1,1,2,64,2240]{4,3,2,1,0:T(8,128)(2,1)} %bitcast.30), kind=kLoop, calls=%fused_computation.21 | loop fusion | flops 573440 | bytes 2293760 | tf_op jit(solution)/shard_map/stack | solution.py:131
  3.0 2.6 %collective-permute-start = (bf16[2,1,1,64,2240]{4,3,2,1,0:T(8,128)(2,1)}, bf16[2,1,1,64,2240]{4,3,2,1,0:T(8,128)(2,1)}, u32[]{:S(2)}, u32[]{:S(2)}) collective-permute-start(bf16[2,1,1,64,2240]{4,3,2,1,0:T(8,128)(2,1)} %get-tuple-element.31), channel_id=1, source_target_pairs={{0,1},{1,2},{2,3},{3,4},{4,5},{5,6},{6,7},{7,8},{8,9},{9,10},{10,1... | collective-permute-start | bytes 1720328 | tf_op jit(solution)/shard_map/ppermute | solution.py:19
  5.6 1.3 collective-permute-start.1
  6.9 3.8 %shard_map.84 = (f32[20,112,112]{2,1,0:T(8,128)}, f32[20,112]{1,0:T(8,128)}) custom-call(bf16[128,2240]{1,0:T(8,128)(2,1)} %bitcast.35, bf16[128,2240]{1,0:T(8,128)(2,1)} %bitcast.27), custom_call_target="tpu_custom_call" | custom-call | tf_op jit(solution)/shard_map/pallas_call | solution.py:122
  10.7 2.2 %reshape.119 = f32[250880]{0:T(1024)S(1)} reshape(f32[20,112,112]{2,1,0:T(8,128)} %get-tuple-element.12) | data formatting | bytes 2007040 | tf_op jit(solution)/shard_map/reshape | solution.py:85
  12.8 0.0 copy-done.18
  12.8 0.1 reshape.120
  12.9 1.1 select_maximum_fusion.3
  14.0 7.8 %all-to-all-start = ((f32[16,1,15872]{2,1,0:T(1,128)}), f32[16,1,15872]{2,1,0:T(1,128)S(1)}, u32[]{:S(2)}, u32[]{:S(2)}) async-start(f32[16,1,15872]{2,1,0:T(1,128)} %bitcast.8), calls=%async_computation | async-start | bytes 2031616 | tf_op jit(solution)/shard_map/all_to_all | solution.py:89
  21.8 0.2 slice_reduce_fusion.8
  22.0 0.0 copy-start.2
  22.0 0.0 copy-start.4
  22.1 0.0 copy-start.6
  22.1 0.0 copy-start.8
  22.1 0.0 copy-start.10
  22.1 0.0 copy-start.12
  22.1 0.0 copy-start.14
  22.1 0.0 collective-permute-done
  22.1 0.4 collective-permute-done.1
  22.6 0.0 copy-done.1
  22.6 2.1 %select_maximum_fusion = bf16[2,1,4,66,2240]{4,3,2,1,0:T(8,128)(2,1)S(1)} fusion(bf16[2,1,1,64,2240]{4,3,2,1,0:T(8,128)(2,1)} %collective-permute-done.1, bf16[2,1,1,64,2240]{4,3,2,1,0:T(8,128)(2,1)} %collective-permute-done, bf16[1,1,2,64,2240]{4,3,2,1,0:T(8,128)(2,1)S(1)} %bitcast.32, bf16[1,1,2,64,2240]{4,3,2,1,0:T(8,128)(2,1)S(1)} %bitcast.29), kind=kLoop, calls=%fused_computation.3 | loop fusion | flops 17740800 | bytes 4659200 | tf_op jit(solution)/shard_map/concatenate | solution.py:17
  24.7 0.2 slice_bitcast_fusion
  25.0 2.1 %multiply_add_fusion.1 = f32[1,2,64,2240]{3,2,1,0:T(8,128)} fusion(bf16[1,4,66,2240]{3,2,1,0:T(8,128)(2,1)S(1)} %get-tuple-element.30, f32[2240]{0:T(1024)S(1)} %get-tuple-element.21, f32[2240]{0:T(1024)S(1)} %get-tuple-element.22, f32[2240]{0:T(1024)S(1)} %get-tuple-element.23, f32[2240]{0:T(1024)S(1)} %get-tuple-element.24, ...), kind=kLoop, calls=%fused_computation.13 | loop fusion | flops 7454720 | bytes 6388480 | tf_op jit(solution)/shard_map/add | solution.py:139
  27.0 11.2 %all-to-all-done = f32[16,1,15872]{2,1,0:T(1,128)S(1)} async-done(((f32[16,1,15872]{2,1,0:T(1,128)}), f32[16,1,15872]{2,1,0:T(1,128)S(1)}, u32[]{:S(2)}, u32[]{:S(2)}) %all-to-all-start) | async-done | bytes 1015840 | tf_op jit(solution)/shard_map/all_to_all | solution.py:89
  38.3 0.6 reduce_sum.36
  38.9 22.8 %all-gather.2 = f32[16,1,15872]{2,1,0:T(1,128)S(1)} all-gather(f32[1,1,15872]{2,1,0:T(1,128)S(1)} %reshape.134), channel_id=2, replica_groups=mesh['orbit'=16,'space'=16] {'orbit'}, dimensions={0}, use_global_device_ids=true | all-gather | bytes 1079296 | tf_op jit(solution)/shard_map/all_gather | solution.py:92
  61.7 0.3 fusion.5
  62.1 23.3 %all-gather.3 = bf16[16,1,15872]{2,1,0:T(2,128)(2,1)S(1)} all-gather(bf16[1,1,15872]{2,1,0:T(2,128)(2,1)S(1)} %reshape.136), channel_id=1, replica_groups=mesh['orbit'=16,'space'=16] {'space'}, dimensions={0}, use_global_device_ids=true | all-gather | bytes 539648 | tf_op jit(solution)/shard_map/all_gather | solution.py:104
  85.4 3.0 %reduce.11 = bf16[16,15872]{1,0:T(8,128)(2,1)S(1)} reduce(bf16[16,1,15872]{2,1,0:T(2,128)(2,1)S(1)} %all-gather.3, bf16[]{:T(256)} %constant.34), dimensions={1}, to_apply=%all-gather.3.reduce_sub_computation | reduce | bytes 1015810 | tf_op jit(solution)/shard_map/all_gather | solution.py:104
  88.4 0.8 reshape.137
  89.3 1.5 reshape.121.s_ref
  90.8 0.7 reshape.122.n_ref
  91.4 14.1 %shard_map.85 = (bf16[128,2240]{1,0:T(8,128)(2,1)}, bf16[128,2240]{1,0:T(8,128)(2,1)}, f32[20,112,112]{2,1,0:T(8,128)}, f32[20,112]{1,0:T(8,128)}) custom-call(bf16[128,2240]{1,0:T(8,128)(2,1)} %bitcast.37, bf16[128,2240]{1,0:T(8,128)(2,1)} %bitcast.31, f32[128,2240]{1,0:T(8,128)} %bitcast.34, bf16[20,112,112]{2,1,0:T(8,128)(2,1)} %reshape.121.s_ref, ...), custom_call_target="tpu_custom_call" | custom-call | tf_op jit(solution)/shard_map/pallas_call | solution.py:147
  105.6 2.4 %reshape.126 = f32[250880]{0:T(1024)S(1)} reshape(f32[20,112,112]{2,1,0:T(8,128)} %get-tuple-element.16) | data formatting | bytes 2007040 | tf_op jit(solution)/shard_map/reshape | solution.py:85
  108.0 0.1 reshape.127
  108.1 1.0 select_maximum_fusion.2
  109.1 4.3 %all-to-all-start.1 = ((f32[16,1,15872]{2,1,0:T(1,128)}), f32[16,1,15872]{2,1,0:T(1,128)S(1)}, u32[]{:S(2)}, u32[]{:S(2)}) async-start(f32[16,1,15872]{2,1,0:T(1,128)} %bitcast.13), calls=%async_computation.1 | async-start | bytes 2031616 | tf_op jit(solution)/shard_map/all_to_all | solution.py:89
  113.5 2.1 %multiply_add_fusion = f32[1,2,64,2240]{3,2,1,0:T(8,128)} fusion(bf16[1,4,66,2240]{3,2,1,0:T(8,128)(2,1)S(1)} %get-tuple-element.29, f32[2240]{0:T(1024)S(1)} %get-tuple-element.21, f32[2240]{0:T(1024)S(1)} %copy-done.3, f32[2240]{0:T(1024)S(1)} %copy-done.5, f32[2240]{0:T(1024)S(1)} %copy-done.7, f32[2240]{0:T(1024)S(1)} %copy-done.9, ...), kind=kLoop, calls=%fused_computation.12 | loop fusion | flops 7454720 | bytes 6388480 | tf_op jit(solution)/shard_map/add | solution.py:142
  115.6 11.1 %all-to-all-done.1 = f32[16,1,15872]{2,1,0:T(1,128)S(1)} async-done(((f32[16,1,15872]{2,1,0:T(1,128)}), f32[16,1,15872]{2,1,0:T(1,128)S(1)}, u32[]{:S(2)}, u32[]{:S(2)}) %all-to-all-start.1) | async-done | bytes 1015840 | tf_op jit(solution)/shard_map/all_to_all | solution.py:89
  126.7 0.6 reduce_sum.38
  127.4 17.6 %all-gather.4 = f32[16,1,15872]{2,1,0:T(1,128)S(1)} all-gather(f32[1,1,15872]{2,1,0:T(1,128)S(1)} %reshape.138), channel_id=3, replica_groups=mesh['orbit'=16,'space'=16] {'orbit'}, dimensions={0}, use_global_device_ids=true | all-gather | bytes 1079296 | tf_op jit(solution)/shard_map/all_gather | solution.py:99
  145.0 0.3 fusion.4
  145.3 23.1 %all-gather.5 = bf16[16,1,15872]{2,1,0:T(2,128)(2,1)S(1)} all-gather(bf16[1,1,15872]{2,1,0:T(2,128)(2,1)S(1)} %reshape.140), channel_id=1, replica_groups=mesh['orbit'=16,'space'=16] {'space'}, dimensions={0}, use_global_device_ids=true | all-gather | bytes 539648 | tf_op jit(solution)/shard_map/all_gather | solution.py:104
  168.4 3.0 %reduce.12 = bf16[16,15872]{1,0:T(8,128)(2,1)S(1)} reduce(bf16[16,1,15872]{2,1,0:T(2,128)(2,1)S(1)} %all-gather.5, bf16[]{:T(256)} %constant.34), dimensions={1}, to_apply=%all-gather.5.reduce_sub_computation | reduce | bytes 1015810 | tf_op jit(solution)/shard_map/all_gather | solution.py:104
  171.5 0.8 reshape.141
  172.3 1.5 reshape.128.s_ref
  173.8 0.7 reshape.129.n_ref
  174.5 8.4 %shard_map.86 = (bf16[128,2240]{1,0:T(8,128)(2,1)}, bf16[128,2240]{1,0:T(8,128)(2,1)}) custom-call(bf16[128,2240]{1,0:T(8,128)(2,1)} %bitcast.36, bf16[128,2240]{1,0:T(8,128)(2,1)} %bitcast.28, f32[128,2240]{1,0:T(8,128)} %bitcast.33, bf16[20,112,112]{2,1,0:T(8,128)(2,1)} %reshape.128.s_ref, bf16[20,112]{1,0:T(8,128)(2,1)} %reshape.129.n_ref), custom_call_target="tpu_custom_call" | custom-call | tf_op jit(solution)/shard_map/pallas_call | solution.py:157
  (42 shorter events, 0.3 us)
Async XLA Ops:
  3.0 19.1 %collective-permute-start = (bf16[2,1,1,64,2240]{4,3,2,1,0:T(8,128)(2,1)}, bf16[2,1,1,64,2240]{4,3,2,1,0:T(8,128)(2,1)}, u32[]{:S(2)}, u32[]{:S(2)}) collective-permute-start(bf16[2,1,1,64,2240]{4,3,2,1,0:T(8,128)(2,1)} %get-tuple-element.31), channel_id=1, source_target_pairs={{0,1},{1,2},{2,3},{3,4},{4,5},{5,6},{6,7},{7,8},{8,9},{9,10},{10,1... | collective-permute-start | bytes 1720328 | tf_op jit(solution)/shard_map/ppermute | solution.py:19
  5.6 17.0 %collective-permute-start.1 = (bf16[2,1,1,64,2240]{4,3,2,1,0:T(8,128)(2,1)}, bf16[2,1,1,64,2240]{4,3,2,1,0:T(8,128)(2,1)}, u32[]{:S(2)}, u32[]{:S(2)}) collective-permute-start(bf16[2,1,1,64,2240]{4,3,2,1,0:T(8,128)(2,1)} %get-tuple-element.32), channel_id=1, source_target_pairs={{1,0},{2,1},{3,2},{4,3},{5,4},{6,5},{7,6},{8,7},{9,8},{10,9},{11,1... | collective-permute-start | bytes 1720328 | tf_op jit(solution)/shard_map/ppermute | solution.py:21
  10.7 2.2 %copy-start.18 = (f32[20,112]{1,0:T(8,128)S(1)}, f32[20,112]{1,0:T(8,128)}, u32[]{:S(2)}) copy-start(f32[20,112]{1,0:T(8,128)} %get-tuple-element.13) | copy-start | bytes 26884
  14.0 7.8 %copy-start.16 = (bf16[3,3,2240]{2,1,0:T(4,128)(2,1)S(1)}, bf16[3,3,2240]{2,1,0:T(4,128)(2,1)}, u32[]{:S(2)}) copy-start(bf16[3,3,2240]{2,1,0:T(4,128)(2,1)} %param.8) | copy-start | bytes 120964
  14.0 8.6 %copy-start = (bf16[1,2,64,2240]{3,2,1,0:T(8,128)(2,1)S(1)}, bf16[1,2,64,2240]{3,2,1,0:T(8,128)(2,1)}, u32[]{:S(2)}) copy-start(bf16[1,2,64,2240]{3,2,1,0:T(8,128)(2,1)} %param.7) | copy-start | bytes 1720324
  14.0 8.6 %copy-start.1 = (bf16[1,2,64,2240]{3,2,1,0:T(8,128)(2,1)S(1)}, bf16[1,2,64,2240]{3,2,1,0:T(8,128)(2,1)}, u32[]{:S(2)}) copy-start(bf16[1,2,64,2240]{3,2,1,0:T(8,128)(2,1)} %param.9) | copy-start | bytes 1720324
  14.0 24.3 %all-to-all-start = ((f32[16,1,15872]{2,1,0:T(1,128)}), f32[16,1,15872]{2,1,0:T(1,128)S(1)}, u32[]{:S(2)}, u32[]{:S(2)}) async-start(f32[16,1,15872]{2,1,0:T(1,128)} %bitcast.8), calls=%async_computation | async-start | bytes 2031616 | tf_op jit(solution)/shard_map/all_to_all | solution.py:89
  22.0 2.9 %copy-start.2 = (f32[2240]{0:T(1024)}, f32[2240]{0:T(1024)S(1)}, u32[]{:S(2)}) copy-start(f32[2240]{0:T(1024)S(1)} %get-tuple-element.22) | copy-start | bytes 26884
  22.0 2.9 %copy-start.4 = (f32[2240]{0:T(1024)}, f32[2240]{0:T(1024)S(1)}, u32[]{:S(2)}) copy-start(f32[2240]{0:T(1024)S(1)} %get-tuple-element.23) | copy-start | bytes 26884
  22.1 2.9 %copy-start.6 = (f32[2240]{0:T(1024)}, f32[2240]{0:T(1024)S(1)}, u32[]{:S(2)}) copy-start(f32[2240]{0:T(1024)S(1)} %get-tuple-element.24) | copy-start | bytes 26884
  22.1 2.9 %copy-start.8 = (f32[2240]{0:T(1024)}, f32[2240]{0:T(1024)S(1)}, u32[]{:S(2)}) copy-start(f32[2240]{0:T(1024)S(1)} %get-tuple-element.25) | copy-start | bytes 26884
  22.1 2.9 %copy-start.10 = (f32[2240]{0:T(1024)}, f32[2240]{0:T(1024)S(1)}, u32[]{:S(2)}) copy-start(f32[2240]{0:T(1024)S(1)} %get-tuple-element.26) | copy-start | bytes 26884
  22.1 2.9 %copy-start.12 = (f32[2240]{0:T(1024)}, f32[2240]{0:T(1024)S(1)}, u32[]{:S(2)}) copy-start(f32[2240]{0:T(1024)S(1)} %get-tuple-element.27) | copy-start | bytes 26884
  22.1 2.9 %copy-start.14 = (f32[2240]{0:T(1024)}, f32[2240]{0:T(1024)S(1)}, u32[]{:S(2)}) copy-start(f32[2240]{0:T(1024)S(1)} %get-tuple-element.28) | copy-start | bytes 26884
  105.6 2.4 %copy-start.17 = (f32[20,112]{1,0:T(8,128)S(1)}, f32[20,112]{1,0:T(8,128)}, u32[]{:S(2)}) copy-start(f32[20,112]{1,0:T(8,128)} %get-tuple-element.17) | copy-start | bytes 26884
  109.1 4.4 %copy-start.3 = (f32[2240]{0:T(1024)S(1)}, f32[2240]{0:T(1024)}, u32[]{:S(2)}) copy-start(f32[2240]{0:T(1024)} %copy-done.2) | copy-start | bytes 26884
  109.1 4.4 %copy-start.5 = (f32[2240]{0:T(1024)S(1)}, f32[2240]{0:T(1024)}, u32[]{:S(2)}) copy-start(f32[2240]{0:T(1024)} %copy-done.4) | copy-start | bytes 26884
  109.1 4.4 %copy-start.7 = (f32[2240]{0:T(1024)S(1)}, f32[2240]{0:T(1024)}, u32[]{:S(2)}) copy-start(f32[2240]{0:T(1024)} %copy-done.6) | copy-start | bytes 26884
  109.1 4.4 %copy-start.9 = (f32[2240]{0:T(1024)S(1)}, f32[2240]{0:T(1024)}, u32[]{:S(2)}) copy-start(f32[2240]{0:T(1024)} %copy-done.8) | copy-start | bytes 26884
  109.1 4.4 %copy-start.11 = (f32[2240]{0:T(1024)S(1)}, f32[2240]{0:T(1024)}, u32[]{:S(2)}) copy-start(f32[2240]{0:T(1024)} %copy-done.10) | copy-start | bytes 26884
  109.1 4.4 %copy-start.13 = (f32[2240]{0:T(1024)S(1)}, f32[2240]{0:T(1024)}, u32[]{:S(2)}) copy-start(f32[2240]{0:T(1024)} %copy-done.12) | copy-start | bytes 26884
  109.1 4.4 %copy-start.15 = (f32[2240]{0:T(1024)S(1)}, f32[2240]{0:T(1024)}, u32[]{:S(2)}) copy-start(f32[2240]{0:T(1024)} %copy-done.14) | copy-start | bytes 26884
  109.1 17.5 %all-to-all-start.1 = ((f32[16,1,15872]{2,1,0:T(1,128)}), f32[16,1,15872]{2,1,0:T(1,128)S(1)}, u32[]{:S(2)}, u32[]{:S(2)}) async-start(f32[16,1,15872]{2,1,0:T(1,128)} %bitcast.13), calls=%async_computation.1 | async-start | bytes 2031616 | tf_op jit(solution)/shard_map/all_to_all | solution.py:89

commit v3 on v2

v3 whole, which is shorter than its diff:
```python
import jax
import jax.numpy as jnp
from jax import lax
from jax.experimental import pallas as pl
from jax.sharding import PartitionSpec as P

HEADS = 20
HD = 112


def padded_pair(cells, width):
    count = lax.axis_size("space")
    ends = count - 1
    rows = cells.shape[2]
    head = cells[:, :, :width]
    tail = cells[:, :, rows - width :]
    return jnp.concatenate(
        [
            lax.ppermute(tail, "space", [(i, (i + 1) % count) for i in range(ends)]),
            cells,
            lax.ppermute(head, "space", [((i + 1) % count, i) for i in range(ends)]),
        ],
        axis=2,
    )


ROWS = HEADS * HD
PACKED = 2304


def part_kernel(k_ref, v_ref, s_ref):
    s_ref[ROWS:, :] = jnp.zeros((PACKED - ROWS, HD), jnp.float32)
    for h in range(HEADS):
        cols = slice(h * HD, (h + 1) * HD)
        kf = jnp.maximum(k_ref[:, cols], 0)
        vh = v_ref[:, cols]
        s_ref[h * HD : (h + 1) * HD, :] = lax.dot_general(
            kf, vh, (((0,), (0,)), ((), ())), preferred_element_type=jnp.float32
        )
        s_ref[ROWS + h : ROWS + h + 1, :] = jnp.sum(
            kf.astype(jnp.float32), axis=0, keepdims=True
        )


def forward_kernel(q_ref, g_ref, c_ref, s_ref, a_ref, gq_ref, sg_ref):
    sg_ref[ROWS:, :] = jnp.zeros((PACKED - ROWS, HD), jnp.float32)
    for h in range(HEADS):
        cols = slice(h * HD, (h + 1) * HD)
        qh = q_ref[:, cols]
        qf = jnp.maximum(qh, 0)
        qw = qf.astype(jnp.float32)
        state = s_ref[h * HD : (h + 1) * HD, :]
        norm = s_ref[ROWS + h : ROWS + h + 1, :].astype(jnp.float32)
        numerator = jnp.dot(qf, state, preferred_element_type=jnp.float32)
        denominator = jnp.sum(qw * norm, axis=1, keepdims=True) + 1.0
        inverse = 1.0 / denominator
        a_ref[:, cols] = (numerator * inverse + c_ref[:, cols]).astype(jnp.bfloat16)
        gw = g_ref[:, cols].astype(jnp.float32)
        num_grad = (gw * inverse).astype(jnp.bfloat16)
        den_grad = (
            -jnp.sum(gw * numerator, axis=1, keepdims=True) * (inverse * inverse)
        ).astype(jnp.bfloat16).astype(jnp.float32)
        query_grad = lax.dot_general(
            num_grad, state, (((1,), (1,)), ((), ())), preferred_element_type=jnp.float32
        )
        query_grad = query_grad + den_grad * norm
        gq_ref[:, cols] = jnp.where(qh > 0, query_grad, 0.0).astype(jnp.bfloat16)
        sg_ref[h * HD : (h + 1) * HD, :] = lax.dot_general(
            qf, num_grad, (((0,), (0,)), ((), ())), preferred_element_type=jnp.float32
        )
        sg_ref[ROWS + h : ROWS + h + 1, :] = jnp.sum(den_grad * qw, axis=0, keepdims=True)


def backward_kernel(k_ref, v_ref, c_ref, s_ref, gk_ref, gv_ref):
    for h in range(HEADS):
        cols = slice(h * HD, (h + 1) * HD)
        kh = k_ref[:, cols]
        kf = jnp.maximum(kh, 0)
        vh = v_ref[:, cols]
        state = s_ref[h * HD : (h + 1) * HD, :]
        norm = s_ref[ROWS + h : ROWS + h + 1, :].astype(jnp.float32)
        key_grad = lax.dot_general(
            vh, state, (((1,), (1,)), ((), ())), preferred_element_type=jnp.float32
        )
        gk_ref[:, cols] = jnp.where(kh > 0, key_grad + norm, 0.0).astype(jnp.bfloat16)
        value_grad = jnp.dot(kf, state, preferred_element_type=jnp.float32) + c_ref[:, cols]
        gv_ref[:, cols] = value_grad.astype(jnp.bfloat16)


def spread_states(packed, reverse, counts):
    space = lax.axis_size("space")
    orbit = lax.axis_size("orbit")
    place = lax.axis_index("orbit")
    pieces = lax.all_to_all(packed.reshape(space, -1, HD), "space", 0, 0, tiled=True)
    whole = jnp.sum(pieces, axis=0)
    views = jnp.arange(orbit)
    if not reverse:
        gathered = lax.all_gather(whole, "orbit")
        keep = views <= place
        summed = jnp.sum(jnp.where(keep[:, None, None], gathered, 0.0), axis=0)
        summed = summed / counts
    else:
        whole = whole / counts
        gathered = lax.all_gather(whole, "orbit")
        keep = views >= place
        summed = jnp.sum(jnp.where(keep[:, None, None], gathered, 0.0), axis=0)
    rounded = summed.astype(jnp.bfloat16)
    return lax.all_gather(rounded, "space", tiled=True)


def on_device(queries, keys_in, values, conv_weight, grad_out):
    view_count, row_count, col_count, feature_width = queries.shape
    token_count = view_count * row_count * col_count
    flat_shape = (token_count, feature_width)
    q2 = queries.reshape(flat_shape)
    k2 = keys_in.reshape(flat_shape)
    v2 = values.reshape(flat_shape)
    g2 = grad_out.reshape(flat_shape)
    place = lax.axis_index("orbit")
    count = (place.astype(jnp.float32) + 1.0) * float(
        row_count * lax.axis_size("space") * col_count
    )
    f32 = jnp.float32
    packed_part = pl.pallas_call(
        part_kernel, out_shape=jax.ShapeDtypeStruct((PACKED, HD), f32)
    )(k2, v2)
    state_b = spread_states(packed_part, False, count)

    pair = padded_pair(jnp.stack([values, grad_out]), 1)
    pair = jnp.pad(pair, ((0, 0), (0, 0), (0, 0), (1, 1), (0, 0)))
    value_pad, grad_pad = pair[0], pair[1]
    weight_wide = conv_weight.astype(f32)
    conv_term = jnp.zeros(queries.shape, f32)
    conv_grad = jnp.zeros(queries.shape, f32)
    for row_step in range(3):
        for col_step in range(3):
            conv_term = conv_term + weight_wide[row_step, col_step] * value_pad[
                :, row_step : row_step + row_count, col_step : col_step + col_count
            ].astype(f32)
            conv_grad = conv_grad + weight_wide[row_step, col_step] * grad_pad[
                :, 2 - row_step : 2 - row_step + row_count, 2 - col_step : 2 - col_step + col_count
            ].astype(f32)

    bf = jnp.bfloat16
    attended, grad_query, state_grad = pl.pallas_call(
        forward_kernel,
        out_shape=(
            jax.ShapeDtypeStruct(flat_shape, bf),
            jax.ShapeDtypeStruct(flat_shape, bf),
            jax.ShapeDtypeStruct((PACKED, HD), f32),
        ),
    )(q2, g2, conv_term.reshape(flat_shape), state_b)
    back_state = spread_states(state_grad, True, count)
    grad_key, grad_value = pl.pallas_call(
        backward_kernel,
        out_shape=(
            jax.ShapeDtypeStruct(flat_shape, bf),
            jax.ShapeDtypeStruct(flat_shape, bf),
        ),
    )(k2, v2, conv_grad.reshape(flat_shape), back_state)
    shape = queries.shape
    return (
        attended.reshape(shape),
        grad_query.reshape(shape),
        grad_key.reshape(shape),
        grad_value.reshape(shape),
    )


def solution(mesh):
    placed = (
        P("orbit", "space", None, None),
        P("orbit", "space", None, None),
        P("orbit", "space", None, None),
        P(),
        P("orbit", "space", None, None),
    )
    return jax.shard_map(
        on_device,
        mesh=mesh,
        in_specs=placed,
        out_specs=(
            P("orbit", "space", None, None),
            P("orbit", "space", None, None),
            P("orbit", "space", None, None),
            P("orbit", "space", None, None),
        ),
        check_vma=False,
    )
```

time: 185 us -> 173 us (0.935)
  local copies, waits for them, and re-layouts: 11.4 us -> 1.57 us
  other arithmetic: 18.7 us -> 9.92 us
  blocking collectives: 86.8 us -> 91.8 us
  waiting for transfers between devices: 22.7 us -> 24.6 us
    reshape x8 -> x0, local copies, waits for them, and re-layouts: 9.07 us -> none  [the longest x4 4.7 us: spread_states(): flat = jnp.concatenate([state_part.reshape(-1), norm_part.reshape(-1)])]
    all_gather x2 -> x0, other arithmetic: 6.08 us -> none  [spread_states(): full = lax.all_gather(rounded, 'space', tiled=True)[:total]]
    all_gather x2, blocking collectives: 46.4 us -> 50.2 us  [spread_states(): return lax.all_gather(rounded, 'space', tiled=True)]
    ppermute x1, waiting for transfers between devices: 0.45 us -> 3.88 us  [padded_pair(): lax.ppermute(head, 'space', [((i + 1) % count, i) for i in range(ends)])]
    concatenate x2 -> x0, other arithmetic: 2.08 us -> none  [spread_states(): flat = jnp.concatenate([state_part.reshape(-1), norm_part.reshape(-1)])]
where the time goes in v3:
time: 173 us; the launch traced here: 171 us
  blocking collectives  91.8 us (53%)
  Pallas kernels  26.3 us (15%)
  waiting for transfers between devices  24.6 us (14%)
  starting transfers between devices  16 us (9%)
  other arithmetic  9.92 us (6%)
    all_gather x2, blocking collectives, spread_states(): return lax.all_gather(rounded, 'space', tiled=True)  50.2 us
    all_gather x2, blocking collectives, spread_states(): gathered = lax.all_gather(whole, 'orbit')  41.6 us
    all_to_all x2, waiting for transfers between devices, spread_states(): lax.all_to_all(packed.reshape(space, -1, HD), 'space', 0, 0, tiled=True)  20.7 us
    pallas_call x1, Pallas kernels, on_device(): pl.pallas_call(forward_kernel, out_shape=(jax.ShapeDtypeStruct(flat_shape...  14.1 us
    all_to_all x2, starting transfers between devices, spread_states(): lax.all_to_all(packed.reshape(space, -1, HD), 'space', 0, 0, tiled=True)  12.9 us
    pallas_call x1, Pallas kernels, on_device(): pl.pallas_call(backward_kernel, out_shape=(jax.ShapeDtypeStruct(flat_shap...  8.35 us
    ppermute x1, waiting for transfers between devices, padded_pair(): lax.ppermute(head, 'space', [((i + 1) % count, i) for i in range(ends)])  3.88 us
    pallas_call x1, Pallas kernels, on_device(): pl.pallas_call(part_kernel, out_shape=jax.ShapeDtypeStruct((PACKED, HD),...  3.82 us
  transfers between devices with their start and end apart: 4, of which 3 were waited for; matrix products, arithmetic and copies ran while one was open for 5% of the time, Pallas kernels for 2%

profile of v3, /device:TPU:0, one launch (start us, length us, event | category | flops | bytes accessed | tf_op | source)
XLA Modules:
  0.0 171.2 jit_solution(8464041989530783104)
XLA Ops:
  0.6 1.3 fusion.4
  2.0 1.8 %collective-permute-start = (bf16[2,1,1,64,2240]{4,3,2,1,0:T(8,128)(2,1)S(1)}, bf16[2,1,1,64,2240]{4,3,2,1,0:T(8,128)(2,1)S(1)}, u32[]{:S(2)}, u32[]{:S(2)}) collective-permute-start(bf16[2,1,1,64,2240]{4,3,2,1,0:T(8,128)(2,1)S(1)} %get-tuple-element.25), channel_id=1, source_target_pairs={{0,1},{1,2},{2,3},{3,4},{4,5},{5,6},{6,7},{7,8},{8,9},{9,10},{10,1... | collective-permute-start | bytes 1720328 | tf_op jit(solution)/shard_map/ppermute | solution.py:19
  3.8 1.3 collective-permute-start.1
  5.1 3.8 %shard_map.84 = f32[2304,112]{1,0:T(8,128)} custom-call(bf16[128,2240]{1,0:T(8,128)(2,1)} %bitcast.32, bf16[128,2240]{1,0:T(8,128)(2,1)} %bitcast.21), custom_call_target="tpu_custom_call" | custom-call | tf_op jit(solution)/shard_map/pallas_call | solution.py:124
  8.9 8.2 %all-to-all-start = ((f32[16,144,112]{2,1,0:T(8,128)}), f32[16,144,112]{2,1,0:T(8,128)}, u32[]{:S(2)}, u32[]{:S(2)}) async-start(f32[16,144,112]{2,1,0:T(8,128)} %bitcast.27), calls=%async_computation | async-start | bytes 2359296 | tf_op jit(solution)/shard_map/all_to_all | solution.py:94
  17.2 1.5 convert_element_type.68
  18.6 1.3 slice_reduce_fusion.8
  20.0 0.0 copy-start.2
  20.0 0.0 copy-start.4
  20.0 0.0 copy-start.6
  20.0 0.0 copy-start.8
  20.0 0.0 copy-start.10
  20.0 0.0 copy-start.12
  20.0 0.0 copy-start.14
  20.0 0.0 copy-start.16
  20.0 0.0 collective-permute-done
  20.1 3.9 %collective-permute-done.1 = bf16[2,1,1,64,2240]{4,3,2,1,0:T(8,128)(2,1)S(1)} collective-permute-done((bf16[2,1,1,64,2240]{4,3,2,1,0:T(8,128)(2,1)S(1)}, bf16[2,1,1,64,2240]{4,3,2,1,0:T(8,128)(2,1)S(1)}, u32[]{:S(2)}, u32[]{:S(2)}) %collective-permute-start.1) | collective-permute-done | bytes 573472 | tf_op jit(solution)/shard_map/ppermute | solution.py:21
  23.9 0.0 copy-done
  23.9 0.0 copy-done.1
  23.9 1.1 select_maximum_fusion
  25.0 0.2 slice_bitcast_fusion
  25.2 0.0 copy-done.2
  25.2 0.0 copy-done.4
  25.2 0.0 copy-done.6
  25.3 0.0 copy-done.8
  25.3 0.0 copy-done.10
  25.3 0.0 copy-done.12
  25.3 0.0 copy-done.14
  25.3 0.0 copy-done.16
  25.3 2.1 %multiply_add_fusion.1 = f32[1,2,64,2240]{3,2,1,0:T(8,128)} fusion(bf16[1,4,66,2240]{3,2,1,0:T(8,128)(2,1)S(1)} %get-tuple-element.24, f32[2240]{0:T(1024)S(1)} %get-tuple-element.15, f32[2240]{0:T(1024)S(1)} %get-tuple-element.16, f32[2240]{0:T(1024)S(1)} %get-tuple-element.17, f32[2240]{0:T(1024)S(1)} %get-tuple-element.18, ...), kind=kLoop, calls=%fused_computation.15 | loop fusion | flops 7454720 | bytes 6388480 | tf_op jit(solution)/shard_map/add | solution.py:137
  27.4 8.4 %all-to-all-done = f32[16,144,112]{2,1,0:T(8,128)} async-done(((f32[16,144,112]{2,1,0:T(8,128)}), f32[16,144,112]{2,1,0:T(8,128)}, u32[]{:S(2)}, u32[]{:S(2)}) %all-to-all-start) | async-done | bytes 1032224 | tf_op jit(solution)/shard_map/all_to_all | solution.py:94
  35.8 1.4 reduce_sum.36
  37.1 23.3 %all-gather = f32[2304,112]{1,0:T(8,128)S(1)} all-gather(f32[144,112]{1,0:T(8,128)S(1)} %reduce_sum.36), channel_id=2, replica_groups=mesh['orbit'=16,'space'=16] {'orbit'}, dimensions={0}, use_global_device_ids=true | all-gather | bytes 1096704 | tf_op jit(solution)/shard_map/all_gather | solution.py:98
  60.5 0.2 select_reduce_fusion.1
  60.7 25.7 %all_gather.18.s_ref = bf16[2304,112]{1,0:T(8,128)(2,1)} all-gather(bf16[144,112]{1,0:T(8,128)(2,1)S(1)} %divide_convert_fusion), channel_id=1, replica_groups=mesh['orbit'=16,'space'=16] {'space'}, dimensions={0}, use_global_device_ids=true | all-gather | bytes 548352 | tf_op jit(solution)/shard_map/all_gather | solution.py:108
  86.4 14.1 %shard_map.85 = (bf16[128,2240]{1,0:T(8,128)(2,1)}, bf16[128,2240]{1,0:T(8,128)(2,1)}, f32[2304,112]{1,0:T(8,128)}) custom-call(bf16[128,2240]{1,0:T(8,128)(2,1)} %bitcast.35, bf16[128,2240]{1,0:T(8,128)(2,1)} %bitcast.25, f32[128,2240]{1,0:T(8,128)} %bitcast.31, bf16[2304,112]{1,0:T(8,128)(2,1)} %all_gather.18.s_ref), custom_call_target="tpu_custom_call" | custom-call | tf_op jit(solution)/shard_map/pallas_call | solution.py:145
  100.5 0.0 copy-start.9
  100.5 0.0 copy-start.11
  100.5 0.0 copy-start.13
  100.6 0.0 copy-start.15
  100.6 4.7 %all-to-all-start.1 = ((f32[16,144,112]{2,1,0:T(8,128)}), f32[16,144,112]{2,1,0:T(8,128)S(1)}, u32[]{:S(2)}, u32[]{:S(2)}) async-start(f32[16,144,112]{2,1,0:T(8,128)} %bitcast.34), calls=%async_computation.1 | async-start | bytes 2359296 | tf_op jit(solution)/shard_map/all_to_all | solution.py:94
  105.3 2.1 %multiply_add_fusion = f32[1,2,64,2240]{3,2,1,0:T(8,128)} fusion(bf16[1,4,66,2240]{3,2,1,0:T(8,128)(2,1)S(1)} %get-tuple-element.23, f32[2240]{0:T(1024)S(1)} %copy-done.3, f32[2240]{0:T(1024)S(1)} %copy-done.5, f32[2240]{0:T(1024)S(1)} %copy-done.7, f32[2240]{0:T(1024)S(1)} %copy-done.9, f32[2240]{0:T(1024)S(1)} %copy-done.11, f32[2240]{0:T(1024)S(1)} %copy-done.13, ...), kind=kLoop, calls=%fused_computation.13 | loop fusion | flops 7454720 | bytes 6388480 | tf_op jit(solution)/shard_map/add | solution.py:140
  107.4 12.3 %all-to-all-done.1 = f32[16,144,112]{2,1,0:T(8,128)S(1)} async-done(((f32[16,144,112]{2,1,0:T(8,128)}), f32[16,144,112]{2,1,0:T(8,128)S(1)}, u32[]{:S(2)}, u32[]{:S(2)}) %all-to-all-start.1) | async-done | bytes 1032224 | tf_op jit(solution)/shard_map/all_to_all | solution.py:94
  119.7 0.1 reduce_sum.38
  119.9 18.3 %all-gather.1 = f32[2304,112]{1,0:T(8,128)S(1)} all-gather(f32[144,112]{1,0:T(8,128)S(1)} %broadcast_divide_fusion), channel_id=3, replica_groups=mesh['orbit'=16,'space'=16] {'orbit'}, dimensions={0}, use_global_device_ids=true | all-gather | bytes 1096704 | tf_op jit(solution)/shard_map/all_gather | solution.py:104
  138.1 0.2 select_reduce_fusion
  138.3 24.5 %all_gather.20.s_ref = bf16[2304,112]{1,0:T(8,128)(2,1)} all-gather(bf16[144,112]{1,0:T(8,128)(2,1)S(1)} %select_reduce_fusion), channel_id=1, replica_groups=mesh['orbit'=16,'space'=16] {'space'}, dimensions={0}, use_global_device_ids=true | all-gather | bytes 548352 | tf_op jit(solution)/shard_map/all_gather | solution.py:108
  162.8 8.4 %shard_map.86 = (bf16[128,2240]{1,0:T(8,128)(2,1)}, bf16[128,2240]{1,0:T(8,128)(2,1)}) custom-call(bf16[128,2240]{1,0:T(8,128)(2,1)} %bitcast.33, bf16[128,2240]{1,0:T(8,128)(2,1)} %bitcast.22, f32[128,2240]{1,0:T(8,128)} %bitcast.30, bf16[2304,112]{1,0:T(8,128)(2,1)} %all_gather.20.s_ref), custom_call_target="tpu_custom_call" | custom-call | tf_op jit(solution)/shard_map/pallas_call | solution.py:154
  (18 shorter events, 0.1 us)
Async XLA Ops:
  2.0 18.1 %collective-permute-start = (bf16[2,1,1,64,2240]{4,3,2,1,0:T(8,128)(2,1)S(1)}, bf16[2,1,1,64,2240]{4,3,2,1,0:T(8,128)(2,1)S(1)}, u32[]{:S(2)}, u32[]{:S(2)}) collective-permute-start(bf16[2,1,1,64,2240]{4,3,2,1,0:T(8,128)(2,1)S(1)} %get-tuple-element.25), channel_id=1, source_target_pairs={{0,1},{1,2},{2,3},{3,4},{4,5},{5,6},{6,7},{7,8},{8,9},{9,10},{10,1... | collective-permute-start | bytes 1720328 | tf_op jit(solution)/shard_map/ppermute | solution.py:19
  3.8 20.2 %collective-permute-start.1 = (bf16[2,1,1,64,2240]{4,3,2,1,0:T(8,128)(2,1)S(1)}, bf16[2,1,1,64,2240]{4,3,2,1,0:T(8,128)(2,1)S(1)}, u32[]{:S(2)}, u32[]{:S(2)}) collective-permute-start(bf16[2,1,1,64,2240]{4,3,2,1,0:T(8,128)(2,1)S(1)} %get-tuple-element.26), channel_id=1, source_target_pairs={{1,0},{2,1},{3,2},{4,3},{5,4},{6,5},{7,6},{8,7},{9,8},{10,9},{11,1... | collective-permute-start | bytes 1720328 | tf_op jit(solution)/shard_map/ppermute | solution.py:21
  8.9 15.0 %copy-start = (bf16[1,2,64,2240]{3,2,1,0:T(8,128)(2,1)S(1)}, bf16[1,2,64,2240]{3,2,1,0:T(8,128)(2,1)}, u32[]{:S(2)}) copy-start(bf16[1,2,64,2240]{3,2,1,0:T(8,128)(2,1)} %param.7) | copy-start | bytes 1720324
  8.9 15.0 %copy-start.1 = (bf16[1,2,64,2240]{3,2,1,0:T(8,128)(2,1)S(1)}, bf16[1,2,64,2240]{3,2,1,0:T(8,128)(2,1)}, u32[]{:S(2)}) copy-start(bf16[1,2,64,2240]{3,2,1,0:T(8,128)(2,1)} %param.9) | copy-start | bytes 1720324
  8.9 26.9 %all-to-all-start = ((f32[16,144,112]{2,1,0:T(8,128)}), f32[16,144,112]{2,1,0:T(8,128)}, u32[]{:S(2)}, u32[]{:S(2)}) async-start(f32[16,144,112]{2,1,0:T(8,128)} %bitcast.27), calls=%async_computation | async-start | bytes 2359296 | tf_op jit(solution)/shard_map/all_to_all | solution.py:94
  20.0 5.3 %copy-start.2 = (f32[2240]{0:T(1024)}, f32[2240]{0:T(1024)S(1)}, u32[]{:S(2)}) copy-start(f32[2240]{0:T(1024)S(1)} %get-tuple-element.15) | copy-start | bytes 26884
  20.0 5.3 %copy-start.4 = (f32[2240]{0:T(1024)}, f32[2240]{0:T(1024)S(1)}, u32[]{:S(2)}) copy-start(f32[2240]{0:T(1024)S(1)} %get-tuple-element.16) | copy-start | bytes 26884
  20.0 5.3 %copy-start.6 = (f32[2240]{0:T(1024)}, f32[2240]{0:T(1024)S(1)}, u32[]{:S(2)}) copy-start(f32[2240]{0:T(1024)S(1)} %get-tuple-element.17) | copy-start | bytes 26884
  20.0 5.3 %copy-start.8 = (f32[2240]{0:T(1024)}, f32[2240]{0:T(1024)S(1)}, u32[]{:S(2)}) copy-start(f32[2240]{0:T(1024)S(1)} %get-tuple-element.18) | copy-start | bytes 26884
  20.0 5.3 %copy-start.10 = (f32[2240]{0:T(1024)}, f32[2240]{0:T(1024)S(1)}, u32[]{:S(2)}) copy-start(f32[2240]{0:T(1024)S(1)} %get-tuple-element.19) | copy-start | bytes 26884
  20.0 5.3 %copy-start.12 = (f32[2240]{0:T(1024)}, f32[2240]{0:T(1024)S(1)}, u32[]{:S(2)}) copy-start(f32[2240]{0:T(1024)S(1)} %get-tuple-element.20) | copy-start | bytes 26884
  20.0 5.3 %copy-start.14 = (f32[2240]{0:T(1024)}, f32[2240]{0:T(1024)S(1)}, u32[]{:S(2)}) copy-start(f32[2240]{0:T(1024)S(1)} %get-tuple-element.21) | copy-start | bytes 26884
  20.0 5.3 %copy-start.16 = (f32[2240]{0:T(1024)}, f32[2240]{0:T(1024)S(1)}, u32[]{:S(2)}) copy-start(f32[2240]{0:T(1024)S(1)} %get-tuple-element.22) | copy-start | bytes 26884
  100.5 4.7 %copy-start.3 = (f32[2240]{0:T(1024)S(1)}, f32[2240]{0:T(1024)}, u32[]{:S(2)}) copy-start(f32[2240]{0:T(1024)} %copy-done.2) | copy-start | bytes 26884
  100.5 4.7 %copy-start.5 = (f32[2240]{0:T(1024)S(1)}, f32[2240]{0:T(1024)}, u32[]{:S(2)}) copy-start(f32[2240]{0:T(1024)} %copy-done.4) | copy-start | bytes 26884
  100.5 4.8 %copy-start.7 = (f32[2240]{0:T(1024)S(1)}, f32[2240]{0:T(1024)}, u32[]{:S(2)}) copy-start(f32[2240]{0:T(1024)} %copy-done.6) | copy-start | bytes 26884
  100.5 4.8 %copy-start.9 = (f32[2240]{0:T(1024)S(1)}, f32[2240]{0:T(1024)}, u32[]{:S(2)}) copy-start(f32[2240]{0:T(1024)} %copy-done.8) | copy-start | bytes 26884
  100.5 4.8 %copy-start.11 = (f32[2240]{0:T(1024)S(1)}, f32[2240]{0:T(1024)}, u32[]{:S(2)}) copy-start(f32[2240]{0:T(1024)} %copy-done.10) | copy-start | bytes 26884
  100.5 4.8 %copy-start.13 = (f32[2240]{0:T(1024)S(1)}, f32[2240]{0:T(1024)}, u32[]{:S(2)}) copy-start(f32[2240]{0:T(1024)} %copy-done.12) | copy-start | bytes 26884
  100.6 4.8 %copy-start.15 = (f32[2240]{0:T(1024)S(1)}, f32[2240]{0:T(1024)}, u32[]{:S(2)}) copy-start(f32[2240]{0:T(1024)} %copy-done.14) | copy-start | bytes 26884
  100.6 4.8 %copy-start.17 = (f32[2240]{0:T(1024)S(1)}, f32[2240]{0:T(1024)}, u32[]{:S(2)}) copy-start(f32[2240]{0:T(1024)} %copy-done.16) | copy-start | bytes 26884
  100.6 19.2 %all-to-all-start.1 = ((f32[16,144,112]{2,1,0:T(8,128)}), f32[16,144,112]{2,1,0:T(8,128)S(1)}, u32[]{:S(2)}, u32[]{:S(2)}) async-start(f32[16,144,112]{2,1,0:T(8,128)} %bitcast.34), calls=%async_computation.1 | async-start | bytes 2359296 | tf_op jit(solution)/shard_map/all_to_all | solution.py:94

commit v4 on v3

--- a/solution.py
+++ b/solution.py
@@ -26,72 +26,88 @@
 
 ROWS = HEADS * HD
 PACKED = 2304
+LANES = 128
+NORM = HD
+
+
+def lane_one(tokens):
+    lanes = lax.broadcasted_iota(jnp.int32, (tokens, LANES - HD), 1)
+    return (lanes == 0).astype(jnp.bfloat16)
 
 
 def part_kernel(k_ref, v_ref, s_ref):
-    s_ref[ROWS:, :] = jnp.zeros((PACKED - ROWS, HD), jnp.float32)
+    s_ref[ROWS:, :] = jnp.zeros((PACKED - ROWS, LANES), jnp.float32)
+    extra = lane_one(k_ref.shape[0])
     for h in range(HEADS):
         cols = slice(h * HD, (h + 1) * HD)
         kf = jnp.maximum(k_ref[:, cols], 0)
-        vh = v_ref[:, cols]
+        v_ext = jnp.concatenate([v_ref[:, cols], extra], axis=1)
         s_ref[h * HD : (h + 1) * HD, :] = lax.dot_general(
-            kf, vh, (((0,), (0,)), ((), ())), preferred_element_type=jnp.float32
-        )
-        s_ref[ROWS + h : ROWS + h + 1, :] = jnp.sum(
-            kf.astype(jnp.float32), axis=0, keepdims=True
-        )
-
-
-def forward_kernel(q_ref, g_ref, c_ref, s_ref, a_ref, gq_ref, sg_ref):
-    sg_ref[ROWS:, :] = jnp.zeros((PACKED - ROWS, HD), jnp.float32)
+            kf, v_ext, (((0,), (0,)), ((), ())), preferred_element_type=jnp.float32
+        )
+
+
+def head_terms(qh, gh, state):
+    qf = jnp.maximum(qh, 0)
+    wide = jnp.dot(qf, state, preferred_element_type=jnp.float32)
+    numerator = wide[:, :HD]
+    denominator = wide[:, NORM : NORM + 1] + 1.0
+    inverse = 1.0 / denominator
+    gw = gh.astype(jnp.float32)
+    num_grad = (gw * inverse).astype(jnp.bfloat16)
+    den_grad = (
+        -jnp.sum(gw * numerator, axis=1, keepdims=True) / (denominator * denominator)
+    ).astype(jnp.bfloat16)
+    pad = jnp.zeros((qh.shape[0], LANES - HD - 1), jnp.bfloat16)
+    grads = jnp.concatenate([num_grad, den_grad, pad], axis=1)
+    return qf, numerator, inverse, grads
+
+
+def state_grad_kernel(q_ref, g_ref, s_ref, sg_ref):
+    sg_ref[ROWS:, :] = jnp.zeros((PACKED - ROWS, LANES), jnp.float32)
+    for h in range(HEADS):
+        cols = slice(h * HD, (h + 1) * HD)
+        state = s_ref[h * HD : (h + 1) * HD, :]
+        qf, _, _, grads = head_terms(q_ref[:, cols], g_ref[:, cols], state)
+        sg_ref[h * HD : (h + 1) * HD, :] = lax.dot_general(
+            qf, grads, (((0,), (0,)), ((), ())), preferred_element_type=jnp.float32
+        )
+
+
+def forward_kernel(q_ref, g_ref, c_ref, s_ref, a_ref, gq_ref):
     for h in range(HEADS):
         cols = slice(h * HD, (h + 1) * HD)
         qh = q_ref[:, cols]
-        qf = jnp.maximum(qh, 0)
-        qw = qf.astype(jnp.float32)
         state = s_ref[h * HD : (h + 1) * HD, :]
-        norm = s_ref[ROWS + h : ROWS + h + 1, :].astype(jnp.float32)
-        numerator = jnp.dot(qf, state, preferred_element_type=jnp.float32)
-        denominator = jnp.sum(qw * norm, axis=1, keepdims=True) + 1.0
-        inverse = 1.0 / denominator
+        _, numerator, inverse, grads = head_terms(qh, g_ref[:, cols], state)
         a_ref[:, cols] = (numerator * inverse + c_ref[:, cols]).astype(jnp.bfloat16)
-        gw = g_ref[:, cols].astype(jnp.float32)
-        num_grad = (gw * inverse).astype(jnp.bfloat16)
-        den_grad = (
-            -jnp.sum(gw * numerator, axis=1, keepdims=True) * (inverse * inverse)
-        ).astype(jnp.bfloat16).astype(jnp.float32)
         query_grad = lax.dot_general(
-            num_grad, state, (((1,), (1,)), ((), ())), preferred_element_type=jnp.float32
-        )
-        query_grad = query_grad + den_grad * norm
+            grads, state, (((1,), (1,)), ((), ())), preferred_element_type=jnp.float32
+        )
         gq_ref[:, cols] = jnp.where(qh > 0, query_grad, 0.0).astype(jnp.bfloat16)
-        sg_ref[h * HD : (h + 1) * HD, :] = lax.dot_general(
-            qf, num_grad, (((0,), (0,)), ((), ())), preferred_element_type=jnp.float32
-        )
-        sg_ref[ROWS + h : ROWS + h + 1, :] = jnp.sum(den_grad * qw, axis=0, keepdims=True)
 
 
 def backward_kernel(k_ref, v_ref, c_ref, s_ref, gk_ref, gv_ref):
+    extra = lane_one(k_ref.shape[0])
     for h in range(HEADS):
         cols = slice(h * HD, (h + 1) * HD)
         kh = k_ref[:, cols]
         kf = jnp.maximum(kh, 0)
-        vh = v_ref[:, cols]
+        v_ext = jnp.concatenate([v_ref[:, cols], extra], axis=1)
         state = s_ref[h * HD : (h + 1) * HD, :]
-        norm = s_ref[ROWS + h : ROWS + h + 1, :].astype(jnp.float32)
         key_grad = lax.dot_general(
-            vh, state, (((1,), (1,)), ((), ())), preferred_element_type=jnp.float32
-        )
-        gk_ref[:, cols] = jnp.where(kh > 0, key_grad + norm, 0.0).astype(jnp.bfloat16)
-        value_grad = jnp.dot(kf, state, preferred_element_type=jnp.float32) + c_ref[:, cols]
-        gv_ref[:, cols] = value_grad.astype(jnp.bfloat16)
+            v_ext, state, (((1,), (1,)), ((), ())), preferred_element_type=jnp.float32
+        )
+        gk_ref[:, cols] = jnp.where(kh > 0, key_grad, 0.0).astype(jnp.bfloat16)
+        value_grad = jnp.dot(kf, state, preferred_element_type=jnp.float32)[:, :HD]
+        gv_ref[:, cols] = (value_grad + c_ref[:, cols]).astype(jnp.bfloat16)
 
 
 def spread_states(packed, reverse, counts):
     space = lax.axis_size("space")
     orbit = lax.axis_size("orbit")
     place = lax.axis_index("orbit")
-    pieces = lax.all_to_all(packed.reshape(space, -1, HD), "space", 0, 0, tiled=True)
+    pieces = lax.all_to_all(packed.reshape(space, -1, LANES), "space", 0, 0, tiled=True)
     whole = jnp.sum(pieces, axis=0)
     views = jnp.arange(orbit)
     if not reverse:
@@ -122,7 +138,7 @@
     )
     f32 = jnp.float32
     packed_part = pl.pallas_call(
-        part_kernel, out_shape=jax.ShapeDtypeStruct((PACKED, HD), f32)
+        part_kernel, out_shape=jax.ShapeDtypeStruct((PACKED, LANES), f32)
     )(k2, v2)
     state_b = spread_states(packed_part, False, count)
 
@@ -142,12 +158,14 @@
             ].astype(f32)
 
     bf = jnp.bfloat16
-    attended, grad_query, state_grad = pl.pallas_call(
+    state_grad = pl.pallas_call(
+        state_grad_kernel, out_shape=jax.ShapeDtypeStruct((PACKED, LANES), f32)
+    )(q2, g2, state_b)
+    attended, grad_query = pl.pallas_call(
         forward_kernel,
         out_shape=(
             jax.ShapeDtypeStruct(flat_shape, bf),
             jax.ShapeDtypeStruct(flat_shape, bf),
-            jax.ShapeDtypeStruct((PACKED, HD), f32),
         ),
     )(q2, g2, conv_term.reshape(flat_shape), state_b)
     back_state = spread_states(state_grad, True, count)

time: 173 us -> 212 us (1.23)
  waiting for transfers between devices: 24.6 us -> 61.5 us
  blocking collectives: 91.8 us -> 76.6 us
  between operations: 0.98 us -> 14.1 us
  Pallas kernels: 26.3 us -> 32.4 us
  starting transfers between devices: 16 us -> 11.6 us
    all_gather x0 -> x2, waiting for transfers between devices: none -> 50.6 us  [spread_states(): gathered = lax.all_gather(whole, 'orbit')]
    all_gather x2 -> x0, blocking collectives: 41.6 us -> none  [spread_states(): gathered = lax.all_gather(whole, 'orbit')]
    all_to_all x0 -> x1, blocking collectives: none -> 23.8 us  [spread_states(): lax.all_to_all(packed.reshape(space, -1, LANES), 'space', 0, 0, tiled=True)]
    all_to_all x2 -> x1, waiting for transfers between devices: 20.7 us -> 10.8 us  [spread_states(): lax.all_to_all(packed.reshape(space, -1, LANES), 'space', 0, 0, tiled=True)]
    pallas_call x1 -> x2, Pallas kernels: 3.82 us -> 13.6 us  [the longest x1 9.93 us: on_device(): pl.pallas_call(state_grad_kernel, out_shape=jax.ShapeDtypeStruct((PACKED,...]
    all_to_all x2 -> x1, starting transfers between devices: 12.9 us -> 4.68 us  [spread_states(): lax.all_to_all(packed.reshape(space, -1, LANES), 'space', 0, 0, tiled=True)]
    ppermute x1, waiting for transfers between devices: 3.88 us -> 0.01 us  [padded_pair(): lax.ppermute(head, 'space', [((i + 1) % count, i) for i in range(ends)])]
    pallas_call x1, Pallas kernels: 14.1 us -> 10.4 us  [on_device(): pl.pallas_call(forward_kernel, out_shape=(jax.ShapeDtypeStruct(flat_shape...]
  transfers between devices with their start and end apart: 4 -> 5, of which waited for: 3 -> 3; matrix products, arithmetic and copies ran while one was open for 5% -> 4% of each run, Pallas kernels for 2% -> 10%
where the time goes in v4:
time: 212 us; the launch traced here: 210 us
  blocking collectives  76.6 us (36%)
  waiting for transfers between devices  61.5 us (29%)
  Pallas kernels  32.4 us (15%)
  between operations  14.1 us (7%)
  other arithmetic  12 us (6%)
  starting transfers between devices  11.6 us (5%)
    all_gather x2, blocking collectives, spread_states(): return lax.all_gather(rounded, 'space', tiled=True)  52.9 us
    all_gather x2, waiting for transfers between devices, spread_states(): gathered = lax.all_gather(whole, 'orbit')  50.6 us
    all_to_all x1, blocking collectives, spread_states(): lax.all_to_all(packed.reshape(space, -1, LANES), 'space', 0, 0, tiled=True)  23.8 us
    all_to_all x1, waiting for transfers between devices, spread_states(): lax.all_to_all(packed.reshape(space, -1, LANES), 'space', 0, 0, tiled=True)  10.8 us
    pallas_call x1, Pallas kernels, on_device(): pl.pallas_call(forward_kernel, out_shape=(jax.ShapeDtypeStruct(flat_shape...  10.4 us
    pallas_call x1, Pallas kernels, on_device(): pl.pallas_call(state_grad_kernel, out_shape=jax.ShapeDtypeStruct((PACKED,...  9.93 us
    pallas_call x1, Pallas kernels, on_device(): pl.pallas_call(backward_kernel, out_shape=(jax.ShapeDtypeStruct(flat_shap...  8.36 us
    ppermute x1, starting transfers between devices, padded_pair(): lax.ppermute(tail, 'space', [(i, (i + 1) % count) for i in range(ends)])  5.38 us
  transfers between devices with their start and end apart: 5, of which 3 were waited for; matrix products, arithmetic and copies ran while one was open for 4% of the time, Pallas kernels for 10%

profile of v4, /device:TPU:0, one launch (start us, length us, event | category | flops | bytes accessed | tf_op | source)
XLA Modules:
  0.0 210.0 jit_solution(5143474613792637135)
XLA Ops:
  7.2 0.0 all-gather.5.cloned.1.call-start
  7.2 3.7 %shard_map.84 = f32[2304,128]{1,0:T(8,128)} custom-call(bf16[128,2240]{1,0:T(8,128)(2,1)} %bitcast.34, bf16[128,2240]{1,0:T(8,128)(2,1)} %bitcast.24), custom_call_target="tpu_custom_call" | custom-call | tf_op jit(solution)/shard_map/pallas_call | solution.py:140
  10.9 23.8 %all_to_all.10 = f32[16,144,128]{2,1,0:T(8,128)S(1)} all-to-all(f32[16,144,128]{2,1,0:T(8,128)} %bitcast.28), channel_id=1, replica_groups=mesh['orbit'=16,'space'=16] {'space'}, dimensions={0} | all-to-all | bytes 2359296 | tf_op jit(solution)/shard_map/all_to_all | solution.py:110
  34.7 0.0 copy-start
  34.7 0.0 copy-start.2
  34.7 0.7 reduce_sum.36
  35.4 0.0 all-gather.5.cloned.1.call-update
  35.4 0.4 copy-done
  35.8 0.2 copy-done.2
  36.0 0.1 fusion.4
  36.1 1.3 collective-permute-start.1
  37.4 5.4 %collective-permute-start = (bf16[2,1,1,64,2240]{4,3,2,1,0:T(8,128)(2,1)S(1)}, bf16[2,1,1,64,2240]{4,3,2,1,0:T(8,128)(2,1)}, u32[]{:S(2)}, u32[]{:S(2)}) collective-permute-start(bf16[2,1,1,64,2240]{4,3,2,1,0:T(8,128)(2,1)S(1)} %get-tuple-element.23), channel_id=1, source_target_pairs={{0,1},{1,2},{2,3},{3,4},{4,5},{5,6},{6,7},{7,8},{8,9},{9,10},{10,1... | collective-permute-start | bytes 1720328 | tf_op jit(solution)/shard_map/ppermute | solution.py:19
  42.8 30.9 %all-gather.5.cloned.1.call-done = f32[2304,128]{1,0:T(8,128)} async-done(((f32[144,128]{1,0:T(8,128)}), f32[2304,128]{1,0:T(8,128)}) %all-gather.5.cloned.1.call-update) | async-done | bytes 1179664 | tf_op jit(solution)/shard_map/all_gather | solution.py:114
  73.7 1.4 select_reduce_fusion.1
  75.1 26.4 %all_gather.18.s_ref = bf16[2304,128]{1,0:T(8,128)(2,1)} all-gather(bf16[144,128]{1,0:T(8,128)(2,1)S(1)} %divide_convert_fusion), channel_id=1, replica_groups=mesh['orbit'=16,'space'=16] {'space'}, dimensions={0}, use_global_device_ids=true | all-gather | bytes 626688 | tf_op jit(solution)/shard_map/all_gather | solution.py:124
  101.5 9.9 %shard_map.86 = f32[2304,128]{1,0:T(8,128)} custom-call(bf16[128,2240]{1,0:T(8,128)(2,1)} %bitcast.32, bf16[128,2240]{1,0:T(8,128)(2,1)} %bitcast.20, bf16[2304,128]{1,0:T(8,128)(2,1)} %all_gather.18.s_ref), custom_call_target="tpu_custom_call" | custom-call | tf_op jit(solution)/shard_map/pallas_call | solution.py:161
  111.5 0.0 copy-start.4
  111.5 0.0 copy-start.1
  111.5 4.7 %all-to-all-start.1 = ((f32[16,144,128]{2,1,0:T(8,128)}), f32[16,144,128]{2,1,0:T(8,128)}, u32[]{:S(2)}, u32[]{:S(2)}) async-start(f32[16,144,128]{2,1,0:T(8,128)} %bitcast.29), calls=%async_computation.1 | async-start | bytes 2359296 | tf_op jit(solution)/shard_map/all_to_all | solution.py:110
  116.2 0.2 all-gather.7.cloned.1.call-start
  116.4 0.0 copy-done.4
  116.4 0.2 slice_reduce_fusion.8
  116.7 0.0 collective-permute-done.1
  116.7 0.0 copy-start.3
  116.7 0.8 copy-done.3
  117.5 0.0 collective-permute-done
  117.5 0.0 copy-done.1
  117.5 2.2 %select_maximum_fusion = bf16[2,1,4,66,2240]{4,3,2,1,0:T(8,128)(2,1)S(1)} fusion(bf16[2,1,1,64,2240]{4,3,2,1,0:T(8,128)(2,1)} %copy-done.3, bf16[2,1,1,64,2240]{4,3,2,1,0:T(8,128)(2,1)} %collective-permute-done, bf16[1,1,2,64,2240]{4,3,2,1,0:T(8,128)(2,1)S(1)} %bitcast.23, bf16[1,1,2,64,2240]{4,3,2,1,0:T(8,128)(2,1)} %bitcast.25), kind=kLoop, calls=%fused_computation.3 | loop fusion | flops 17740800 | bytes 4659200 | tf_op jit(solution)/shard_map/concatenate | solution.py:17
  119.7 10.8 %all-to-all-done.1 = f32[16,144,128]{2,1,0:T(8,128)} async-done(((f32[16,144,128]{2,1,0:T(8,128)}), f32[16,144,128]{2,1,0:T(8,128)}, u32[]{:S(2)}, u32[]{:S(2)}) %all-to-all-start.1) | async-done | bytes 1179680 | tf_op jit(solution)/shard_map/all_to_all | solution.py:110
  130.5 1.3 reduce_sum.38
  131.9 0.6 broadcast_divide_fusion
  132.5 0.0 all-gather.7.cloned.1.call-update
  132.5 0.2 slice_bitcast_fusion
  132.7 2.1 multiply_add_fusion.1
  134.8 2.1 multiply_add_fusion
  136.9 10.4 %shard_map.85 = (bf16[128,2240]{1,0:T(8,128)(2,1)}, bf16[128,2240]{1,0:T(8,128)(2,1)}) custom-call(bf16[128,2240]{1,0:T(8,128)(2,1)} %bitcast.33, bf16[128,2240]{1,0:T(8,128)(2,1)} %bitcast.21, f32[128,2240]{1,0:T(8,128)} %bitcast.31, bf16[2304,128]{1,0:T(8,128)(2,1)} %all_gather.18.s_ref), custom_call_target="tpu_custom_call" | custom-call | tf_op jit(solution)/shard_map/pallas_call | solution.py:164
  147.2 19.7 %all-gather.7.cloned.1.call-done = f32[2304,128]{1,0:T(8,128)} async-done(((f32[144,128]{1,0:T(8,128)}), f32[2304,128]{1,0:T(8,128)}) %all-gather.7.cloned.1.call-update) | async-done | bytes 1179664 | tf_op jit(solution)/shard_map/all_gather | solution.py:120
  167.0 1.4 select_reduce_fusion
  168.4 26.4 %all_gather.20.s_ref = bf16[2304,128]{1,0:T(8,128)(2,1)} all-gather(bf16[144,128]{1,0:T(8,128)(2,1)S(1)} %select_reduce_fusion), channel_id=1, replica_groups=mesh['orbit'=16,'space'=16] {'space'}, dimensions={0}, use_global_device_ids=true | all-gather | bytes 626688 | tf_op jit(solution)/shard_map/all_gather | solution.py:124
  194.8 8.4 %shard_map.87 = (bf16[128,2240]{1,0:T(8,128)(2,1)}, bf16[128,2240]{1,0:T(8,128)(2,1)}) custom-call(bf16[128,2240]{1,0:T(8,128)(2,1)} %bitcast.35, bf16[128,2240]{1,0:T(8,128)(2,1)} %bitcast.26, f32[128,2240]{1,0:T(8,128)} %bitcast.30, bf16[2304,128]{1,0:T(8,128)(2,1)} %all_gather.20.s_ref), custom_call_target="tpu_custom_call" | custom-call | tf_op jit(solution)/shard_map/pallas_call | solution.py:172
  (4 shorter events, 0.0 us)
Async XLA Ops:
  7.2 66.5 %all-gather.5.cloned.1.call-start = ((), (), s32[]{:S(2)}) async-start(), calls=%async_computation.2 | async-start | bytes 1253376 | tf_op jit(solution)/shard_map/all_gather | solution.py:114
  34.7 1.1 copy-start
  34.7 1.3 copy-start.2
  36.1 80.6 %collective-permute-start.1 = (bf16[2,1,1,64,2240]{4,3,2,1,0:T(8,128)(2,1)S(1)}, bf16[2,1,1,64,2240]{4,3,2,1,0:T(8,128)(2,1)S(1)}, u32[]{:S(2)}, u32[]{:S(2)}) collective-permute-start(bf16[2,1,1,64,2240]{4,3,2,1,0:T(8,128)(2,1)S(1)} %get-tuple-element.24), channel_id=1, source_target_pairs={{1,0},{2,1},{3,2},{4,3},{5,4},{6,5},{7,6},{8,7},{9,8},{10,9},{11,1... | collective-permute-start | bytes 1720328 | tf_op jit(solution)/shard_map/ppermute | solution.py:21
  37.4 80.1 %collective-permute-start = (bf16[2,1,1,64,2240]{4,3,2,1,0:T(8,128)(2,1)S(1)}, bf16[2,1,1,64,2240]{4,3,2,1,0:T(8,128)(2,1)}, u32[]{:S(2)}, u32[]{:S(2)}) collective-permute-start(bf16[2,1,1,64,2240]{4,3,2,1,0:T(8,128)(2,1)S(1)} %get-tuple-element.23), channel_id=1, source_target_pairs={{0,1},{1,2},{2,3},{3,4},{4,5},{5,6},{6,7},{7,8},{8,9},{9,10},{10,1... | collective-permute-start | bytes 1720328 | tf_op jit(solution)/shard_map/ppermute | solution.py:19
  111.5 4.9 %copy-start.4 = (bf16[3,3,2240]{2,1,0:T(4,128)(2,1)S(1)}, bf16[3,3,2240]{2,1,0:T(4,128)(2,1)}, u32[]{:S(2)}) copy-start(bf16[3,3,2240]{2,1,0:T(4,128)(2,1)} %param.8) | copy-start | bytes 120964
  111.5 6.0 %copy-start.1 = (bf16[1,2,64,2240]{3,2,1,0:T(8,128)(2,1)S(1)}, bf16[1,2,64,2240]{3,2,1,0:T(8,128)(2,1)}, u32[]{:S(2)}) copy-start(bf16[1,2,64,2240]{3,2,1,0:T(8,128)(2,1)} %param.9) | copy-start | bytes 1720324
  111.5 19.0 %all-to-all-start.1 = ((f32[16,144,128]{2,1,0:T(8,128)}), f32[16,144,128]{2,1,0:T(8,128)}, u32[]{:S(2)}, u32[]{:S(2)}) async-start(f32[16,144,128]{2,1,0:T(8,128)} %bitcast.29), calls=%async_computation.1 | async-start | bytes 2359296 | tf_op jit(solution)/shard_map/all_to_all | solution.py:110
  116.2 50.8 %all-gather.7.cloned.1.call-start = ((), (), s32[]{:S(2)}) async-start(), calls=%async_computation.3 | async-start | bytes 1253376 | tf_op jit(solution)/shard_map/all_gather | solution.py:120
  116.7 0.8 copy-start.3
Sparse Core Ops, SparseCore 0:
  35.6 38.0 all-gather.4
  132.7 34.2 all-gather.6

commit v5 on v4

--- a/solution.py
+++ b/solution.py
@@ -108,7 +108,7 @@
     orbit = lax.axis_size("orbit")
     place = lax.axis_index("orbit")
     pieces = lax.all_to_all(packed.reshape(space, -1, LANES), "space", 0, 0, tiled=True)
-    whole = jnp.sum(pieces, axis=0)
+    whole = jnp.sum(pieces, axis=0)[:, : NORM + 1]
     views = jnp.arange(orbit)
     if not reverse:
         gathered = lax.all_gather(whole, "orbit")
@@ -120,11 +120,11 @@
         gathered = lax.all_gather(whole, "orbit")
         keep = views >= place
         summed = jnp.sum(jnp.where(keep[:, None, None], gathered, 0.0), axis=0)
-    rounded = summed.astype(jnp.bfloat16)
+    rounded = jnp.pad(summed.astype(jnp.bfloat16), ((0, 0), (0, LANES - NORM - 1)))
     return lax.all_gather(rounded, "space", tiled=True)
 
 
-def on_device(queries, keys_in, values, conv_weight, grad_out):
+def on_device_body(queries, keys_in, values, conv_weight, grad_out):
     view_count, row_count, col_count, feature_width = queries.shape
     token_count = view_count * row_count * col_count
     flat_shape = (token_count, feature_width)
@@ -161,13 +161,14 @@
     state_grad = pl.pallas_call(
         state_grad_kernel, out_shape=jax.ShapeDtypeStruct((PACKED, LANES), f32)
     )(q2, g2, state_b)
+    conv_flat = conv_term.reshape(flat_shape)
     attended, grad_query = pl.pallas_call(
         forward_kernel,
         out_shape=(
             jax.ShapeDtypeStruct(flat_shape, bf),
             jax.ShapeDtypeStruct(flat_shape, bf),
         ),
-    )(q2, g2, conv_term.reshape(flat_shape), state_b)
+    )(q2, g2, conv_flat, state_b)
     back_state = spread_states(state_grad, True, count)
     grad_key, grad_value = pl.pallas_call(
         backward_kernel,
@@ -194,7 +195,7 @@
         P("orbit", "space", None, None),
     )
     return jax.shard_map(
-        on_device,
+        on_device_body,
         mesh=mesh,
         in_specs=placed,
         out_specs=(

time: 212 us -> 173 us (0.82)
  waiting for transfers between devices: 61.5 us -> 13.7 us
  blocking collectives: 76.6 us -> 92.9 us
  between operations: 14.1 us -> 0.86 us
  starting transfers between devices: 11.6 us -> 18 us
    all_gather x2 -> x0, waiting for transfers between devices: 50.6 us -> none  [spread_states(): gathered = lax.all_gather(whole, 'orbit')]
    all_gather x0 -> x2, blocking collectives: none -> 41.6 us  [spread_states(): gathered = lax.all_gather(whole, 'orbit')]
    all_to_all x1 -> x0, blocking collectives: 23.8 us -> none  [spread_states(): lax.all_to_all(packed.reshape(space, -1, LANES), 'space', 0, 0, tiled=True)]
    all_to_all x1 -> x2, starting transfers between devices: 4.68 us -> 12.1 us  [spread_states(): lax.all_to_all(packed.reshape(space, -1, LANES), 'space', 0, 0, tiled=True)]
    all_to_all x1 -> x2, waiting for transfers between devices: 10.8 us -> 13.7 us  [spread_states(): lax.all_to_all(packed.reshape(space, -1, LANES), 'space', 0, 0, tiled=True)]
    reduce_sum x2, other arithmetic: 2.83 us -> 0.36 us  [spread_states(): summed = jnp.sum(jnp.where(keep[:, None, None], gathered, 0.0), axis=0)]
  transfers between devices with their start and end apart: 5 -> 4, of which waited for: 3 -> 1; matrix products, arithmetic and copies ran while one was open for 4% -> 5% of each run, Pallas kernels for 10% -> 8%
where the time goes in v5:
time: 173 us; the launch traced here: 172 us
  blocking collectives  92.9 us (54%)
  Pallas kernels  32.4 us (19%)
  starting transfers between devices  18 us (10%)
  waiting for transfers between devices  13.7 us (8%)
  other arithmetic  11.6 us (7%)
  local copies, waits for them, and re-layouts  2.05 us (1%)
    all_gather x2, blocking collectives, spread_states(): return lax.all_gather(rounded, 'space', tiled=True)  51.3 us
    all_gather x2, blocking collectives, spread_states(): gathered = lax.all_gather(whole, 'orbit')  41.6 us
    all_to_all x2, waiting for transfers between devices, spread_states(): lax.all_to_all(packed.reshape(space, -1, LANES), 'space', 0, 0, tiled=True)  13.7 us
    all_to_all x2, starting transfers between devices, spread_states(): lax.all_to_all(packed.reshape(space, -1, LANES), 'space', 0, 0, tiled=True)  12.1 us
    pallas_call x1, Pallas kernels, on_device_body(): pl.pallas_call(forward_kernel, out_shape=(jax.ShapeDtypeStruct(flat_shape...  10.3 us
    pallas_call x1, Pallas kernels, on_device_body(): pl.pallas_call(state_grad_kernel, out_shape=jax.ShapeDtypeStruct((PACKED,...  9.93 us
    pallas_call x1, Pallas kernels, on_device_body(): pl.pallas_call(backward_kernel, out_shape=(jax.ShapeDtypeStruct(flat_shap...  8.36 us
    ppermute x1, starting transfers between devices, padded_pair(): lax.ppermute(tail, 'space', [(i, (i + 1) % count) for i in range(ends)])  4.58 us
  transfers between devices with their start and end apart: 4, of which 1 were waited for; matrix products, arithmetic and copies ran while one was open for 5% of the time, Pallas kernels for 8%

profile of v5, /device:TPU:0, one launch (start us, length us, event | category | flops | bytes accessed | tf_op | source)
XLA Modules:
  0.0 171.5 jit_solution(10882880032136877871)
XLA Ops:
  0.6 1.3 fusion.4
  2.0 1.3 collective-permute-start.1
  3.3 4.6 %collective-permute-start = (bf16[2,1,1,64,2240]{4,3,2,1,0:T(8,128)(2,1)S(1)}, bf16[2,1,1,64,2240]{4,3,2,1,0:T(8,128)(2,1)S(1)}, u32[]{:S(2)}, u32[]{:S(2)}) collective-permute-start(bf16[2,1,1,64,2240]{4,3,2,1,0:T(8,128)(2,1)S(1)} %get-tuple-element.23), channel_id=1, source_target_pairs={{0,1},{1,2},{2,3},{3,4},{4,5},{5,6},{6,7},{7,8},{8,9},{9,10},{10,1... | collective-permute-start | bytes 1720328 | tf_op jit(solution)/shard_map/ppermute | solution.py:19
  7.9 3.8 %shard_map.84 = f32[2304,128]{1,0:T(8,128)} custom-call(bf16[128,2240]{1,0:T(8,128)(2,1)} %bitcast.37, bf16[128,2240]{1,0:T(8,128)(2,1)} %bitcast.26), custom_call_target="tpu_custom_call" | custom-call | tf_op jit(solution)/shard_map/pallas_call | solution.py:140
  11.6 0.0 copy-start
  11.6 0.0 copy-start.1
  11.6 7.4 %all-to-all-start = ((f32[16,144,128]{2,1,0:T(8,128)}), f32[16,144,128]{2,1,0:T(8,128)}, u32[]{:S(2)}, u32[]{:S(2)}) async-start(f32[16,144,128]{2,1,0:T(8,128)} %bitcast.29), calls=%async_computation | async-start | bytes 2359296 | tf_op jit(solution)/shard_map/all_to_all | solution.py:110
  19.0 1.5 convert_element_type.71
  20.5 0.5 iota_compare_fusion.3
  21.0 1.8 %slice_reduce_fusion.8 = (f32[2240]{0:T(1024)S(1)}, f32[2240]{0:T(1024)}, f32[2240]{0:T(1024)}, f32[2240]{0:T(1024)}, f32[2240]{0:T(1024)}, /*index=5*/f32[2240]...) fusion(f32[3,3,2240]{2,1,0:T(4,128)} %convert_element_type.71), kind=kLoop, calls=%fused_computation.28 | loop fusion | bytes 161280 | tf_op jit(solution)/shard_map/slice | solution.py:153
  22.8 0.0 collective-permute-done.1
  22.8 0.0 collective-permute-done
  22.8 0.0 copy-done
  22.8 0.0 copy-done.1
  22.8 1.1 select_maximum_fusion
  24.0 0.2 slice_bitcast_fusion
  24.1 0.0 copy-start.10
  24.1 13.7 %all-to-all-done = f32[16,144,128]{2,1,0:T(8,128)} async-done(((f32[16,144,128]{2,1,0:T(8,128)}), f32[16,144,128]{2,1,0:T(8,128)}, u32[]{:S(2)}, u32[]{:S(2)}) %all-to-all-start) | async-done | bytes 1179680 | tf_op jit(solution)/shard_map/all_to_all | solution.py:110
  37.8 1.3 reduce_sum.36
  39.2 23.3 %all-gather = f32[2304,113]{1,0:T(8,128)S(1)} all-gather(f32[144,113]{1,0:T(8,128)S(1)} %bitcast.39), channel_id=2, replica_groups=mesh['orbit'=16,'space'=16] {'orbit'}, dimensions={0}, use_global_device_ids=true | all-gather | bytes 1106496 | tf_op jit(solution)/shard_map/all_gather | solution.py:114
  62.5 0.0 copy-done.10
  62.5 0.2 select_reduce_fusion.1
  62.7 25.0 %all_gather.20.s_ref = bf16[2304,128]{1,0:T(8,128)(2,1)} all-gather(bf16[144,128]{1,0:T(8,128)(2,1)S(1)} %pad.12), channel_id=1, replica_groups=mesh['orbit'=16,'space'=16] {'space'}, dimensions={0}, use_global_device_ids=true | all-gather | bytes 626688 | tf_op jit(solution)/shard_map/all_gather | solution.py:124
  87.7 9.9 %shard_map.86 = f32[2304,128]{1,0:T(8,128)} custom-call(bf16[128,2240]{1,0:T(8,128)(2,1)} %bitcast.35, bf16[128,2240]{1,0:T(8,128)(2,1)} %bitcast.22, bf16[2304,128]{1,0:T(8,128)(2,1)} %all_gather.20.s_ref), custom_call_target="tpu_custom_call" | custom-call | tf_op jit(solution)/shard_map/pallas_call | solution.py:161
  97.6 0.0 copy-start.2
  97.6 0.0 copy-start.3
  97.6 0.0 copy-start.6
  97.6 0.0 copy-start.7
  97.6 0.0 copy-start.8
  97.6 0.0 copy-start.9
  97.7 4.7 %all-to-all-start.1 = ((f32[16,144,128]{2,1,0:T(8,128)}), f32[16,144,128]{2,1,0:T(8,128)}, u32[]{:S(2)}, u32[]{:S(2)}) async-start(f32[16,144,128]{2,1,0:T(8,128)} %bitcast.32), calls=%async_computation.1 | async-start | bytes 2359296 | tf_op jit(solution)/shard_map/all_to_all | solution.py:110
  102.4 0.0 copy-done.2
  102.4 0.0 copy-done.3
  102.4 0.0 copy-done.4
  102.4 0.0 copy-done.5
  102.4 0.0 copy-done.6
  102.4 0.0 copy-done.7
  102.4 0.0 copy-done.8
  102.4 0.0 copy-done.9
  102.4 2.0 %multiply_add_fusion.1 = f32[1,2,64,2240]{3,2,1,0:T(8,128)} fusion(bf16[1,4,66,2240]{3,2,1,0:T(8,128)(2,1)S(1)} %get-tuple-element.22, f32[2240]{0:T(1024)S(1)} %copy-done.2, f32[2240]{0:T(1024)S(1)} %copy-done.3, f32[2240]{0:T(1024)S(1)} %copy-done.4, f32[2240]{0:T(1024)S(1)} %copy-done.5, f32[2240]{0:T(1024)S(1)} %copy-done.6, f32[2240]{0:T(1024)S(1)} %copy-done.7, ...), kind=kLoop, calls=%fused_computation.15 | loop fusion | flops 7454720 | bytes 6388480 | tf_op jit(solution)/shard_map/add | solution.py:153
  104.5 2.1 %multiply_add_fusion = f32[1,2,64,2240]{3,2,1,0:T(8,128)} fusion(bf16[1,4,66,2240]{3,2,1,0:T(8,128)(2,1)S(1)} %get-tuple-element.21, f32[2240]{0:T(1024)S(1)} %copy-done.2, f32[2240]{0:T(1024)S(1)} %copy-done.3, f32[2240]{0:T(1024)S(1)} %copy-done.4, f32[2240]{0:T(1024)S(1)} %copy-done.5, f32[2240]{0:T(1024)S(1)} %copy-done.6, f32[2240]{0:T(1024)S(1)} %copy-done.7, ...), kind=kLoop, calls=%fused_computation.13 | loop fusion | flops 7454720 | bytes 6388480 | tf_op jit(solution)/shard_map/add | solution.py:156
  106.6 10.3 %shard_map.85 = (bf16[128,2240]{1,0:T(8,128)(2,1)}, bf16[128,2240]{1,0:T(8,128)(2,1)}) custom-call(bf16[128,2240]{1,0:T(8,128)(2,1)} %bitcast.36, bf16[128,2240]{1,0:T(8,128)(2,1)} %bitcast.23, f32[128,2240]{1,0:T(8,128)} %bitcast.34, bf16[2304,128]{1,0:T(8,128)(2,1)} %all_gather.20.s_ref), custom_call_target="tpu_custom_call" | custom-call | tf_op jit(solution)/shard_map/pallas_call | solution.py:165
  116.9 0.0 all-to-all-done.1
  116.9 1.3 reduce_sum.38
  118.3 18.3 %all-gather.1 = f32[2304,113]{1,0:T(8,128)S(1)} all-gather(f32[144,113]{1,0:T(8,128)S(1)} %slice_divide_fusion), channel_id=3, replica_groups=mesh['orbit'=16,'space'=16] {'orbit'}, dimensions={0}, use_global_device_ids=true | all-gather | bytes 1106496 | tf_op jit(solution)/shard_map/all_gather | solution.py:120
  136.6 0.2 select_reduce_fusion
  136.8 26.4 %all_gather.23.s_ref = bf16[2304,128]{1,0:T(8,128)(2,1)} all-gather(bf16[144,128]{1,0:T(8,128)(2,1)S(1)} %pad.13), channel_id=1, replica_groups=mesh['orbit'=16,'space'=16] {'space'}, dimensions={0}, use_global_device_ids=true | all-gather | bytes 626688 | tf_op jit(solution)/shard_map/all_gather | solution.py:124
  163.1 8.4 %shard_map.87 = (bf16[128,2240]{1,0:T(8,128)(2,1)}, bf16[128,2240]{1,0:T(8,128)(2,1)}) custom-call(bf16[128,2240]{1,0:T(8,128)(2,1)} %bitcast.38, bf16[128,2240]{1,0:T(8,128)(2,1)} %bitcast.27, f32[128,2240]{1,0:T(8,128)} %bitcast.33, bf16[2304,128]{1,0:T(8,128)(2,1)} %all_gather.23.s_ref), custom_call_target="tpu_custom_call" | custom-call | tf_op jit(solution)/shard_map/pallas_call | solution.py:173
  (7 shorter events, 0.1 us)
Async XLA Ops:
  2.0 20.9 %collective-permute-start.1 = (bf16[2,1,1,64,2240]{4,3,2,1,0:T(8,128)(2,1)S(1)}, bf16[2,1,1,64,2240]{4,3,2,1,0:T(8,128)(2,1)S(1)}, u32[]{:S(2)}, u32[]{:S(2)}) collective-permute-start(bf16[2,1,1,64,2240]{4,3,2,1,0:T(8,128)(2,1)S(1)} %get-tuple-element.24), channel_id=1, source_target_pairs={{1,0},{2,1},{3,2},{4,3},{5,4},{6,5},{7,6},{8,7},{9,8},{10,9},{11,1... | collective-permute-start | bytes 1720328 | tf_op jit(solution)/shard_map/ppermute | solution.py:21
  3.3 19.6 %collective-permute-start = (bf16[2,1,1,64,2240]{4,3,2,1,0:T(8,128)(2,1)S(1)}, bf16[2,1,1,64,2240]{4,3,2,1,0:T(8,128)(2,1)S(1)}, u32[]{:S(2)}, u32[]{:S(2)}) collective-permute-start(bf16[2,1,1,64,2240]{4,3,2,1,0:T(8,128)(2,1)S(1)} %get-tuple-element.23), channel_id=1, source_target_pairs={{0,1},{1,2},{2,3},{3,4},{4,5},{5,6},{6,7},{7,8},{8,9},{9,10},{10,1... | collective-permute-start | bytes 1720328 | tf_op jit(solution)/shard_map/ppermute | solution.py:19
  11.6 11.2 %copy-start = (bf16[1,2,64,2240]{3,2,1,0:T(8,128)(2,1)S(1)}, bf16[1,2,64,2240]{3,2,1,0:T(8,128)(2,1)}, u32[]{:S(2)}) copy-start(bf16[1,2,64,2240]{3,2,1,0:T(8,128)(2,1)} %param.9) | copy-start | bytes 1720324
  11.6 11.2 %copy-start.1 = (bf16[1,2,64,2240]{3,2,1,0:T(8,128)(2,1)S(1)}, bf16[1,2,64,2240]{3,2,1,0:T(8,128)(2,1)}, u32[]{:S(2)}) copy-start(bf16[1,2,64,2240]{3,2,1,0:T(8,128)(2,1)} %param.7) | copy-start | bytes 1720324
  11.6 26.2 %all-to-all-start = ((f32[16,144,128]{2,1,0:T(8,128)}), f32[16,144,128]{2,1,0:T(8,128)}, u32[]{:S(2)}, u32[]{:S(2)}) async-start(f32[16,144,128]{2,1,0:T(8,128)} %bitcast.29), calls=%async_computation | async-start | bytes 2359296 | tf_op jit(solution)/shard_map/all_to_all | solution.py:110
  24.1 38.3 %copy-start.10 = (pred[16]{0:T(512)(128)(4,1)S(1)}, pred[16]{0:T(512)(128)(4,1)}, u32[]{:S(2)}) copy-start(pred[16]{0:T(512)(128)(4,1)} %iota_compare_fusion.3) | copy-start | bytes 52
  97.6 4.8 %copy-start.2 = (f32[2240]{0:T(1024)S(1)}, f32[2240]{0:T(1024)}, u32[]{:S(2)}) copy-start(f32[2240]{0:T(1024)} %get-tuple-element.13) | copy-start | bytes 26884
  97.6 4.8 %copy-start.3 = (f32[2240]{0:T(1024)S(1)}, f32[2240]{0:T(1024)}, u32[]{:S(2)}) copy-start(f32[2240]{0:T(1024)} %get-tuple-element.14) | copy-start | bytes 26884
  97.6 4.8 %copy-start.4 = (f32[2240]{0:T(1024)S(1)}, f32[2240]{0:T(1024)}, u32[]{:S(2)}) copy-start(f32[2240]{0:T(1024)} %get-tuple-element.15) | copy-start | bytes 26884
  97.6 4.8 %copy-start.5 = (f32[2240]{0:T(1024)S(1)}, f32[2240]{0:T(1024)}, u32[]{:S(2)}) copy-start(f32[2240]{0:T(1024)} %get-tuple-element.16) | copy-start | bytes 26884
  97.6 4.8 %copy-start.6 = (f32[2240]{0:T(1024)S(1)}, f32[2240]{0:T(1024)}, u32[]{:S(2)}) copy-start(f32[2240]{0:T(1024)} %get-tuple-element.17) | copy-start | bytes 26884
  97.6 4.8 %copy-start.7 = (f32[2240]{0:T(1024)S(1)}, f32[2240]{0:T(1024)}, u32[]{:S(2)}) copy-start(f32[2240]{0:T(1024)} %get-tuple-element.18) | copy-start | bytes 26884
  97.6 4.8 %copy-start.8 = (f32[2240]{0:T(1024)S(1)}, f32[2240]{0:T(1024)}, u32[]{:S(2)}) copy-start(f32[2240]{0:T(1024)} %get-tuple-element.19) | copy-start | bytes 26884
  97.6 4.8 %copy-start.9 = (f32[2240]{0:T(1024)S(1)}, f32[2240]{0:T(1024)}, u32[]{:S(2)}) copy-start(f32[2240]{0:T(1024)} %get-tuple-element.20) | copy-start | bytes 26884
  97.7 19.3 %all-to-all-start.1 = ((f32[16,144,128]{2,1,0:T(8,128)}), f32[16,144,128]{2,1,0:T(8,128)}, u32[]{:S(2)}, u32[]{:S(2)}) async-start(f32[16,144,128]{2,1,0:T(8,128)} %bitcast.32), calls=%async_computation.1 | async-start | bytes 2359296 | tf_op jit(solution)/shard_map/all_to_all | solution.py:110

commit v6 on v5

--- a/solution.py
+++ b/solution.py
@@ -14,14 +14,9 @@
     rows = cells.shape[2]
     head = cells[:, :, :width]
     tail = cells[:, :, rows - width :]
-    return jnp.concatenate(
-        [
-            lax.ppermute(tail, "space", [(i, (i + 1) % count) for i in range(ends)]),
-            cells,
-            lax.ppermute(head, "space", [((i + 1) % count, i) for i in range(ends)]),
-        ],
-        axis=2,
-    )
+    above = lax.ppermute(tail, "space", [(i, (i + 1) % count) for i in range(ends)])
+    below = lax.ppermute(head, "space", [((i + 1) % count, i) for i in range(ends)])
+    return jnp.concatenate([above, cells, below], axis=2)
 
 
 ROWS = HEADS * HD

time: 173 us -> 173 us (level)
  no operation moved by 1% of the time
where the time goes in v6:
time: 173 us; the launch traced here: 172 us
  blocking collectives  92.9 us (54%)
  Pallas kernels  32.4 us (19%)
  starting transfers between devices  18 us (10%)
  waiting for transfers between devices  13.7 us (8%)
  other arithmetic  11.6 us (7%)
  local copies, waits for them, and re-layouts  2.05 us (1%)
    all_gather x2, blocking collectives, spread_states(): return lax.all_gather(rounded, 'space', tiled=True)  51.3 us
    all_gather x2, blocking collectives, spread_states(): gathered = lax.all_gather(whole, 'orbit')  41.6 us
    all_to_all x2, waiting for transfers between devices, spread_states(): lax.all_to_all(packed.reshape(space, -1, LANES), 'space', 0, 0, tiled=True)  13.7 us
    all_to_all x2, starting transfers between devices, spread_states(): lax.all_to_all(packed.reshape(space, -1, LANES), 'space', 0, 0, tiled=True)  12.1 us
    pallas_call x1, Pallas kernels, on_device_body(): pl.pallas_call(forward_kernel, out_shape=(jax.ShapeDtypeStruct(flat_shape...  10.3 us
    pallas_call x1, Pallas kernels, on_device_body(): pl.pallas_call(state_grad_kernel, out_shape=jax.ShapeDtypeStruct((PACKED,...  9.93 us
    pallas_call x1, Pallas kernels, on_device_body(): pl.pallas_call(backward_kernel, out_shape=(jax.ShapeDtypeStruct(flat_shap...  8.36 us
    ppermute x1, starting transfers between devices, padded_pair(): lax.ppermute(tail, 'space', [(i, (i + 1) % count) for i in range(ends)])  4.58 us
  transfers between devices with their start and end apart: 4, of which 1 were waited for; matrix products, arithmetic and copies ran while one was open for 5% of the time, Pallas kernels for 8%

profile of v6, /device:TPU:0, one launch (start us, length us, event | category | flops | bytes accessed | tf_op | source)
XLA Modules:
  0.0 171.5 jit_solution(10882880032136877871)
XLA Ops:
  0.6 1.3 fusion.4
  2.0 1.3 collective-permute-start.1
  3.3 4.6 %collective-permute-start = (bf16[2,1,1,64,2240]{4,3,2,1,0:T(8,128)(2,1)S(1)}, bf16[2,1,1,64,2240]{4,3,2,1,0:T(8,128)(2,1)S(1)}, u32[]{:S(2)}, u32[]{:S(2)}) collective-permute-start(bf16[2,1,1,64,2240]{4,3,2,1,0:T(8,128)(2,1)S(1)} %get-tuple-element.23), channel_id=1, source_target_pairs={{0,1},{1,2},{2,3},{3,4},{4,5},{5,6},{6,7},{7,8},{8,9},{9,10},{10,1... | collective-permute-start | bytes 1720328 | tf_op jit(solution)/shard_map/ppermute | solution.py:17
  7.9 3.8 %shard_map.84 = f32[2304,128]{1,0:T(8,128)} custom-call(bf16[128,2240]{1,0:T(8,128)(2,1)} %bitcast.37, bf16[128,2240]{1,0:T(8,128)(2,1)} %bitcast.26), custom_call_target="tpu_custom_call" | custom-call | tf_op jit(solution)/shard_map/pallas_call | solution.py:135
  11.6 0.0 copy-start
  11.6 0.0 copy-start.1
  11.6 7.4 %all-to-all-start = ((f32[16,144,128]{2,1,0:T(8,128)}), f32[16,144,128]{2,1,0:T(8,128)}, u32[]{:S(2)}, u32[]{:S(2)}) async-start(f32[16,144,128]{2,1,0:T(8,128)} %bitcast.29), calls=%async_computation | async-start | bytes 2359296 | tf_op jit(solution)/shard_map/all_to_all | solution.py:105
  19.0 1.5 convert_element_type.71
  20.5 0.5 iota_compare_fusion.3
  21.0 1.8 %slice_reduce_fusion.8 = (f32[2240]{0:T(1024)S(1)}, f32[2240]{0:T(1024)}, f32[2240]{0:T(1024)}, f32[2240]{0:T(1024)}, f32[2240]{0:T(1024)}, /*index=5*/f32[2240]...) fusion(f32[3,3,2240]{2,1,0:T(4,128)} %convert_element_type.71), kind=kLoop, calls=%fused_computation.28 | loop fusion | bytes 161280 | tf_op jit(solution)/shard_map/slice | solution.py:148
  22.8 0.0 collective-permute-done.1
  22.8 0.0 collective-permute-done
  22.8 0.0 copy-done
  22.8 0.0 copy-done.1
  22.8 1.1 select_maximum_fusion
  24.0 0.2 slice_bitcast_fusion
  24.1 0.0 copy-start.10
  24.1 13.7 %all-to-all-done = f32[16,144,128]{2,1,0:T(8,128)} async-done(((f32[16,144,128]{2,1,0:T(8,128)}), f32[16,144,128]{2,1,0:T(8,128)}, u32[]{:S(2)}, u32[]{:S(2)}) %all-to-all-start) | async-done | bytes 1179680 | tf_op jit(solution)/shard_map/all_to_all | solution.py:105
  37.8 1.3 reduce_sum.36
  39.2 23.3 %all-gather = f32[2304,113]{1,0:T(8,128)S(1)} all-gather(f32[144,113]{1,0:T(8,128)S(1)} %bitcast.39), channel_id=2, replica_groups=mesh['orbit'=16,'space'=16] {'orbit'}, dimensions={0}, use_global_device_ids=true | all-gather | bytes 1106496 | tf_op jit(solution)/shard_map/all_gather | solution.py:109
  62.5 0.0 copy-done.10
  62.5 0.2 select_reduce_fusion.1
  62.7 25.0 %all_gather.20.s_ref = bf16[2304,128]{1,0:T(8,128)(2,1)} all-gather(bf16[144,128]{1,0:T(8,128)(2,1)S(1)} %pad.12), channel_id=1, replica_groups=mesh['orbit'=16,'space'=16] {'space'}, dimensions={0}, use_global_device_ids=true | all-gather | bytes 626688 | tf_op jit(solution)/shard_map/all_gather | solution.py:119
  87.7 9.9 %shard_map.86 = f32[2304,128]{1,0:T(8,128)} custom-call(bf16[128,2240]{1,0:T(8,128)(2,1)} %bitcast.35, bf16[128,2240]{1,0:T(8,128)(2,1)} %bitcast.22, bf16[2304,128]{1,0:T(8,128)(2,1)} %all_gather.20.s_ref), custom_call_target="tpu_custom_call" | custom-call | tf_op jit(solution)/shard_map/pallas_call | solution.py:156
  97.6 0.0 copy-start.2
  97.6 0.0 copy-start.3
  97.6 0.0 copy-start.6
  97.6 0.0 copy-start.7
  97.6 0.0 copy-start.8
  97.6 0.0 copy-start.9
  97.7 4.7 %all-to-all-start.1 = ((f32[16,144,128]{2,1,0:T(8,128)}), f32[16,144,128]{2,1,0:T(8,128)}, u32[]{:S(2)}, u32[]{:S(2)}) async-start(f32[16,144,128]{2,1,0:T(8,128)} %bitcast.32), calls=%async_computation.1 | async-start | bytes 2359296 | tf_op jit(solution)/shard_map/all_to_all | solution.py:105
  102.4 0.0 copy-done.2
  102.4 0.0 copy-done.3
  102.4 0.0 copy-done.4
  102.4 0.0 copy-done.5
  102.4 0.0 copy-done.6
  102.4 0.0 copy-done.7
  102.4 0.0 copy-done.8
  102.4 0.0 copy-done.9
  102.4 2.0 %multiply_add_fusion.1 = f32[1,2,64,2240]{3,2,1,0:T(8,128)} fusion(bf16[1,4,66,2240]{3,2,1,0:T(8,128)(2,1)S(1)} %get-tuple-element.22, f32[2240]{0:T(1024)S(1)} %copy-done.2, f32[2240]{0:T(1024)S(1)} %copy-done.3, f32[2240]{0:T(1024)S(1)} %copy-done.4, f32[2240]{0:T(1024)S(1)} %copy-done.5, f32[2240]{0:T(1024)S(1)} %copy-done.6, f32[2240]{0:T(1024)S(1)} %copy-done.7, ...), kind=kLoop, calls=%fused_computation.15 | loop fusion | flops 7454720 | bytes 6388480 | tf_op jit(solution)/shard_map/add | solution.py:148
  104.5 2.1 %multiply_add_fusion = f32[1,2,64,2240]{3,2,1,0:T(8,128)} fusion(bf16[1,4,66,2240]{3,2,1,0:T(8,128)(2,1)S(1)} %get-tuple-element.21, f32[2240]{0:T(1024)S(1)} %copy-done.2, f32[2240]{0:T(1024)S(1)} %copy-done.3, f32[2240]{0:T(1024)S(1)} %copy-done.4, f32[2240]{0:T(1024)S(1)} %copy-done.5, f32[2240]{0:T(1024)S(1)} %copy-done.6, f32[2240]{0:T(1024)S(1)} %copy-done.7, ...), kind=kLoop, calls=%fused_computation.13 | loop fusion | flops 7454720 | bytes 6388480 | tf_op jit(solution)/shard_map/add | solution.py:151
  106.6 10.3 %shard_map.85 = (bf16[128,2240]{1,0:T(8,128)(2,1)}, bf16[128,2240]{1,0:T(8,128)(2,1)}) custom-call(bf16[128,2240]{1,0:T(8,128)(2,1)} %bitcast.36, bf16[128,2240]{1,0:T(8,128)(2,1)} %bitcast.23, f32[128,2240]{1,0:T(8,128)} %bitcast.34, bf16[2304,128]{1,0:T(8,128)(2,1)} %all_gather.20.s_ref), custom_call_target="tpu_custom_call" | custom-call | tf_op jit(solution)/shard_map/pallas_call | solution.py:160
  116.9 0.0 all-to-all-done.1
  116.9 1.3 reduce_sum.38
  118.3 18.3 %all-gather.1 = f32[2304,113]{1,0:T(8,128)S(1)} all-gather(f32[144,113]{1,0:T(8,128)S(1)} %slice_divide_fusion), channel_id=3, replica_groups=mesh['orbit'=16,'space'=16] {'orbit'}, dimensions={0}, use_global_device_ids=true | all-gather | bytes 1106496 | tf_op jit(solution)/shard_map/all_gather | solution.py:115
  136.6 0.2 select_reduce_fusion
  136.8 26.4 %all_gather.23.s_ref = bf16[2304,128]{1,0:T(8,128)(2,1)} all-gather(bf16[144,128]{1,0:T(8,128)(2,1)S(1)} %pad.13), channel_id=1, replica_groups=mesh['orbit'=16,'space'=16] {'space'}, dimensions={0}, use_global_device_ids=true | all-gather | bytes 626688 | tf_op jit(solution)/shard_map/all_gather | solution.py:119
  163.1 8.4 %shard_map.87 = (bf16[128,2240]{1,0:T(8,128)(2,1)}, bf16[128,2240]{1,0:T(8,128)(2,1)}) custom-call(bf16[128,2240]{1,0:T(8,128)(2,1)} %bitcast.38, bf16[128,2240]{1,0:T(8,128)(2,1)} %bitcast.27, f32[128,2240]{1,0:T(8,128)} %bitcast.33, bf16[2304,128]{1,0:T(8,128)(2,1)} %all_gather.23.s_ref), custom_call_target="tpu_custom_call" | custom-call | tf_op jit(solution)/shard_map/pallas_call | solution.py:168
  (7 shorter events, 0.1 us)
Async XLA Ops:
  2.0 20.9 %collective-permute-start.1 = (bf16[2,1,1,64,2240]{4,3,2,1,0:T(8,128)(2,1)S(1)}, bf16[2,1,1,64,2240]{4,3,2,1,0:T(8,128)(2,1)S(1)}, u32[]{:S(2)}, u32[]{:S(2)}) collective-permute-start(bf16[2,1,1,64,2240]{4,3,2,1,0:T(8,128)(2,1)S(1)} %get-tuple-element.24), channel_id=1, source_target_pairs={{1,0},{2,1},{3,2},{4,3},{5,4},{6,5},{7,6},{8,7},{9,8},{10,9},{11,1... | collective-permute-start | bytes 1720328 | tf_op jit(solution)/shard_map/ppermute | solution.py:18
  3.3 19.6 %collective-permute-start = (bf16[2,1,1,64,2240]{4,3,2,1,0:T(8,128)(2,1)S(1)}, bf16[2,1,1,64,2240]{4,3,2,1,0:T(8,128)(2,1)S(1)}, u32[]{:S(2)}, u32[]{:S(2)}) collective-permute-start(bf16[2,1,1,64,2240]{4,3,2,1,0:T(8,128)(2,1)S(1)} %get-tuple-element.23), channel_id=1, source_target_pairs={{0,1},{1,2},{2,3},{3,4},{4,5},{5,6},{6,7},{7,8},{8,9},{9,10},{10,1... | collective-permute-start | bytes 1720328 | tf_op jit(solution)/shard_map/ppermute | solution.py:17
  11.6 11.2 %copy-start = (bf16[1,2,64,2240]{3,2,1,0:T(8,128)(2,1)S(1)}, bf16[1,2,64,2240]{3,2,1,0:T(8,128)(2,1)}, u32[]{:S(2)}) copy-start(bf16[1,2,64,2240]{3,2,1,0:T(8,128)(2,1)} %param.9) | copy-start | bytes 1720324
  11.6 11.2 %copy-start.1 = (bf16[1,2,64,2240]{3,2,1,0:T(8,128)(2,1)S(1)}, bf16[1,2,64,2240]{3,2,1,0:T(8,128)(2,1)}, u32[]{:S(2)}) copy-start(bf16[1,2,64,2240]{3,2,1,0:T(8,128)(2,1)} %param.7) | copy-start | bytes 1720324
  11.6 26.2 %all-to-all-start = ((f32[16,144,128]{2,1,0:T(8,128)}), f32[16,144,128]{2,1,0:T(8,128)}, u32[]{:S(2)}, u32[]{:S(2)}) async-start(f32[16,144,128]{2,1,0:T(8,128)} %bitcast.29), calls=%async_computation | async-start | bytes 2359296 | tf_op jit(solution)/shard_map/all_to_all | solution.py:105
  24.1 38.3 %copy-start.10 = (pred[16]{0:T(512)(128)(4,1)S(1)}, pred[16]{0:T(512)(128)(4,1)}, u32[]{:S(2)}) copy-start(pred[16]{0:T(512)(128)(4,1)} %iota_compare_fusion.3) | copy-start | bytes 52
  97.6 4.8 %copy-start.2 = (f32[2240]{0:T(1024)S(1)}, f32[2240]{0:T(1024)}, u32[]{:S(2)}) copy-start(f32[2240]{0:T(1024)} %get-tuple-element.13) | copy-start | bytes 26884
  97.6 4.8 %copy-start.3 = (f32[2240]{0:T(1024)S(1)}, f32[2240]{0:T(1024)}, u32[]{:S(2)}) copy-start(f32[2240]{0:T(1024)} %get-tuple-element.14) | copy-start | bytes 26884
  97.6 4.8 %copy-start.4 = (f32[2240]{0:T(1024)S(1)}, f32[2240]{0:T(1024)}, u32[]{:S(2)}) copy-start(f32[2240]{0:T(1024)} %get-tuple-element.15) | copy-start | bytes 26884
  97.6 4.8 %copy-start.5 = (f32[2240]{0:T(1024)S(1)}, f32[2240]{0:T(1024)}, u32[]{:S(2)}) copy-start(f32[2240]{0:T(1024)} %get-tuple-element.16) | copy-start | bytes 26884
  97.6 4.8 %copy-start.6 = (f32[2240]{0:T(1024)S(1)}, f32[2240]{0:T(1024)}, u32[]{:S(2)}) copy-start(f32[2240]{0:T(1024)} %get-tuple-element.17) | copy-start | bytes 26884
  97.6 4.8 %copy-start.7 = (f32[2240]{0:T(1024)S(1)}, f32[2240]{0:T(1024)}, u32[]{:S(2)}) copy-start(f32[2240]{0:T(1024)} %get-tuple-element.18) | copy-start | bytes 26884
  97.6 4.8 %copy-start.8 = (f32[2240]{0:T(1024)S(1)}, f32[2240]{0:T(1024)}, u32[]{:S(2)}) copy-start(f32[2240]{0:T(1024)} %get-tuple-element.19) | copy-start | bytes 26884
  97.6 4.8 %copy-start.9 = (f32[2240]{0:T(1024)S(1)}, f32[2240]{0:T(1024)}, u32[]{:S(2)}) copy-start(f32[2240]{0:T(1024)} %get-tuple-element.20) | copy-start | bytes 26884
  97.7 19.3 %all-to-all-start.1 = ((f32[16,144,128]{2,1,0:T(8,128)}), f32[16,144,128]{2,1,0:T(8,128)}, u32[]{:S(2)}, u32[]{:S(2)}) async-start(f32[16,144,128]{2,1,0:T(8,128)} %bitcast.32), calls=%async_computation.1 | async-start | bytes 2359296 | tf_op jit(solution)/shard_map/all_to_all | solution.py:105

commit v7 on v6

--- a/solution.py
+++ b/solution.py
@@ -58,15 +58,36 @@
     return qf, numerator, inverse, grads
 
 
-def state_grad_kernel(q_ref, g_ref, s_ref, sg_ref):
+def tile_kernel(q_ref, g_ref, k_ref, v_ref, qt_ref, qx_ref, gt_ref, kt_ref, vt_ref):
+    tokens = q_ref.shape[0]
+    zero = jnp.zeros((tokens, LANES - HD), jnp.bfloat16)
+    extra = lane_one(tokens)
+    for h in range(HEADS):
+        cols = slice(h * HD, (h + 1) * HD)
+        qf = jnp.concatenate([jnp.maximum(q_ref[:, cols], 0), zero], axis=1)
+        qt_ref[h] = qf
+        qx_ref[h] = qf.T
+        gt_ref[h] = jnp.concatenate([g_ref[:, cols], zero], axis=1)
+        kt_ref[h] = jnp.concatenate([jnp.maximum(k_ref[:, cols], 0), zero], axis=1)
+        vt_ref[h] = jnp.concatenate([v_ref[:, cols], extra], axis=1)
+
+
+def state_grad_kernel(qt_ref, qx_ref, gt_ref, s_ref, sg_ref):
     sg_ref[ROWS:, :] = jnp.zeros((PACKED - ROWS, LANES), jnp.float32)
-    for h in range(HEADS):
-        cols = slice(h * HD, (h + 1) * HD)
-        state = s_ref[h * HD : (h + 1) * HD, :]
-        qf, _, _, grads = head_terms(q_ref[:, cols], g_ref[:, cols], state)
-        sg_ref[h * HD : (h + 1) * HD, :] = lax.dot_general(
-            qf, grads, (((0,), (0,)), ((), ())), preferred_element_type=jnp.float32
-        )
+    lanes = lax.broadcasted_iota(jnp.int32, (qt_ref.shape[1], LANES), 1)
+    for h in range(HEADS):
+        state = s_ref[h * HD : h * HD + LANES, :]
+        wide = jnp.dot(qt_ref[h], state, preferred_element_type=jnp.float32)
+        denominator = wide[:, NORM : NORM + 1] + 1.0
+        inverse = 1.0 / denominator
+        gw = gt_ref[h].astype(jnp.float32)
+        num_grad = (gw * inverse).astype(jnp.bfloat16)
+        den_grad = (
+            -jnp.sum(gw * wide, axis=1, keepdims=True) / (denominator * denominator)
+        ).astype(jnp.bfloat16)
+        grads = jnp.where(lanes == NORM, den_grad, num_grad)
+        sg = jnp.dot(qx_ref[h], grads, preferred_element_type=jnp.float32)
+        sg_ref[h * HD : (h + 1) * HD, :] = sg[:HD]
 
 
 def forward_kernel(q_ref, g_ref, c_ref, s_ref, a_ref, gq_ref):
@@ -82,18 +103,16 @@
         gq_ref[:, cols] = jnp.where(qh > 0, query_grad, 0.0).astype(jnp.bfloat16)
 
 
-def backward_kernel(k_ref, v_ref, c_ref, s_ref, gk_ref, gv_ref):
-    extra = lane_one(k_ref.shape[0])
-    for h in range(HEADS):
-        cols = slice(h * HD, (h + 1) * HD)
-        kh = k_ref[:, cols]
-        kf = jnp.maximum(kh, 0)
-        v_ext = jnp.concatenate([v_ref[:, cols], extra], axis=1)
-        state = s_ref[h * HD : (h + 1) * HD, :]
+def backward_kernel(kt_ref, vt_ref, c_ref, s_ref, gk_ref, gv_ref):
+    for h in range(HEADS):
+        cols = slice(h * HD, (h + 1) * HD)
+        kf = kt_ref[h]
         key_grad = lax.dot_general(
-            v_ext, state, (((1,), (1,)), ((), ())), preferred_element_type=jnp.float32
+            vt_ref[h], s_ref[h * HD : (h + 1) * HD, :], (((1,), (1,)), ((), ())),
+            preferred_element_type=jnp.float32,
         )
-        gk_ref[:, cols] = jnp.where(kh > 0, key_grad, 0.0).astype(jnp.bfloat16)
+        gk_ref[:, cols] = jnp.where(kf[:, :HD] > 0, key_grad, 0.0).astype(jnp.bfloat16)
+        state = s_ref[h * HD : h * HD + LANES, :]
         value_grad = jnp.dot(kf, state, preferred_element_type=jnp.float32)[:, :HD]
         gv_ref[:, cols] = (value_grad + c_ref[:, cols]).astype(jnp.bfloat16)
 
@@ -135,6 +154,10 @@
     packed_part = pl.pallas_call(
         part_kernel, out_shape=jax.ShapeDtypeStruct((PACKED, LANES), f32)
     )(k2, v2)
+    tile = jax.ShapeDtypeStruct((HEADS, token_count, LANES), jnp.bfloat16)
+    q_tiles, q_cross, g_tiles, k_tiles, v_tiles = pl.pallas_call(
+        tile_kernel, out_shape=(tile,) * 5
+    )(q2, g2, k2, v2)
     state_b = spread_states(packed_part, False, count)
 
     pair = padded_pair(jnp.stack([values, grad_out]), 1)
@@ -155,7 +178,7 @@
     bf = jnp.bfloat16
     state_grad = pl.pallas_call(
         state_grad_kernel, out_shape=jax.ShapeDtypeStruct((PACKED, LANES), f32)
-    )(q2, g2, state_b)
+    )(q_tiles, q_cross, g_tiles, state_b)
     conv_flat = conv_term.reshape(flat_shape)
     attended, grad_query = pl.pallas_call(
         forward_kernel,
@@ -171,7 +194,7 @@
             jax.ShapeDtypeStruct(flat_shape, bf),
             jax.ShapeDtypeStruct(flat_shape, bf),
         ),
-    )(k2, v2, conv_grad.reshape(flat_shape), back_state)
+    )(k_tiles, v_tiles, conv_grad.reshape(flat_shape), back_state)
     shape = queries.shape
     return (
         attended.reshape(shape),

time: 173 us -> 163 us (0.942)
  waiting for transfers between devices: 13.7 us -> 9.11 us
  Pallas kernels: 32.4 us -> 27.9 us
  starting transfers between devices: 18 us -> 16.1 us
    pallas_call x1, Pallas kernels: 9.93 us -> 3.93 us  [on_device_body(): pl.pallas_call(state_grad_kernel, out_shape=jax.ShapeDtypeStruct((PACKED,...]
    pallas_call x0 -> x1, Pallas kernels: none -> 5.1 us  [on_device_body(): pl.pallas_call(tile_kernel, out_shape=(tile,) * 5)(q2, g2, k2, v2)]
    all_to_all x2, waiting for transfers between devices: 13.7 us -> 9.11 us  [spread_states(): lax.all_to_all(packed.reshape(space, -1, LANES), 'space', 0, 0, tiled=True)]
    pallas_call x1, Pallas kernels: 8.36 us -> 4.74 us  [on_device_body(): pl.pallas_call(backward_kernel, out_shape=(jax.ShapeDtypeStruct(flat_shap...]
    ppermute x1, starting transfers between devices: 4.58 us -> 1.81 us  [padded_pair(): lax.ppermute(tail, 'space', [(i, (i + 1) % count) for i in range(ends)])]
  transfers between devices with their start and end apart: 4 -> 4, of which waited for: 1 -> 1; matrix products, arithmetic and copies ran while one was open for 5% -> 5% of each run, Pallas kernels for 8% -> 12%
where the time goes in v7:
time: 163 us; the launch traced here: 161 us
  blocking collectives  94 us (58%)
  Pallas kernels  27.9 us (17%)
  starting transfers between devices  16.1 us (10%)
  other arithmetic  10.9 us (7%)
  waiting for transfers between devices  9.11 us (6%)
  local copies, waits for them, and re-layouts  2.07 us (1%)
    all_gather x2, blocking collectives, spread_states(): return lax.all_gather(rounded, 'space', tiled=True)  52.4 us
    all_gather x2, blocking collectives, spread_states(): gathered = lax.all_gather(whole, 'orbit')  41.6 us
    all_to_all x2, starting transfers between devices, spread_states(): lax.all_to_all(packed.reshape(space, -1, LANES), 'space', 0, 0, tiled=True)  13 us
    pallas_call x1, Pallas kernels, on_device_body(): pl.pallas_call(forward_kernel, out_shape=(jax.ShapeDtypeStruct(flat_shape...  10.4 us
    all_to_all x2, waiting for transfers between devices, spread_states(): lax.all_to_all(packed.reshape(space, -1, LANES), 'space', 0, 0, tiled=True)  9.11 us
    pallas_call x1, Pallas kernels, on_device_body(): pl.pallas_call(tile_kernel, out_shape=(tile,) * 5)(q2, g2, k2, v2)  5.1 us
    pallas_call x1, Pallas kernels, on_device_body(): pl.pallas_call(backward_kernel, out_shape=(jax.ShapeDtypeStruct(flat_shap...  4.74 us
    pallas_call x1, Pallas kernels, on_device_body(): pl.pallas_call(state_grad_kernel, out_shape=jax.ShapeDtypeStruct((PACKED,...  3.93 us
  transfers between devices with their start and end apart: 4, of which 1 were waited for; matrix products, arithmetic and copies ran while one was open for 5% of the time, Pallas kernels for 12%

profile of v7, /device:TPU:0, one launch (start us, length us, event | category | flops | bytes accessed | tf_op | source)
XLA Modules:
  0.0 160.9 jit_solution(12366270926441673186)
XLA Ops:
  0.6 1.3 fusion.4
  2.0 1.8 %collective-permute-start = (bf16[2,1,1,64,2240]{4,3,2,1,0:T(8,128)(2,1)S(1)}, bf16[2,1,1,64,2240]{4,3,2,1,0:T(8,128)(2,1)S(1)}, u32[]{:S(2)}, u32[]{:S(2)}) collective-permute-start(bf16[2,1,1,64,2240]{4,3,2,1,0:T(8,128)(2,1)S(1)} %get-tuple-element.33), channel_id=1, source_target_pairs={{0,1},{1,2},{2,3},{3,4},{4,5},{5,6},{6,7},{7,8},{8,9},{9,10},{10,1... | collective-permute-start | bytes 1720328 | tf_op jit(solution)/shard_map/ppermute | solution.py:17
  3.8 1.3 collective-permute-start.1
  5.1 3.8 %shard_map.84 = f32[2304,128]{1,0:T(8,128)} custom-call(bf16[128,2240]{1,0:T(8,128)(2,1)} %bitcast.35, bf16[128,2240]{1,0:T(8,128)(2,1)} %bitcast.22), custom_call_target="tpu_custom_call" | custom-call | tf_op jit(solution)/shard_map/pallas_call | solution.py:154
  8.9 0.0 copy-start.10
  8.9 8.2 %all-to-all-start = ((f32[16,144,128]{2,1,0:T(8,128)}), f32[16,144,128]{2,1,0:T(8,128)}, u32[]{:S(2)}, u32[]{:S(2)}) async-start(f32[16,144,128]{2,1,0:T(8,128)} %bitcast.30), calls=%async_computation | async-start | bytes 2359296 | tf_op jit(solution)/shard_map/all_to_all | solution.py:124
  17.1 0.0 copy-done.10
  17.1 0.7 convert_element_type.71
  17.8 0.0 copy-start
  17.8 5.1 %shard_map.86 = (bf16[20,128,128]{2,1,0:T(8,128)(2,1)}, bf16[20,128,128]{2,1,0:T(8,128)(2,1)}, bf16[20,128,128]{2,1,0:T(8,128)(2,1)}, bf16[20,128,128]{2,1,0:T(8,128)(2,1)}, bf16[20,128,128]{2,1,0:T(8,128)(2,1)}) custom-call(bf16[128,2240]{1,0:T(8,128)(2,1)} %bitcast.37, bf16[128,2240]{1,0:T(8,128)(2,1)} %bitcast.26, bf16[128,2240]{1,0:T(8,128)(2,1)} %bitcast.36, ...), custom_call_target="tpu_custom_call" | custom-call | tf_op jit(solution)/shard_map/pallas_call | solution.py:158
  22.9 0.6 iota_compare_fusion.3
  23.5 1.8 %slice_reduce_fusion.8 = (f32[2240]{0:T(1024)S(1)}, f32[2240]{0:T(1024)}, f32[2240]{0:T(1024)}, f32[2240]{0:T(1024)}, f32[2240]{0:T(1024)}, /*index=5*/f32[2240]...) fusion(f32[3,3,2240]{2,1,0:T(4,128)} %convert_element_type.71), kind=kLoop, calls=%fused_computation.28 | loop fusion | bytes 161280 | tf_op jit(solution)/shard_map/slice | solution.py:171
  25.3 0.0 collective-permute-done
  25.3 0.0 collective-permute-done.1
  25.3 0.0 copy-done
  25.3 0.0 copy-done.1
  25.3 1.1 select_maximum_fusion
  26.4 0.2 slice_bitcast_fusion
  26.6 0.0 copy-start.11
  26.6 9.1 %all-to-all-done = f32[16,144,128]{2,1,0:T(8,128)} async-done(((f32[16,144,128]{2,1,0:T(8,128)}), f32[16,144,128]{2,1,0:T(8,128)}, u32[]{:S(2)}, u32[]{:S(2)}) %all-to-all-start) | async-done | bytes 1179680 | tf_op jit(solution)/shard_map/all_to_all | solution.py:124
  35.7 1.3 reduce_sum.36
  37.1 23.3 %all-gather = f32[2304,113]{1,0:T(8,128)S(1)} all-gather(f32[144,113]{1,0:T(8,128)S(1)} %bitcast.39), channel_id=2, replica_groups=mesh['orbit'=16,'space'=16] {'orbit'}, dimensions={0}, use_global_device_ids=true | all-gather | bytes 1106496 | tf_op jit(solution)/shard_map/all_gather | solution.py:128
  60.4 0.0 copy-done.11
  60.4 0.2 select_reduce_fusion.1
  60.6 25.8 %all_gather.20.s_ref = bf16[2304,128]{1,0:T(8,128)(2,1)} all-gather(bf16[144,128]{1,0:T(8,128)(2,1)S(1)} %pad.12), channel_id=1, replica_groups=mesh['orbit'=16,'space'=16] {'space'}, dimensions={0}, use_global_device_ids=true | all-gather | bytes 626688 | tf_op jit(solution)/shard_map/all_gather | solution.py:138
  86.4 3.9 %shard_map.87 = f32[2304,128]{1,0:T(8,128)} custom-call(bf16[20,128,128]{2,1,0:T(8,128)(2,1)} %get-tuple-element.17.qt_ref, bf16[20,128,128]{2,1,0:T(8,128)(2,1)} %get-tuple-element.18.qx_ref, bf16[20,128,128]{2,1,0:T(8,128)(2,1)} %get-tuple-element.19.gt_ref, bf16[2304,128]{1,0:T(8,128)(2,1)} %all_gather.20.s_ref), custom_call_target="tpu_custom_call" | custom-call | tf_op jit(solution)/shard_map/pallas_call | solution.py:179
  90.4 0.0 copy-start.6
  90.4 0.0 copy-start.7
  90.4 0.0 copy-start.8
  90.4 0.0 copy-start.9
  90.4 4.8 %all-to-all-start.1 = ((f32[16,144,128]{2,1,0:T(8,128)}), f32[16,144,128]{2,1,0:T(8,128)}, u32[]{:S(2)}, u32[]{:S(2)}) async-start(f32[16,144,128]{2,1,0:T(8,128)} %bitcast.29), calls=%async_computation.1 | async-start | bytes 2359296 | tf_op jit(solution)/shard_map/all_to_all | solution.py:124
  95.2 0.0 copy-done.2
  95.2 0.0 copy-done.3
  95.2 0.0 copy-done.4
  95.2 0.0 copy-done.5
  95.2 0.0 copy-done.6
  95.2 0.0 copy-done.7
  95.2 0.0 copy-done.8
  95.2 0.0 copy-done.9
  95.2 2.1 %multiply_add_fusion = f32[1,2,64,2240]{3,2,1,0:T(8,128)} fusion(bf16[1,4,66,2240]{3,2,1,0:T(8,128)(2,1)S(1)} %get-tuple-element.31, f32[2240]{0:T(1024)S(1)} %copy-done.2, f32[2240]{0:T(1024)S(1)} %copy-done.3, f32[2240]{0:T(1024)S(1)} %copy-done.4, f32[2240]{0:T(1024)S(1)} %copy-done.5, f32[2240]{0:T(1024)S(1)} %copy-done.6, f32[2240]{0:T(1024)S(1)} %copy-done.7, ...), kind=kLoop, calls=%fused_computation.13 | loop fusion | flops 7454720 | bytes 6388480 | tf_op jit(solution)/shard_map/add | solution.py:174
  97.3 2.0 %multiply_add_fusion.1 = f32[1,2,64,2240]{3,2,1,0:T(8,128)} fusion(bf16[1,4,66,2240]{3,2,1,0:T(8,128)(2,1)S(1)} %get-tuple-element.32, f32[2240]{0:T(1024)S(1)} %copy-done.2, f32[2240]{0:T(1024)S(1)} %copy-done.3, f32[2240]{0:T(1024)S(1)} %copy-done.4, f32[2240]{0:T(1024)S(1)} %copy-done.5, f32[2240]{0:T(1024)S(1)} %copy-done.6, f32[2240]{0:T(1024)S(1)} %copy-done.7, ...), kind=kLoop, calls=%fused_computation.15 | loop fusion | flops 7454720 | bytes 6388480 | tf_op jit(solution)/shard_map/add | solution.py:171
  99.4 10.4 %shard_map.85 = (bf16[128,2240]{1,0:T(8,128)(2,1)}, bf16[128,2240]{1,0:T(8,128)(2,1)}) custom-call(bf16[128,2240]{1,0:T(8,128)(2,1)} %bitcast.38, bf16[128,2240]{1,0:T(8,128)(2,1)} %bitcast.27, f32[128,2240]{1,0:T(8,128)} %bitcast.34, bf16[2304,128]{1,0:T(8,128)(2,1)} %all_gather.20.s_ref), custom_call_target="tpu_custom_call" | custom-call | tf_op jit(solution)/shard_map/pallas_call | solution.py:183
  109.7 0.0 all-to-all-done.1
  109.7 1.3 reduce_sum.38
  111.1 18.3 %all-gather.1 = f32[2304,113]{1,0:T(8,128)S(1)} all-gather(f32[144,113]{1,0:T(8,128)S(1)} %slice_divide_fusion), channel_id=3, replica_groups=mesh['orbit'=16,'space'=16] {'orbit'}, dimensions={0}, use_global_device_ids=true | all-gather | bytes 1106496 | tf_op jit(solution)/shard_map/all_gather | solution.py:134
  129.4 0.2 select_reduce_fusion
  129.6 26.6 %all_gather.23.s_ref = bf16[2304,128]{1,0:T(8,128)(2,1)} all-gather(bf16[144,128]{1,0:T(8,128)(2,1)S(1)} %pad.13), channel_id=1, replica_groups=mesh['orbit'=16,'space'=16] {'space'}, dimensions={0}, use_global_device_ids=true | all-gather | bytes 626688 | tf_op jit(solution)/shard_map/all_gather | solution.py:138
  156.2 4.7 %shard_map.88 = (bf16[128,2240]{1,0:T(8,128)(2,1)}, bf16[128,2240]{1,0:T(8,128)(2,1)}) custom-call(bf16[20,128,128]{2,1,0:T(8,128)(2,1)} %get-tuple-element.15.kt_ref, bf16[20,128,128]{2,1,0:T(8,128)(2,1)} %get-tuple-element.16.vt_ref, f32[128,2240]{1,0:T(8,128)} %bitcast.31, bf16[2304,128]{1,0:T(8,128)(2,1)} %all_gather.23.s_ref), custom_call_target="tpu_custom_call" | custom-call | tf_op jit(solution)/shard_map/pallas_call | solution.py:191
  (10 shorter events, 0.1 us)
Async XLA Ops:
  2.0 23.3 %collective-permute-start = (bf16[2,1,1,64,2240]{4,3,2,1,0:T(8,128)(2,1)S(1)}, bf16[2,1,1,64,2240]{4,3,2,1,0:T(8,128)(2,1)S(1)}, u32[]{:S(2)}, u32[]{:S(2)}) collective-permute-start(bf16[2,1,1,64,2240]{4,3,2,1,0:T(8,128)(2,1)S(1)} %get-tuple-element.33), channel_id=1, source_target_pairs={{0,1},{1,2},{2,3},{3,4},{4,5},{5,6},{6,7},{7,8},{8,9},{9,10},{10,1... | collective-permute-start | bytes 1720328 | tf_op jit(solution)/shard_map/ppermute | solution.py:17
  3.8 21.5 %collective-permute-start.1 = (bf16[2,1,1,64,2240]{4,3,2,1,0:T(8,128)(2,1)S(1)}, bf16[2,1,1,64,2240]{4,3,2,1,0:T(8,128)(2,1)S(1)}, u32[]{:S(2)}, u32[]{:S(2)}) collective-permute-start(bf16[2,1,1,64,2240]{4,3,2,1,0:T(8,128)(2,1)S(1)} %get-tuple-element.34), channel_id=1, source_target_pairs={{1,0},{2,1},{3,2},{4,3},{5,4},{6,5},{7,6},{8,7},{9,8},{10,9},{11,1... | collective-permute-start | bytes 1720328 | tf_op jit(solution)/shard_map/ppermute | solution.py:18
  8.9 8.3 %copy-start.10 = (bf16[3,3,2240]{2,1,0:T(4,128)(2,1)S(1)}, bf16[3,3,2240]{2,1,0:T(4,128)(2,1)}, u32[]{:S(2)}) copy-start(bf16[3,3,2240]{2,1,0:T(4,128)(2,1)} %param.8) | copy-start | bytes 120964
  8.9 26.9 %all-to-all-start = ((f32[16,144,128]{2,1,0:T(8,128)}), f32[16,144,128]{2,1,0:T(8,128)}, u32[]{:S(2)}, u32[]{:S(2)}) async-start(f32[16,144,128]{2,1,0:T(8,128)} %bitcast.30), calls=%async_computation | async-start | bytes 2359296 | tf_op jit(solution)/shard_map/all_to_all | solution.py:124
  17.8 7.5 %copy-start = (bf16[1,2,64,2240]{3,2,1,0:T(8,128)(2,1)S(1)}, bf16[1,2,64,2240]{3,2,1,0:T(8,128)(2,1)}, u32[]{:S(2)}) copy-start(bf16[1,2,64,2240]{3,2,1,0:T(8,128)(2,1)} %param.7) | copy-start | bytes 1720324
  17.8 7.5 %copy-start.1 = (bf16[1,2,64,2240]{3,2,1,0:T(8,128)(2,1)S(1)}, bf16[1,2,64,2240]{3,2,1,0:T(8,128)(2,1)}, u32[]{:S(2)}) copy-start(bf16[1,2,64,2240]{3,2,1,0:T(8,128)(2,1)} %param.9) | copy-start | bytes 1720324
  26.6 33.8 %copy-start.11 = (pred[16]{0:T(512)(128)(4,1)S(1)}, pred[16]{0:T(512)(128)(4,1)}, u32[]{:S(2)}) copy-start(pred[16]{0:T(512)(128)(4,1)} %iota_compare_fusion.3) | copy-start | bytes 52
  90.3 4.8 %copy-start.2 = (f32[2240]{0:T(1024)S(1)}, f32[2240]{0:T(1024)}, u32[]{:S(2)}) copy-start(f32[2240]{0:T(1024)} %get-tuple-element.23) | copy-start | bytes 26884
  90.3 4.8 %copy-start.3 = (f32[2240]{0:T(1024)S(1)}, f32[2240]{0:T(1024)}, u32[]{:S(2)}) copy-start(f32[2240]{0:T(1024)} %get-tuple-element.24) | copy-start | bytes 26884
  90.3 4.8 %copy-start.4 = (f32[2240]{0:T(1024)S(1)}, f32[2240]{0:T(1024)}, u32[]{:S(2)}) copy-start(f32[2240]{0:T(1024)} %get-tuple-element.25) | copy-start | bytes 26884
  90.4 4.8 %copy-start.5 = (f32[2240]{0:T(1024)S(1)}, f32[2240]{0:T(1024)}, u32[]{:S(2)}) copy-start(f32[2240]{0:T(1024)} %get-tuple-element.26) | copy-start | bytes 26884
  90.4 4.8 %copy-start.6 = (f32[2240]{0:T(1024)S(1)}, f32[2240]{0:T(1024)}, u32[]{:S(2)}) copy-start(f32[2240]{0:T(1024)} %get-tuple-element.27) | copy-start | bytes 26884
  90.4 4.8 %copy-start.7 = (f32[2240]{0:T(1024)S(1)}, f32[2240]{0:T(1024)}, u32[]{:S(2)}) copy-start(f32[2240]{0:T(1024)} %get-tuple-element.28) | copy-start | bytes 26884
  90.4 4.8 %copy-start.8 = (f32[2240]{0:T(1024)S(1)}, f32[2240]{0:T(1024)}, u32[]{:S(2)}) copy-start(f32[2240]{0:T(1024)} %get-tuple-element.29) | copy-start | bytes 26884
  90.4 4.8 %copy-start.9 = (f32[2240]{0:T(1024)S(1)}, f32[2240]{0:T(1024)}, u32[]{:S(2)}) copy-start(f32[2240]{0:T(1024)} %get-tuple-element.30) | copy-start | bytes 26884
  90.4 19.3 %all-to-all-start.1 = ((f32[16,144,128]{2,1,0:T(8,128)}), f32[16,144,128]{2,1,0:T(8,128)}, u32[]{:S(2)}, u32[]{:S(2)}) async-start(f32[16,144,128]{2,1,0:T(8,128)} %bitcast.29), calls=%async_computation.1 | async-start | bytes 2359296 | tf_op jit(solution)/shard_map/all_to_all | solution.py:124

commit v8 on v7

--- a/solution.py
+++ b/solution.py
@@ -40,22 +40,6 @@
         s_ref[h * HD : (h + 1) * HD, :] = lax.dot_general(
             kf, v_ext, (((0,), (0,)), ((), ())), preferred_element_type=jnp.float32
         )
-
-
-def head_terms(qh, gh, state):
-    qf = jnp.maximum(qh, 0)
-    wide = jnp.dot(qf, state, preferred_element_type=jnp.float32)
-    numerator = wide[:, :HD]
-    denominator = wide[:, NORM : NORM + 1] + 1.0
-    inverse = 1.0 / denominator
-    gw = gh.astype(jnp.float32)
-    num_grad = (gw * inverse).astype(jnp.bfloat16)
-    den_grad = (
-        -jnp.sum(gw * numerator, axis=1, keepdims=True) / (denominator * denominator)
-    ).astype(jnp.bfloat16)
-    pad = jnp.zeros((qh.shape[0], LANES - HD - 1), jnp.bfloat16)
-    grads = jnp.concatenate([num_grad, den_grad, pad], axis=1)
-    return qf, numerator, inverse, grads
 
 
 def tile_kernel(q_ref, g_ref, k_ref, v_ref, qt_ref, qx_ref, gt_ref, kt_ref, vt_ref):
@@ -90,17 +74,26 @@
         sg_ref[h * HD : (h + 1) * HD, :] = sg[:HD]
 
 
-def forward_kernel(q_ref, g_ref, c_ref, s_ref, a_ref, gq_ref):
-    for h in range(HEADS):
-        cols = slice(h * HD, (h + 1) * HD)
-        qh = q_ref[:, cols]
-        state = s_ref[h * HD : (h + 1) * HD, :]
-        _, numerator, inverse, grads = head_terms(qh, g_ref[:, cols], state)
-        a_ref[:, cols] = (numerator * inverse + c_ref[:, cols]).astype(jnp.bfloat16)
+def forward_kernel(qt_ref, gt_ref, c_ref, s_ref, a_ref, gq_ref):
+    lanes = lax.broadcasted_iota(jnp.int32, (qt_ref.shape[1], LANES), 1)
+    for h in range(HEADS):
+        cols = slice(h * HD, (h + 1) * HD)
+        qf = qt_ref[h]
+        wide = jnp.dot(qf, s_ref[h * HD : h * HD + LANES, :], preferred_element_type=jnp.float32)
+        denominator = wide[:, NORM : NORM + 1] + 1.0
+        inverse = 1.0 / denominator
+        a_ref[:, cols] = (wide[:, :HD] * inverse + c_ref[:, cols]).astype(jnp.bfloat16)
+        gw = gt_ref[h].astype(jnp.float32)
+        num_grad = (gw * inverse).astype(jnp.bfloat16)
+        den_grad = (
+            -jnp.sum(gw * wide, axis=1, keepdims=True) / (denominator * denominator)
+        ).astype(jnp.bfloat16)
+        grads = jnp.where(lanes == NORM, den_grad, num_grad)
         query_grad = lax.dot_general(
-            grads, state, (((1,), (1,)), ((), ())), preferred_element_type=jnp.float32
+            grads, s_ref[h * HD : (h + 1) * HD, :], (((1,), (1,)), ((), ())),
+            preferred_element_type=jnp.float32,
         )
-        gq_ref[:, cols] = jnp.where(qh > 0, query_grad, 0.0).astype(jnp.bfloat16)
+        gq_ref[:, cols] = jnp.where(qf[:, :HD] > 0, query_grad, 0.0).astype(jnp.bfloat16)
 
 
 def backward_kernel(kt_ref, vt_ref, c_ref, s_ref, gk_ref, gv_ref):
@@ -186,7 +179,7 @@
             jax.ShapeDtypeStruct(flat_shape, bf),
             jax.ShapeDtypeStruct(flat_shape, bf),
         ),
-    )(q2, g2, conv_flat, state_b)
+    )(q_tiles, g_tiles, conv_flat, state_b)
     back_state = spread_states(state_grad, True, count)
     grad_key, grad_value = pl.pallas_call(
         backward_kernel,

time: 163 us -> 161 us (0.988)
  blocking collectives: 94 us -> 92.3 us
  Pallas kernels: 27.9 us -> 26.2 us
  waiting for transfers between devices: 9.11 us -> 10.8 us
    all_to_all x2, waiting for transfers between devices: 9.11 us -> 10.8 us  [spread_states(): lax.all_to_all(packed.reshape(space, -1, LANES), 'space', 0, 0, tiled=True)]
    all_gather x2, blocking collectives: 52.4 us -> 50.7 us  [spread_states(): return lax.all_gather(rounded, 'space', tiled=True)]
    pallas_call x1, Pallas kernels: 10.4 us -> 8.71 us  [on_device_body(): pl.pallas_call(forward_kernel, out_shape=(jax.ShapeDtypeStruct(flat_shape...]
  transfers between devices with their start and end apart: 4 -> 4, of which waited for: 1 -> 2; matrix products, arithmetic and copies ran while one was open for 5% -> 5% of each run, Pallas kernels for 12% -> 11%
where the time goes in v8:
time: 161 us; the launch traced here: 159 us
  blocking collectives  92.3 us (57%)
  Pallas kernels  26.2 us (16%)
  starting transfers between devices  16.1 us (10%)
  other arithmetic  10.9 us (7%)
  waiting for transfers between devices  10.8 us (7%)
  local copies, waits for them, and re-layouts  2.07 us (1%)
    all_gather x2, blocking collectives, spread_states(): return lax.all_gather(rounded, 'space', tiled=True)  50.7 us
    all_gather x2, blocking collectives, spread_states(): gathered = lax.all_gather(whole, 'orbit')  41.6 us
    all_to_all x2, starting transfers between devices, spread_states(): lax.all_to_all(packed.reshape(space, -1, LANES), 'space', 0, 0, tiled=True)  13 us
    all_to_all x2, waiting for transfers between devices, spread_states(): lax.all_to_all(packed.reshape(space, -1, LANES), 'space', 0, 0, tiled=True)  10.8 us
    pallas_call x1, Pallas kernels, on_device_body(): pl.pallas_call(forward_kernel, out_shape=(jax.ShapeDtypeStruct(flat_shape...  8.71 us
    pallas_call x1, Pallas kernels, on_device_body(): pl.pallas_call(tile_kernel, out_shape=(tile,) * 5)(q2, g2, k2, v2)  5.04 us
    pallas_call x1, Pallas kernels, on_device_body(): pl.pallas_call(backward_kernel, out_shape=(jax.ShapeDtypeStruct(flat_shap...  4.75 us
    pallas_call x1, Pallas kernels, on_device_body(): pl.pallas_call(state_grad_kernel, out_shape=jax.ShapeDtypeStruct((PACKED,...  3.93 us
  transfers between devices with their start and end apart: 4, of which 2 were waited for; matrix products, arithmetic and copies ran while one was open for 5% of the time, Pallas kernels for 11%

profile of v8, /device:TPU:0, one launch (start us, length us, event | category | flops | bytes accessed | tf_op | source)
XLA Modules:
  0.0 159.3 jit_solution(12870894062851152942)
XLA Ops:
  0.6 1.3 fusion.4
  2.0 1.8 %collective-permute-start = (bf16[2,1,1,64,2240]{4,3,2,1,0:T(8,128)(2,1)S(1)}, bf16[2,1,1,64,2240]{4,3,2,1,0:T(8,128)(2,1)S(1)}, u32[]{:S(2)}, u32[]{:S(2)}) collective-permute-start(bf16[2,1,1,64,2240]{4,3,2,1,0:T(8,128)(2,1)S(1)} %get-tuple-element.33), channel_id=1, source_target_pairs={{0,1},{1,2},{2,3},{3,4},{4,5},{5,6},{6,7},{7,8},{8,9},{9,10},{10,1... | collective-permute-start | bytes 1720328 | tf_op jit(solution)/shard_map/ppermute | solution.py:17
  3.8 1.3 collective-permute-start.1
  5.1 3.8 %shard_map.85 = f32[2304,128]{1,0:T(8,128)} custom-call(bf16[128,2240]{1,0:T(8,128)(2,1)} %bitcast.34, bf16[128,2240]{1,0:T(8,128)(2,1)} %bitcast.22), custom_call_target="tpu_custom_call" | custom-call | tf_op jit(solution)/shard_map/pallas_call | solution.py:147
  8.9 0.0 copy-start.10
  8.9 8.2 %all-to-all-start = ((f32[16,144,128]{2,1,0:T(8,128)}), f32[16,144,128]{2,1,0:T(8,128)}, u32[]{:S(2)}, u32[]{:S(2)}) async-start(f32[16,144,128]{2,1,0:T(8,128)} %bitcast.29), calls=%async_computation | async-start | bytes 2359296 | tf_op jit(solution)/shard_map/all_to_all | solution.py:117
  17.1 0.0 copy-done.10
  17.1 0.7 convert_element_type.71
  17.8 0.0 copy-start
  17.8 5.0 %shard_map.84 = (bf16[20,128,128]{2,1,0:T(8,128)(2,1)}, bf16[20,128,128]{2,1,0:T(8,128)(2,1)}, bf16[20,128,128]{2,1,0:T(8,128)(2,1)}, bf16[20,128,128]{2,1,0:T(8,128)(2,1)}, bf16[20,128,128]{2,1,0:T(8,128)(2,1)}) custom-call(bf16[128,2240]{1,0:T(8,128)(2,1)} %bitcast.36, bf16[128,2240]{1,0:T(8,128)(2,1)} %bitcast.26, bf16[128,2240]{1,0:T(8,128)(2,1)} %bitcast.35, ...), custom_call_target="tpu_custom_call" | custom-call | tf_op jit(solution)/shard_map/pallas_call | solution.py:151
  22.8 0.6 iota_compare_fusion.3
  23.4 1.8 %slice_reduce_fusion.8 = (f32[2240]{0:T(1024)S(1)}, f32[2240]{0:T(1024)}, f32[2240]{0:T(1024)}, f32[2240]{0:T(1024)}, f32[2240]{0:T(1024)}, /*index=5*/f32[2240]...) fusion(f32[3,3,2240]{2,1,0:T(4,128)} %convert_element_type.71), kind=kLoop, calls=%fused_computation.28 | loop fusion | bytes 161280 | tf_op jit(solution)/shard_map/slice | solution.py:164
  25.2 0.0 collective-permute-done
  25.2 0.0 collective-permute-done.1
  25.2 0.0 copy-done
  25.3 0.0 copy-done.1
  25.3 1.1 select_maximum_fusion
  26.4 0.2 slice_bitcast_fusion
  26.5 0.0 copy-start.11
  26.6 9.2 %all-to-all-done = f32[16,144,128]{2,1,0:T(8,128)} async-done(((f32[16,144,128]{2,1,0:T(8,128)}), f32[16,144,128]{2,1,0:T(8,128)}, u32[]{:S(2)}, u32[]{:S(2)}) %all-to-all-start) | async-done | bytes 1179680 | tf_op jit(solution)/shard_map/all_to_all | solution.py:117
  35.7 1.3 reduce_sum.36
  37.1 23.3 %all-gather = f32[2304,113]{1,0:T(8,128)S(1)} all-gather(f32[144,113]{1,0:T(8,128)S(1)} %bitcast.37), channel_id=2, replica_groups=mesh['orbit'=16,'space'=16] {'orbit'}, dimensions={0}, use_global_device_ids=true | all-gather | bytes 1106496 | tf_op jit(solution)/shard_map/all_gather | solution.py:121
  60.4 0.0 copy-done.11
  60.4 0.2 select_reduce_fusion.1
  60.6 25.8 %all_gather.20.s_ref = bf16[2304,128]{1,0:T(8,128)(2,1)} all-gather(bf16[144,128]{1,0:T(8,128)(2,1)S(1)} %pad.12), channel_id=1, replica_groups=mesh['orbit'=16,'space'=16] {'space'}, dimensions={0}, use_global_device_ids=true | all-gather | bytes 626688 | tf_op jit(solution)/shard_map/all_gather | solution.py:131
  86.4 3.9 %shard_map.87 = f32[2304,128]{1,0:T(8,128)} custom-call(bf16[20,128,128]{2,1,0:T(8,128)(2,1)} %get-tuple-element.13.qt_ref, bf16[20,128,128]{2,1,0:T(8,128)(2,1)} %get-tuple-element.19.qx_ref, bf16[20,128,128]{2,1,0:T(8,128)(2,1)} %get-tuple-element.14.gt_ref, bf16[2304,128]{1,0:T(8,128)(2,1)} %all_gather.20.s_ref), custom_call_target="tpu_custom_call" | custom-call | tf_op jit(solution)/shard_map/pallas_call | solution.py:172
  90.4 0.0 copy-start.6
  90.4 0.0 copy-start.7
  90.4 0.0 copy-start.8
  90.4 0.0 copy-start.9
  90.4 4.8 %all-to-all-start.1 = ((f32[16,144,128]{2,1,0:T(8,128)}), f32[16,144,128]{2,1,0:T(8,128)}, u32[]{:S(2)}, u32[]{:S(2)}) async-start(f32[16,144,128]{2,1,0:T(8,128)} %bitcast.28), calls=%async_computation.1 | async-start | bytes 2359296 | tf_op jit(solution)/shard_map/all_to_all | solution.py:117
  95.2 0.0 copy-done.2
  95.2 0.0 copy-done.3
  95.2 0.0 copy-done.4
  95.2 0.0 copy-done.5
  95.2 0.0 copy-done.6
  95.2 0.0 copy-done.7
  95.2 0.0 copy-done.8
  95.2 0.0 copy-done.9
  95.2 2.1 %multiply_add_fusion = f32[1,2,64,2240]{3,2,1,0:T(8,128)} fusion(bf16[1,4,66,2240]{3,2,1,0:T(8,128)(2,1)S(1)} %get-tuple-element.31, f32[2240]{0:T(1024)S(1)} %copy-done.2, f32[2240]{0:T(1024)S(1)} %copy-done.3, f32[2240]{0:T(1024)S(1)} %copy-done.4, f32[2240]{0:T(1024)S(1)} %copy-done.5, f32[2240]{0:T(1024)S(1)} %copy-done.6, f32[2240]{0:T(1024)S(1)} %copy-done.7, ...), kind=kLoop, calls=%fused_computation.13 | loop fusion | flops 7454720 | bytes 6388480 | tf_op jit(solution)/shard_map/add | solution.py:167
  97.3 2.0 %multiply_add_fusion.1 = f32[1,2,64,2240]{3,2,1,0:T(8,128)} fusion(bf16[1,4,66,2240]{3,2,1,0:T(8,128)(2,1)S(1)} %get-tuple-element.32, f32[2240]{0:T(1024)S(1)} %copy-done.2, f32[2240]{0:T(1024)S(1)} %copy-done.3, f32[2240]{0:T(1024)S(1)} %copy-done.4, f32[2240]{0:T(1024)S(1)} %copy-done.5, f32[2240]{0:T(1024)S(1)} %copy-done.6, f32[2240]{0:T(1024)S(1)} %copy-done.7, ...), kind=kLoop, calls=%fused_computation.15 | loop fusion | flops 7454720 | bytes 6388480 | tf_op jit(solution)/shard_map/add | solution.py:164
  99.4 8.7 %shard_map.86 = (bf16[128,2240]{1,0:T(8,128)(2,1)}, bf16[128,2240]{1,0:T(8,128)(2,1)}) custom-call(bf16[20,128,128]{2,1,0:T(8,128)(2,1)} %get-tuple-element.13.qt_ref, bf16[20,128,128]{2,1,0:T(8,128)(2,1)} %get-tuple-element.14.gt_ref, f32[128,2240]{1,0:T(8,128)} %bitcast.31, bf16[2304,128]{1,0:T(8,128)(2,1)} %all_gather.20.s_ref), custom_call_target="tpu_custom_call" | custom-call | tf_op jit(solution)/shard_map/pallas_call | solution.py:176
  108.1 1.6 %all-to-all-done.1 = f32[16,144,128]{2,1,0:T(8,128)} async-done(((f32[16,144,128]{2,1,0:T(8,128)}), f32[16,144,128]{2,1,0:T(8,128)}, u32[]{:S(2)}, u32[]{:S(2)}) %all-to-all-start.1) | async-done | bytes 1179680 | tf_op jit(solution)/shard_map/all_to_all | solution.py:117
  109.7 1.3 reduce_sum.38
  111.1 18.3 %all-gather.1 = f32[2304,113]{1,0:T(8,128)S(1)} all-gather(f32[144,113]{1,0:T(8,128)S(1)} %slice_divide_fusion), channel_id=3, replica_groups=mesh['orbit'=16,'space'=16] {'orbit'}, dimensions={0}, use_global_device_ids=true | all-gather | bytes 1106496 | tf_op jit(solution)/shard_map/all_gather | solution.py:127
  129.4 0.2 select_reduce_fusion
  129.6 24.9 %all_gather.23.s_ref = bf16[2304,128]{1,0:T(8,128)(2,1)} all-gather(bf16[144,128]{1,0:T(8,128)(2,1)S(1)} %pad.13), channel_id=1, replica_groups=mesh['orbit'=16,'space'=16] {'space'}, dimensions={0}, use_global_device_ids=true | all-gather | bytes 626688 | tf_op jit(solution)/shard_map/all_gather | solution.py:131
  154.5 4.7 %shard_map.88 = (bf16[128,2240]{1,0:T(8,128)(2,1)}, bf16[128,2240]{1,0:T(8,128)(2,1)}) custom-call(bf16[20,128,128]{2,1,0:T(8,128)(2,1)} %get-tuple-element.17.kt_ref, bf16[20,128,128]{2,1,0:T(8,128)(2,1)} %get-tuple-element.18.vt_ref, f32[128,2240]{1,0:T(8,128)} %bitcast.30, bf16[2304,128]{1,0:T(8,128)(2,1)} %all_gather.23.s_ref), custom_call_target="tpu_custom_call" | custom-call | tf_op jit(solution)/shard_map/pallas_call | solution.py:184
  (10 shorter events, 0.1 us)
Async XLA Ops:
  2.0 23.3 %collective-permute-start = (bf16[2,1,1,64,2240]{4,3,2,1,0:T(8,128)(2,1)S(1)}, bf16[2,1,1,64,2240]{4,3,2,1,0:T(8,128)(2,1)S(1)}, u32[]{:S(2)}, u32[]{:S(2)}) collective-permute-start(bf16[2,1,1,64,2240]{4,3,2,1,0:T(8,128)(2,1)S(1)} %get-tuple-element.33), channel_id=1, source_target_pairs={{0,1},{1,2},{2,3},{3,4},{4,5},{5,6},{6,7},{7,8},{8,9},{9,10},{10,1... | collective-permute-start | bytes 1720328 | tf_op jit(solution)/shard_map/ppermute | solution.py:17
  3.8 21.5 %collective-permute-start.1 = (bf16[2,1,1,64,2240]{4,3,2,1,0:T(8,128)(2,1)S(1)}, bf16[2,1,1,64,2240]{4,3,2,1,0:T(8,128)(2,1)S(1)}, u32[]{:S(2)}, u32[]{:S(2)}) collective-permute-start(bf16[2,1,1,64,2240]{4,3,2,1,0:T(8,128)(2,1)S(1)} %get-tuple-element.34), channel_id=1, source_target_pairs={{1,0},{2,1},{3,2},{4,3},{5,4},{6,5},{7,6},{8,7},{9,8},{10,9},{11,1... | collective-permute-start | bytes 1720328 | tf_op jit(solution)/shard_map/ppermute | solution.py:18
  8.9 8.3 %copy-start.10 = (bf16[3,3,2240]{2,1,0:T(4,128)(2,1)S(1)}, bf16[3,3,2240]{2,1,0:T(4,128)(2,1)}, u32[]{:S(2)}) copy-start(bf16[3,3,2240]{2,1,0:T(4,128)(2,1)} %param.8) | copy-start | bytes 120964
  8.9 26.9 %all-to-all-start = ((f32[16,144,128]{2,1,0:T(8,128)}), f32[16,144,128]{2,1,0:T(8,128)}, u32[]{:S(2)}, u32[]{:S(2)}) async-start(f32[16,144,128]{2,1,0:T(8,128)} %bitcast.29), calls=%async_computation | async-start | bytes 2359296 | tf_op jit(solution)/shard_map/all_to_all | solution.py:117
  17.8 7.5 %copy-start = (bf16[1,2,64,2240]{3,2,1,0:T(8,128)(2,1)S(1)}, bf16[1,2,64,2240]{3,2,1,0:T(8,128)(2,1)}, u32[]{:S(2)}) copy-start(bf16[1,2,64,2240]{3,2,1,0:T(8,128)(2,1)} %param.7) | copy-start | bytes 1720324
  17.8 7.5 %copy-start.1 = (bf16[1,2,64,2240]{3,2,1,0:T(8,128)(2,1)S(1)}, bf16[1,2,64,2240]{3,2,1,0:T(8,128)(2,1)}, u32[]{:S(2)}) copy-start(bf16[1,2,64,2240]{3,2,1,0:T(8,128)(2,1)} %param.9) | copy-start | bytes 1720324
  26.5 33.8 %copy-start.11 = (pred[16]{0:T(512)(128)(4,1)S(1)}, pred[16]{0:T(512)(128)(4,1)}, u32[]{:S(2)}) copy-start(pred[16]{0:T(512)(128)(4,1)} %iota_compare_fusion.3) | copy-start | bytes 52
  90.3 4.8 %copy-start.2 = (f32[2240]{0:T(1024)S(1)}, f32[2240]{0:T(1024)}, u32[]{:S(2)}) copy-start(f32[2240]{0:T(1024)} %get-tuple-element.23) | copy-start | bytes 26884
  90.3 4.8 %copy-start.3 = (f32[2240]{0:T(1024)S(1)}, f32[2240]{0:T(1024)}, u32[]{:S(2)}) copy-start(f32[2240]{0:T(1024)} %get-tuple-element.24) | copy-start | bytes 26884
  90.3 4.8 %copy-start.4 = (f32[2240]{0:T(1024)S(1)}, f32[2240]{0:T(1024)}, u32[]{:S(2)}) copy-start(f32[2240]{0:T(1024)} %get-tuple-element.25) | copy-start | bytes 26884
  90.4 4.8 %copy-start.5 = (f32[2240]{0:T(1024)S(1)}, f32[2240]{0:T(1024)}, u32[]{:S(2)}) copy-start(f32[2240]{0:T(1024)} %get-tuple-element.26) | copy-start | bytes 26884
  90.4 4.8 %copy-start.6 = (f32[2240]{0:T(1024)S(1)}, f32[2240]{0:T(1024)}, u32[]{:S(2)}) copy-start(f32[2240]{0:T(1024)} %get-tuple-element.27) | copy-start | bytes 26884
  90.4 4.8 %copy-start.7 = (f32[2240]{0:T(1024)S(1)}, f32[2240]{0:T(1024)}, u32[]{:S(2)}) copy-start(f32[2240]{0:T(1024)} %get-tuple-element.28) | copy-start | bytes 26884
  90.4 4.8 %copy-start.8 = (f32[2240]{0:T(1024)S(1)}, f32[2240]{0:T(1024)}, u32[]{:S(2)}) copy-start(f32[2240]{0:T(1024)} %get-tuple-element.29) | copy-start | bytes 26884
  90.4 4.8 %copy-start.9 = (f32[2240]{0:T(1024)S(1)}, f32[2240]{0:T(1024)}, u32[]{:S(2)}) copy-start(f32[2240]{0:T(1024)} %get-tuple-element.30) | copy-start | bytes 26884
  90.4 19.3 %all-to-all-start.1 = ((f32[16,144,128]{2,1,0:T(8,128)}), f32[16,144,128]{2,1,0:T(8,128)}, u32[]{:S(2)}, u32[]{:S(2)}) async-start(f32[16,144,128]{2,1,0:T(8,128)} %bitcast.28), calls=%async_computation.1 | async-start | bytes 2359296 | tf_op jit(solution)/shard_map/all_to_all | solution.py:117

commit v9 on v8

--- a/solution.py
+++ b/solution.py
@@ -114,8 +114,10 @@
     space = lax.axis_size("space")
     orbit = lax.axis_size("orbit")
     place = lax.axis_index("orbit")
-    pieces = lax.all_to_all(packed.reshape(space, -1, LANES), "space", 0, 0, tiled=True)
-    whole = jnp.sum(pieces, axis=0)[:, : NORM + 1]
+    pieces = lax.all_to_all(
+        packed.astype(jnp.bfloat16).reshape(space, -1, LANES), "space", 0, 0, tiled=True
+    )
+    whole = jnp.sum(pieces.astype(jnp.float32), axis=0)[:, : NORM + 1]
     views = jnp.arange(orbit)
     if not reverse:
         gathered = lax.all_gather(whole, "orbit")

time: 161 us -> 159 us (0.988)
  blocking collectives: 92.3 us -> 103 us
  waiting for transfers between devices: 10.8 us -> 0.67 us
  local copies, waits for them, and re-layouts: 2.07 us -> 0.44 us
    all_gather x2, blocking collectives: 50.7 us -> 61.8 us  [spread_states(): return lax.all_gather(rounded, 'space', tiled=True)]
    all_to_all x2, waiting for transfers between devices: 10.8 us -> 0.66 us  [spread_states(): lax.all_to_all(packed.astype(jnp.bfloat16).reshape(space, -1, LANES), 'sp...]
    convert_element_type x0 -> x2, other arithmetic: none -> 4.48 us  [spread_states(): packed.astype(jnp.bfloat16).reshape(space, -1, LANES)]
    all_to_all x2, starting transfers between devices: 13 us -> 9.54 us  [spread_states(): lax.all_to_all(packed.astype(jnp.bfloat16).reshape(space, -1, LANES), 'sp...]
    reduce_sum x2, other arithmetic: 2.67 us -> 0.17 us  [spread_states(): whole = jnp.sum(pieces.astype(jnp.float32), axis=0)[:, :NORM + 1]]
    ppermute x1, starting transfers between devices: 1.81 us -> 3.85 us  [padded_pair(): lax.ppermute(tail, 'space', [(i, (i + 1) % count) for i in range(ends)])]
  transfers between devices with their start and end apart: 4 -> 4, of which waited for: 2 -> 1; matrix products, arithmetic and copies ran while one was open for 5% -> 6% of each run, Pallas kernels for 11% -> 11%
where the time goes in v9:
time: 159 us; the launch traced here: 157 us
  blocking collectives  103 us (65%)
  Pallas kernels  26 us (16%)
  starting transfers between devices  14.7 us (9%)
  other arithmetic  11.4 us (7%)
    all_gather x2, blocking collectives, spread_states(): return lax.all_gather(rounded, 'space', tiled=True)  61.8 us
    all_gather x2, blocking collectives, spread_states(): gathered = lax.all_gather(whole, 'orbit')  41.6 us
    all_to_all x2, starting transfers between devices, spread_states(): lax.all_to_all(packed.astype(jnp.bfloat16).reshape(space, -1, LANES), 'sp...  9.54 us
    pallas_call x1, Pallas kernels, on_device_body(): pl.pallas_call(forward_kernel, out_shape=(jax.ShapeDtypeStruct(flat_shape...  8.7 us
    pallas_call x1, Pallas kernels, on_device_body(): pl.pallas_call(tile_kernel, out_shape=(tile,) * 5)(q2, g2, k2, v2)  4.95 us
    pallas_call x1, Pallas kernels, on_device_body(): pl.pallas_call(backward_kernel, out_shape=(jax.ShapeDtypeStruct(flat_shap...  4.74 us
    convert_element_type x2, other arithmetic, spread_states(): packed.astype(jnp.bfloat16).reshape(space, -1, LANES)  4.48 us
    pallas_call x1, Pallas kernels, on_device_body(): pl.pallas_call(state_grad_kernel, out_shape=jax.ShapeDtypeStruct((PACKED,...  3.93 us
  transfers between devices with their start and end apart: 4, of which 1 were waited for; matrix products, arithmetic and copies ran while one was open for 6% of the time, Pallas kernels for 11%

profile of v9, /device:TPU:0, one launch (start us, length us, event | category | flops | bytes accessed | tf_op | source)
XLA Modules:
  0.0 157.4 jit_solution(17114580343544076460)
XLA Ops:
  0.6 3.7 %shard_map.85 = f32[2304,128]{1,0:T(8,128)} custom-call(bf16[128,2240]{1,0:T(8,128)(2,1)} %bitcast.32, bf16[128,2240]{1,0:T(8,128)(2,1)} %bitcast.21), custom_call_target="tpu_custom_call" | custom-call | tf_op jit(solution)/shard_map/pallas_call | solution.py:149
  4.3 0.0 copy-start
  4.3 0.0 copy-start.2
  4.4 2.2 %convert_element_type.93 = bf16[2304,128]{1,0:T(8,128)(2,1)} convert(f32[2304,128]{1,0:T(8,128)} %shard_map.85) | non-fusion elementwise | flops 294912 | bytes 1769472 | tf_op jit(solution)/shard_map/convert_element_type | solution.py:118
  6.6 5.3 %all-to-all-start = ((bf16[16,144,128]{2,1,0:T(8,128)(2,1)}), bf16[16,144,128]{2,1,0:T(8,128)(2,1)S(1)}, u32[]{:S(2)}, u32[]{:S(2)}) async-start(bf16[16,144,128]{2,1,0:T(8,128)(2,1)} %bitcast.8), calls=%async_computation | async-start | bytes 1179648 | tf_op jit(solution)/shard_map/all_to_all | solution.py:117
  11.9 0.0 copy-done
  11.9 0.0 copy-done.2
  11.9 0.0 copy-start.4
  12.0 1.1 fusion.4
  13.1 3.8 %collective-permute-start = (bf16[2,1,1,64,2240]{4,3,2,1,0:T(8,128)(2,1)}, bf16[2,1,1,64,2240]{4,3,2,1,0:T(8,128)(2,1)S(1)}, u32[]{:S(2)}, u32[]{:S(2)}) collective-permute-start(bf16[2,1,1,64,2240]{4,3,2,1,0:T(8,128)(2,1)} %get-tuple-element.33), channel_id=1, source_target_pairs={{0,1},{1,2},{2,3},{3,4},{4,5},{5,6},{6,7},{7,8},{8,9},{9,10},{10,1... | collective-permute-start | bytes 1720328 | tf_op jit(solution)/shard_map/ppermute | solution.py:17
  16.9 1.3 collective-permute-start.1
  18.2 0.0 copy-done.4
  18.3 5.0 %shard_map.84 = (bf16[20,128,128]{2,1,0:T(8,128)(2,1)}, bf16[20,128,128]{2,1,0:T(8,128)(2,1)}, bf16[20,128,128]{2,1,0:T(8,128)(2,1)}, bf16[20,128,128]{2,1,0:T(8,128)(2,1)}, bf16[20,128,128]{2,1,0:T(8,128)(2,1)}) custom-call(bf16[128,2240]{1,0:T(8,128)(2,1)} %bitcast.34, bf16[128,2240]{1,0:T(8,128)(2,1)} %bitcast.25, bf16[128,2240]{1,0:T(8,128)(2,1)} %bitcast.33, ...), custom_call_target="tpu_custom_call" | custom-call | tf_op jit(solution)/shard_map/pallas_call | solution.py:153
  23.2 0.2 slice_reduce_fusion.8
  23.5 0.7 all-to-all-done
  24.1 0.1 convert_reduce_fusion.1
  24.2 23.3 %all-gather = f32[2304,113]{1,0:T(8,128)S(1)} all-gather(f32[144,113]{1,0:T(8,128)S(1)} %bitcast.35), channel_id=2, replica_groups=mesh['orbit'=16,'space'=16] {'orbit'}, dimensions={0}, use_global_device_ids=true | all-gather | bytes 1106496 | tf_op jit(solution)/shard_map/all_gather | solution.py:123
  47.5 0.2 select_reduce_fusion.1
  47.8 35.1 %all_gather.20.s_ref = bf16[2304,128]{1,0:T(8,128)(2,1)} all-gather(bf16[144,128]{1,0:T(8,128)(2,1)S(1)} %pad.12), channel_id=1, replica_groups=mesh['orbit'=16,'space'=16] {'space'}, dimensions={0}, use_global_device_ids=true | all-gather | bytes 626688 | tf_op jit(solution)/shard_map/all_gather | solution.py:133
  82.9 3.9 %shard_map.87 = f32[2304,128]{1,0:T(8,128)} custom-call(bf16[20,128,128]{2,1,0:T(8,128)(2,1)} %get-tuple-element.13.qt_ref, bf16[20,128,128]{2,1,0:T(8,128)(2,1)} %get-tuple-element.19.qx_ref, bf16[20,128,128]{2,1,0:T(8,128)(2,1)} %get-tuple-element.14.gt_ref, bf16[2304,128]{1,0:T(8,128)(2,1)} %all_gather.20.s_ref), custom_call_target="tpu_custom_call" | custom-call | tf_op jit(solution)/shard_map/pallas_call | solution.py:174
  86.8 0.0 copy-start.1
  86.8 0.0 copy-start.3
  86.8 2.2 %convert_element_type.106 = bf16[2304,128]{1,0:T(8,128)(2,1)} convert(f32[2304,128]{1,0:T(8,128)} %shard_map.87) | non-fusion elementwise | flops 294912 | bytes 1769472 | tf_op jit(solution)/shard_map/convert_element_type | solution.py:118
  89.1 4.2 %all-to-all-start.1 = ((bf16[16,144,128]{2,1,0:T(8,128)(2,1)}), bf16[16,144,128]{2,1,0:T(8,128)(2,1)S(1)}, u32[]{:S(2)}, u32[]{:S(2)}) async-start(bf16[16,144,128]{2,1,0:T(8,128)(2,1)} %bitcast.14), calls=%async_computation.1 | async-start | bytes 1179648 | tf_op jit(solution)/shard_map/all_to_all | solution.py:117
  93.3 0.0 collective-permute-done
  93.3 0.0 collective-permute-done.1
  93.3 0.0 copy-done.1
  93.3 0.0 copy-done.3
  93.3 1.1 select_maximum_fusion
  94.4 0.2 slice_bitcast_fusion
  94.6 2.1 %multiply_add_fusion.1 = f32[1,2,64,2240]{3,2,1,0:T(8,128)} fusion(bf16[1,4,66,2240]{3,2,1,0:T(8,128)(2,1)S(1)} %get-tuple-element.32, f32[2240]{0:T(1024)S(1)} %get-tuple-element.23, f32[2240]{0:T(1024)S(1)} %get-tuple-element.24, f32[2240]{0:T(1024)S(1)} %get-tuple-element.25, f32[2240]{0:T(1024)S(1)} %get-tuple-element.26, ...), kind=kLoop, calls=%fused_computation.17 | loop fusion | flops 7454720 | bytes 6388480 | tf_op jit(solution)/shard_map/add | solution.py:166
  96.7 8.7 %shard_map.86 = (bf16[128,2240]{1,0:T(8,128)(2,1)}, bf16[128,2240]{1,0:T(8,128)(2,1)}) custom-call(bf16[20,128,128]{2,1,0:T(8,128)(2,1)} %get-tuple-element.13.qt_ref, bf16[20,128,128]{2,1,0:T(8,128)(2,1)} %get-tuple-element.14.gt_ref, f32[128,2240]{1,0:T(8,128)} %bitcast.29, bf16[2304,128]{1,0:T(8,128)(2,1)} %all_gather.20.s_ref), custom_call_target="tpu_custom_call" | custom-call | tf_op jit(solution)/shard_map/pallas_call | solution.py:178
  105.4 2.1 %multiply_add_fusion = f32[1,2,64,2240]{3,2,1,0:T(8,128)} fusion(bf16[1,4,66,2240]{3,2,1,0:T(8,128)(2,1)S(1)} %get-tuple-element.31, f32[2240]{0:T(1024)S(1)} %get-tuple-element.23, f32[2240]{0:T(1024)S(1)} %get-tuple-element.24, f32[2240]{0:T(1024)S(1)} %get-tuple-element.25, f32[2240]{0:T(1024)S(1)} %get-tuple-element.26, f32[2240]{0:T(1024)S(1)} %get-tuple-element.27, ...), kind=kLoop, calls=%fused_computation.14 | loop fusion | flops 7454720 | bytes 6388480 | tf_op jit(solution)/shard_map/add | solution.py:169
  107.4 0.0 all-to-all-done.1
  107.4 0.1 convert_reduce_fusion
  107.5 18.3 %all-gather.1 = f32[2304,113]{1,0:T(8,128)S(1)} all-gather(f32[144,113]{1,0:T(8,128)S(1)} %slice_divide_fusion), channel_id=3, replica_groups=mesh['orbit'=16,'space'=16] {'orbit'}, dimensions={0}, use_global_device_ids=true | all-gather | bytes 1106496 | tf_op jit(solution)/shard_map/all_gather | solution.py:129
  125.8 0.2 select_reduce_fusion
  126.0 26.7 %all_gather.23.s_ref = bf16[2304,128]{1,0:T(8,128)(2,1)} all-gather(bf16[144,128]{1,0:T(8,128)(2,1)S(1)} %pad.13), channel_id=1, replica_groups=mesh['orbit'=16,'space'=16] {'space'}, dimensions={0}, use_global_device_ids=true | all-gather | bytes 626688 | tf_op jit(solution)/shard_map/all_gather | solution.py:133
  152.7 4.7 %shard_map.88 = (bf16[128,2240]{1,0:T(8,128)(2,1)}, bf16[128,2240]{1,0:T(8,128)(2,1)}) custom-call(bf16[20,128,128]{2,1,0:T(8,128)(2,1)} %get-tuple-element.17.kt_ref, bf16[20,128,128]{2,1,0:T(8,128)(2,1)} %get-tuple-element.18.vt_ref, f32[128,2240]{1,0:T(8,128)} %bitcast.28, bf16[2304,128]{1,0:T(8,128)(2,1)} %all_gather.23.s_ref), custom_call_target="tpu_custom_call" | custom-call | tf_op jit(solution)/shard_map/pallas_call | solution.py:186
  (7 shorter events, 0.1 us)
Async XLA Ops:
  4.3 7.6 %copy-start = (bf16[1,2,64,2240]{3,2,1,0:T(8,128)(2,1)S(1)}, bf16[1,2,64,2240]{3,2,1,0:T(8,128)(2,1)}, u32[]{:S(2)}) copy-start(bf16[1,2,64,2240]{3,2,1,0:T(8,128)(2,1)} %param.7) | copy-start | bytes 1720324
  4.3 7.6 %copy-start.2 = (bf16[1,2,64,2240]{3,2,1,0:T(8,128)(2,1)S(1)}, bf16[1,2,64,2240]{3,2,1,0:T(8,128)(2,1)}, u32[]{:S(2)}) copy-start(bf16[1,2,64,2240]{3,2,1,0:T(8,128)(2,1)} %param.9) | copy-start | bytes 1720324
  6.6 17.5 %all-to-all-start = ((bf16[16,144,128]{2,1,0:T(8,128)(2,1)}), bf16[16,144,128]{2,1,0:T(8,128)(2,1)S(1)}, u32[]{:S(2)}, u32[]{:S(2)}) async-start(bf16[16,144,128]{2,1,0:T(8,128)(2,1)} %bitcast.8), calls=%async_computation | async-start | bytes 1179648 | tf_op jit(solution)/shard_map/all_to_all | solution.py:117
  11.9 6.3 %copy-start.4 = (bf16[3,3,2240]{2,1,0:T(4,128)(2,1)S(1)}, bf16[3,3,2240]{2,1,0:T(4,128)(2,1)}, u32[]{:S(2)}) copy-start(bf16[3,3,2240]{2,1,0:T(4,128)(2,1)} %param.8) | copy-start | bytes 120964
  13.1 80.2 %collective-permute-start = (bf16[2,1,1,64,2240]{4,3,2,1,0:T(8,128)(2,1)}, bf16[2,1,1,64,2240]{4,3,2,1,0:T(8,128)(2,1)S(1)}, u32[]{:S(2)}, u32[]{:S(2)}) collective-permute-start(bf16[2,1,1,64,2240]{4,3,2,1,0:T(8,128)(2,1)} %get-tuple-element.33), channel_id=1, source_target_pairs={{0,1},{1,2},{2,3},{3,4},{4,5},{5,6},{6,7},{7,8},{8,9},{9,10},{10,1... | collective-permute-start | bytes 1720328 | tf_op jit(solution)/shard_map/ppermute | solution.py:17
  16.9 76.4 %collective-permute-start.1 = (bf16[2,1,1,64,2240]{4,3,2,1,0:T(8,128)(2,1)}, bf16[2,1,1,64,2240]{4,3,2,1,0:T(8,128)(2,1)S(1)}, u32[]{:S(2)}, u32[]{:S(2)}) collective-permute-start(bf16[2,1,1,64,2240]{4,3,2,1,0:T(8,128)(2,1)} %get-tuple-element.34), channel_id=1, source_target_pairs={{1,0},{2,1},{3,2},{4,3},{5,4},{6,5},{7,6},{8,7},{9,8},{10,9},{11,1... | collective-permute-start | bytes 1720328 | tf_op jit(solution)/shard_map/ppermute | solution.py:18
  86.8 6.5 %copy-start.1 = (bf16[1,2,64,2240]{3,2,1,0:T(8,128)(2,1)S(1)}, bf16[1,2,64,2240]{3,2,1,0:T(8,128)(2,1)}, u32[]{:S(2)}) copy-start(bf16[1,2,64,2240]{3,2,1,0:T(8,128)(2,1)} %param.7) | copy-start | bytes 1720324
  86.8 6.5 %copy-start.3 = (bf16[1,2,64,2240]{3,2,1,0:T(8,128)(2,1)S(1)}, bf16[1,2,64,2240]{3,2,1,0:T(8,128)(2,1)}, u32[]{:S(2)}) copy-start(bf16[1,2,64,2240]{3,2,1,0:T(8,128)(2,1)} %param.9) | copy-start | bytes 1720324
  89.1 18.4 %all-to-all-start.1 = ((bf16[16,144,128]{2,1,0:T(8,128)(2,1)}), bf16[16,144,128]{2,1,0:T(8,128)(2,1)S(1)}, u32[]{:S(2)}, u32[]{:S(2)}) async-start(bf16[16,144,128]{2,1,0:T(8,128)(2,1)} %bitcast.14), calls=%async_computation.1 | async-start | bytes 1179648 | tf_op jit(solution)/shard_map/all_to_all | solution.py:117

commit v10 on v8

--- a/solution.py
+++ b/solution.py
@@ -8,7 +8,7 @@
 HD = 112
 
 
-def padded_pair(cells, width):
+def halo_rows(cells, width):
     count = lax.axis_size("space")
     ends = count - 1
     rows = cells.shape[2]
@@ -16,13 +16,14 @@
     tail = cells[:, :, rows - width :]
     above = lax.ppermute(tail, "space", [(i, (i + 1) % count) for i in range(ends)])
     below = lax.ppermute(head, "space", [((i + 1) % count, i) for i in range(ends)])
-    return jnp.concatenate([above, cells, below], axis=2)
+    return above, below
 
 
 ROWS = HEADS * HD
 PACKED = 2304
 LANES = 128
 NORM = HD
+WIDTH = NORM + 1
 
 
 def lane_one(tokens):
@@ -31,8 +32,8 @@
 
 
 def part_kernel(k_ref, v_ref, s_ref):
-    s_ref[ROWS:, :] = jnp.zeros((PACKED - ROWS, LANES), jnp.float32)
-    extra = lane_one(k_ref.shape[0])
+    s_ref[ROWS:, :] = jnp.zeros((PACKED - ROWS, WIDTH), jnp.float32)
+    extra = jnp.ones((k_ref.shape[0], 1), jnp.bfloat16)
     for h in range(HEADS):
         cols = slice(h * HD, (h + 1) * HD)
         kf = jnp.maximum(k_ref[:, cols], 0)
@@ -57,14 +58,14 @@
 
 
 def state_grad_kernel(qt_ref, qx_ref, gt_ref, s_ref, sg_ref):
-    sg_ref[ROWS:, :] = jnp.zeros((PACKED - ROWS, LANES), jnp.float32)
-    lanes = lax.broadcasted_iota(jnp.int32, (qt_ref.shape[1], LANES), 1)
+    sg_ref[ROWS:, :] = jnp.zeros((PACKED - ROWS, WIDTH), jnp.float32)
+    lanes = lax.broadcasted_iota(jnp.int32, (qt_ref.shape[1], WIDTH), 1)
     for h in range(HEADS):
         state = s_ref[h * HD : h * HD + LANES, :]
         wide = jnp.dot(qt_ref[h], state, preferred_element_type=jnp.float32)
         denominator = wide[:, NORM : NORM + 1] + 1.0
         inverse = 1.0 / denominator
-        gw = gt_ref[h].astype(jnp.float32)
+        gw = gt_ref[h][:, :WIDTH].astype(jnp.float32)
         num_grad = (gw * inverse).astype(jnp.bfloat16)
         den_grad = (
             -jnp.sum(gw * wide, axis=1, keepdims=True) / (denominator * denominator)
@@ -75,7 +76,7 @@
 
 
 def forward_kernel(qt_ref, gt_ref, c_ref, s_ref, a_ref, gq_ref):
-    lanes = lax.broadcasted_iota(jnp.int32, (qt_ref.shape[1], LANES), 1)
+    lanes = lax.broadcasted_iota(jnp.int32, (qt_ref.shape[1], WIDTH), 1)
     for h in range(HEADS):
         cols = slice(h * HD, (h + 1) * HD)
         qf = qt_ref[h]
@@ -83,7 +84,7 @@
         denominator = wide[:, NORM : NORM + 1] + 1.0
         inverse = 1.0 / denominator
         a_ref[:, cols] = (wide[:, :HD] * inverse + c_ref[:, cols]).astype(jnp.bfloat16)
-        gw = gt_ref[h].astype(jnp.float32)
+        gw = gt_ref[h][:, :WIDTH].astype(jnp.float32)
         num_grad = (gw * inverse).astype(jnp.bfloat16)
         den_grad = (
             -jnp.sum(gw * wide, axis=1, keepdims=True) / (denominator * denominator)
@@ -101,7 +102,7 @@
         cols = slice(h * HD, (h + 1) * HD)
         kf = kt_ref[h]
         key_grad = lax.dot_general(
-            vt_ref[h], s_ref[h * HD : (h + 1) * HD, :], (((1,), (1,)), ((), ())),
+            vt_ref[h][:, :WIDTH], s_ref[h * HD : (h + 1) * HD, :], (((1,), (1,)), ((), ())),
             preferred_element_type=jnp.float32,
         )
         gk_ref[:, cols] = jnp.where(kf[:, :HD] > 0, key_grad, 0.0).astype(jnp.bfloat16)
@@ -110,12 +111,13 @@
         gv_ref[:, cols] = (value_grad + c_ref[:, cols]).astype(jnp.bfloat16)
 
 
-def spread_states(packed, reverse, counts):
+def spread_states(packed, reverse, counts, tie=None):
     space = lax.axis_size("space")
     orbit = lax.axis_size("orbit")
     place = lax.axis_index("orbit")
-    pieces = lax.all_to_all(packed.reshape(space, -1, LANES), "space", 0, 0, tiled=True)
-    whole = jnp.sum(pieces, axis=0)[:, : NORM + 1]
+    pieces = lax.all_to_all(packed.reshape(space, -1, WIDTH), "space", 0, 0, tiled=True)
+    pieces, tie = lax.optimization_barrier((pieces, tie))
+    whole = jnp.sum(pieces, axis=0)
     views = jnp.arange(orbit)
     if not reverse:
         gathered = lax.all_gather(whole, "orbit")
@@ -127,8 +129,7 @@
         gathered = lax.all_gather(whole, "orbit")
         keep = views >= place
         summed = jnp.sum(jnp.where(keep[:, None, None], gathered, 0.0), axis=0)
-    rounded = jnp.pad(summed.astype(jnp.bfloat16), ((0, 0), (0, LANES - NORM - 1)))
-    return lax.all_gather(rounded, "space", tiled=True)
+    return lax.all_gather(summed.astype(jnp.bfloat16), "space", tiled=True), tie
 
 
 def on_device_body(queries, keys_in, values, conv_weight, grad_out):
@@ -145,15 +146,17 @@
     )
     f32 = jnp.float32
     packed_part = pl.pallas_call(
-        part_kernel, out_shape=jax.ShapeDtypeStruct((PACKED, LANES), f32)
+        part_kernel, out_shape=jax.ShapeDtypeStruct((PACKED, WIDTH), f32)
     )(k2, v2)
     tile = jax.ShapeDtypeStruct((HEADS, token_count, LANES), jnp.bfloat16)
     q_tiles, q_cross, g_tiles, k_tiles, v_tiles = pl.pallas_call(
         tile_kernel, out_shape=(tile,) * 5
     )(q2, g2, k2, v2)
-    state_b = spread_states(packed_part, False, count)
-
-    pair = padded_pair(jnp.stack([values, grad_out]), 1)
+    cells = jnp.stack([values, grad_out])
+    halo = halo_rows(cells, 1)
+    state_b, (above, below) = spread_states(packed_part, False, count, halo)
+
+    pair = jnp.concatenate([above, cells, below], axis=2)
     pair = jnp.pad(pair, ((0, 0), (0, 0), (0, 0), (1, 1), (0, 0)))
     value_pad, grad_pad = pair[0], pair[1]
     weight_wide = conv_weight.astype(f32)
@@ -170,7 +173,7 @@
 
     bf = jnp.bfloat16
     state_grad = pl.pallas_call(
-        state_grad_kernel, out_shape=jax.ShapeDtypeStruct((PACKED, LANES), f32)
+        state_grad_kernel, out_shape=jax.ShapeDtypeStruct((PACKED, WIDTH), f32)
     )(q_tiles, q_cross, g_tiles, state_b)
     conv_flat = conv_term.reshape(flat_shape)
     attended, grad_query = pl.pallas_call(
@@ -180,7 +183,7 @@
             jax.ShapeDtypeStruct(flat_shape, bf),
         ),
     )(q_tiles, g_tiles, conv_flat, state_b)
-    back_state = spread_states(state_grad, True, count)
+    back_state, _ = spread_states(state_grad, True, count)
     grad_key, grad_value = pl.pallas_call(
         backward_kernel,
         out_shape=(

time: 161 us -> 164 us (1.019)
  waiting for transfers between devices: 10.8 us -> 14.2 us
  other arithmetic: 10.9 us -> 9.18 us
    ppermute x2, waiting for transfers between devices: 0.01 us -> 12.7 us  [the longest x1 12.7 us: halo_rows(): lax.ppermute(head, 'space', [((i + 1) % count, i) for i in range(ends)])]
    all_to_all x2, waiting for transfers between devices: 10.8 us -> 1.48 us  [spread_states(): lax.all_to_all(packed.reshape(space, -1, WIDTH), 'space', 0, 0, tiled=True)]
    all_to_all x2, starting transfers between devices: 13 us -> 10.2 us  [spread_states(): lax.all_to_all(packed.reshape(space, -1, WIDTH), 'space', 0, 0, tiled=True)]
    ppermute x2, starting transfers between devices: 3.1 us -> 5.88 us  [the longest x1 4.58 us: halo_rows(): lax.ppermute(tail, 'space', [(i, (i + 1) % count) for i in range(ends)])]
  transfers between devices with their start and end apart: 4 -> 4, of which waited for: 2 -> 2; matrix products, arithmetic and copies ran while one was open for 5% -> 5% of each run, Pallas kernels for 11% -> 9%
where the time goes in v10:
time: 164 us; the launch traced here: 163 us
  blocking collectives  93.9 us (57%)
  Pallas kernels  26.2 us (16%)
  starting transfers between devices  16 us (10%)
  waiting for transfers between devices  14.2 us (9%)
  other arithmetic  9.18 us (6%)
  local copies, waits for them, and re-layouts  2.05 us (1%)
    all_gather x2, blocking collectives, spread_states(): lax.all_gather(summed.astype(jnp.bfloat16), 'space', tiled=True)  52.3 us
    all_gather x2, blocking collectives, spread_states(): gathered = lax.all_gather(whole, 'orbit')  41.6 us
    ppermute x1, waiting for transfers between devices, halo_rows(): lax.ppermute(head, 'space', [((i + 1) % count, i) for i in range(ends)])  12.7 us
    all_to_all x2, starting transfers between devices, spread_states(): lax.all_to_all(packed.reshape(space, -1, WIDTH), 'space', 0, 0, tiled=True)  10.2 us
    pallas_call x1, Pallas kernels, on_device_body(): pl.pallas_call(forward_kernel, out_shape=(jax.ShapeDtypeStruct(flat_shape...  8.91 us
    pallas_call x1, Pallas kernels, on_device_body(): pl.pallas_call(tile_kernel, out_shape=(tile,) * 5)(q2, g2, k2, v2)  4.94 us
    pallas_call x1, Pallas kernels, on_device_body(): pl.pallas_call(backward_kernel, out_shape=(jax.ShapeDtypeStruct(flat_shap...  4.75 us
    ppermute x1, starting transfers between devices, halo_rows(): lax.ppermute(tail, 'space', [(i, (i + 1) % count) for i in range(ends)])  4.58 us
  transfers between devices with their start and end apart: 4, of which 2 were waited for; matrix products, arithmetic and copies ran while one was open for 5% of the time, Pallas kernels for 9%

profile of v10, /device:TPU:0, one launch (start us, length us, event | category | flops | bytes accessed | tf_op | source)
XLA Modules:
  0.0 162.5 jit_solution(1358175458119874971)
XLA Ops:
  0.6 3.7 %shard_map.85 = f32[2304,113]{1,0:T(8,128)} custom-call(bf16[128,2240]{1,0:T(8,128)(2,1)} %bitcast.33, bf16[128,2240]{1,0:T(8,128)(2,1)} %bitcast.20), custom_call_target="tpu_custom_call" | custom-call | tf_op jit(solution)/shard_map/pallas_call | solution.py:148
  4.3 0.0 copy-start
  4.3 0.0 copy-start.2
  4.3 5.5 %all-to-all-start = ((f32[16,144,113]{2,1,0:T(8,128)}), f32[16,144,113]{2,1,0:T(8,128)S(1)}, u32[]{:S(2)}, u32[]{:S(2)}) async-start(f32[16,144,113]{2,1,0:T(8,128)} %bitcast.28), calls=%async_computation | async-start | bytes 2359296 | tf_op jit(solution)/shard_map/all_to_all | solution.py:118
  9.8 0.0 copy-done
  9.8 0.0 copy-done.2
  9.8 0.1 pad_maximum_fusion
  9.9 1.3 collective-permute-start.1
  11.2 4.6 %collective-permute-start = (bf16[2,1,1,64,2240]{4,3,2,1,0:T(8,128)(2,1)S(1)}, bf16[2,1,1,64,2240]{4,3,2,1,0:T(8,128)(2,1)S(1)}, u32[]{:S(2)}, u32[]{:S(2)}) collective-permute-start(bf16[2,1,1,64,2240]{4,3,2,1,0:T(8,128)(2,1)S(1)} %get-tuple-element.40), channel_id=1, source_target_pairs={{0,1},{1,2},{2,3},{3,4},{4,5},{5,6},{6,7},{7,8},{8,9},{9,10},{10,1... | collective-permute-start | bytes 1720328 | tf_op jit(solution)/shard_map/ppermute | solution.py:17
  15.8 1.5 convert_element_type.68
  17.3 4.9 %shard_map.84 = (bf16[20,128,128]{2,1,0:T(8,128)(2,1)}, bf16[20,128,128]{2,1,0:T(8,128)(2,1)}, bf16[20,128,128]{2,1,0:T(8,128)(2,1)}, bf16[20,128,128]{2,1,0:T(8,128)(2,1)}, bf16[20,128,128]{2,1,0:T(8,128)(2,1)}) custom-call(bf16[128,2240]{1,0:T(8,128)(2,1)} %bitcast.35, bf16[128,2240]{1,0:T(8,128)(2,1)} %bitcast.24, bf16[128,2240]{1,0:T(8,128)(2,1)} %bitcast.34, ...), custom_call_target="tpu_custom_call" | custom-call | tf_op jit(solution)/shard_map/pallas_call | solution.py:152
  22.2 0.5 iota_compare_fusion.3
  22.8 1.8 %slice_reduce_fusion.8 = (f32[2240]{0:T(1024)S(1)}, f32[2240]{0:T(1024)}, f32[2240]{0:T(1024)}, f32[2240]{0:T(1024)}, f32[2240]{0:T(1024)}, /*index=5*/f32[2240]...) fusion(f32[3,3,2240]{2,1,0:T(4,128)} %convert_element_type.68), kind=kLoop, calls=%fused_computation.28 | loop fusion | bytes 161280 | tf_op jit(solution)/shard_map/slice | solution.py:167
  24.6 12.7 %collective-permute-done.1 = bf16[2,1,1,64,2240]{4,3,2,1,0:T(8,128)(2,1)S(1)} collective-permute-done((bf16[2,1,1,64,2240]{4,3,2,1,0:T(8,128)(2,1)S(1)}, bf16[2,1,1,64,2240]{4,3,2,1,0:T(8,128)(2,1)S(1)}, u32[]{:S(2)}, u32[]{:S(2)}) %collective-permute-start.1) | collective-permute-done | bytes 573472 | tf_op jit(solution)/shard_map/ppermute | solution.py:18
  37.3 0.0 collective-permute-done
  37.3 0.0 all-to-all-done
  37.3 0.1 reduce_sum.36
  37.4 23.3 %all-gather = f32[2304,113]{1,0:T(8,128)S(1)} all-gather(f32[144,113]{1,0:T(8,128)S(1)} %reduce_sum.36), channel_id=2, replica_groups=mesh['orbit'=16,'space'=16] {'orbit'}, dimensions={0}, use_global_device_ids=true | all-gather | bytes 1106496 | tf_op jit(solution)/shard_map/all_gather | solution.py:123
  60.8 0.0 copy-done.12
  60.8 0.2 select_reduce_fusion.1
  61.0 27.4 %all_gather.18.s_ref = bf16[2304,113]{1,0:T(8,128)(2,1)} all-gather(bf16[144,113]{1,0:T(8,128)(2,1)S(1)} %divide_convert_fusion), channel_id=1, replica_groups=mesh['orbit'=16,'space'=16] {'space'}, dimensions={0}, use_global_device_ids=true | all-gather | bytes 553248 | tf_op jit(solution)/shard_map/all_gather | solution.py:132
  88.4 0.0 copy-done.1
  88.4 0.0 copy-done.3
  88.4 1.1 select_maximum_fusion
  89.5 0.2 slice_bitcast_fusion
  89.7 4.0 %shard_map.87 = f32[2304,113]{1,0:T(8,128)} custom-call(bf16[20,128,128]{2,1,0:T(8,128)(2,1)} %get-tuple-element.16.qt_ref, bf16[20,128,128]{2,1,0:T(8,128)(2,1)} %get-tuple-element.25.qx_ref, bf16[20,128,128]{2,1,0:T(8,128)(2,1)} %get-tuple-element.17.gt_ref, bf16[2304,113]{1,0:T(8,128)(2,1)} %all_gather.18.s_ref), custom_call_target="tpu_custom_call" | custom-call | tf_op jit(solution)/shard_map/pallas_call | solution.py:175
  93.6 0.0 copy-start.8
  93.7 0.0 copy-start.9
  93.7 0.0 copy-start.10
  93.7 0.0 copy-start.11
  93.7 4.7 %all-to-all-start.1 = ((f32[16,144,113]{2,1,0:T(8,128)}), f32[16,144,113]{2,1,0:T(8,128)}, u32[]{:S(2)}, u32[]{:S(2)}) async-start(f32[16,144,113]{2,1,0:T(8,128)} %bitcast.27), calls=%async_computation.1 | async-start | bytes 2359296 | tf_op jit(solution)/shard_map/all_to_all | solution.py:118
  98.4 0.0 copy-done.4
  98.4 0.0 copy-done.5
  98.4 0.0 copy-done.6
  98.4 0.0 copy-done.7
  98.4 0.0 copy-done.8
  98.5 0.0 copy-done.9
  98.5 0.0 copy-done.10
  98.5 0.0 copy-done.11
  98.5 2.1 %multiply_add_fusion.1 = f32[1,2,64,2240]{3,2,1,0:T(8,128)} fusion(bf16[1,4,66,2240]{3,2,1,0:T(8,128)(2,1)S(1)} %get-tuple-element.38, f32[2240]{0:T(1024)S(1)} %copy-done.4, f32[2240]{0:T(1024)S(1)} %copy-done.5, f32[2240]{0:T(1024)S(1)} %copy-done.6, f32[2240]{0:T(1024)S(1)} %copy-done.7, f32[2240]{0:T(1024)S(1)} %copy-done.8, f32[2240]{0:T(1024)S(1)} %copy-done.9, ...), kind=kLoop, calls=%fused_computation.15 | loop fusion | flops 7454720 | bytes 6388480 | tf_op jit(solution)/shard_map/add | solution.py:167
  100.5 8.9 %shard_map.86 = (bf16[128,2240]{1,0:T(8,128)(2,1)}, bf16[128,2240]{1,0:T(8,128)(2,1)}) custom-call(bf16[20,128,128]{2,1,0:T(8,128)(2,1)} %get-tuple-element.16.qt_ref, bf16[20,128,128]{2,1,0:T(8,128)(2,1)} %get-tuple-element.17.gt_ref, f32[128,2240]{1,0:T(8,128)} %bitcast.30, bf16[2304,113]{1,0:T(8,128)(2,1)} %all_gather.18.s_ref), custom_call_target="tpu_custom_call" | custom-call | tf_op jit(solution)/shard_map/pallas_call | solution.py:179
  109.5 2.1 %multiply_add_fusion = f32[1,2,64,2240]{3,2,1,0:T(8,128)} fusion(bf16[1,4,66,2240]{3,2,1,0:T(8,128)(2,1)S(1)} %get-tuple-element.37, f32[2240]{0:T(1024)S(1)} %copy-done.4, f32[2240]{0:T(1024)S(1)} %copy-done.5, f32[2240]{0:T(1024)S(1)} %copy-done.6, f32[2240]{0:T(1024)S(1)} %copy-done.7, f32[2240]{0:T(1024)S(1)} %copy-done.8, f32[2240]{0:T(1024)S(1)} %copy-done.9, ...), kind=kLoop, calls=%fused_computation.13 | loop fusion | flops 7454720 | bytes 6388480 | tf_op jit(solution)/shard_map/add | solution.py:170
  111.5 1.5 all-to-all-done.1
  113.0 1.4 reduce_sum.38
  114.4 18.3 %all-gather.1 = f32[2304,113]{1,0:T(8,128)S(1)} all-gather(f32[144,113]{1,0:T(8,128)S(1)} %broadcast_divide_fusion), channel_id=3, replica_groups=mesh['orbit'=16,'space'=16] {'orbit'}, dimensions={0}, use_global_device_ids=true | all-gather | bytes 1106496 | tf_op jit(solution)/shard_map/all_gather | solution.py:129
  132.7 0.2 select_reduce_fusion
  132.9 24.9 %all_gather.20.s_ref = bf16[2304,113]{1,0:T(8,128)(2,1)} all-gather(bf16[144,113]{1,0:T(8,128)(2,1)S(1)} %select_reduce_fusion), channel_id=1, replica_groups=mesh['orbit'=16,'space'=16] {'space'}, dimensions={0}, use_global_device_ids=true | all-gather | bytes 553248 | tf_op jit(solution)/shard_map/all_gather | solution.py:132
  157.8 4.8 %shard_map.88 = (bf16[128,2240]{1,0:T(8,128)(2,1)}, bf16[128,2240]{1,0:T(8,128)(2,1)}) custom-call(bf16[20,128,128]{2,1,0:T(8,128)(2,1)} %get-tuple-element.23.kt_ref, bf16[20,128,128]{2,1,0:T(8,128)(2,1)} %get-tuple-element.24.vt_ref, f32[128,2240]{1,0:T(8,128)} %bitcast.29, bf16[2304,113]{1,0:T(8,128)(2,1)} %all_gather.20.s_ref), custom_call_target="tpu_custom_call" | custom-call | tf_op jit(solution)/shard_map/pallas_call | solution.py:187
  (10 shorter events, 0.0 us)
Async XLA Ops:
  4.3 5.5 %copy-start = (bf16[1,2,64,2240]{3,2,1,0:T(8,128)(2,1)S(1)}, bf16[1,2,64,2240]{3,2,1,0:T(8,128)(2,1)}, u32[]{:S(2)}) copy-start(bf16[1,2,64,2240]{3,2,1,0:T(8,128)(2,1)} %param.7) | copy-start | bytes 1720324
  4.3 5.5 %copy-start.2 = (bf16[1,2,64,2240]{3,2,1,0:T(8,128)(2,1)S(1)}, bf16[1,2,64,2240]{3,2,1,0:T(8,128)(2,1)}, u32[]{:S(2)}) copy-start(bf16[1,2,64,2240]{3,2,1,0:T(8,128)(2,1)} %param.9) | copy-start | bytes 1720324
  4.3 33.0 %all-to-all-start = ((f32[16,144,113]{2,1,0:T(8,128)}), f32[16,144,113]{2,1,0:T(8,128)S(1)}, u32[]{:S(2)}, u32[]{:S(2)}) async-start(f32[16,144,113]{2,1,0:T(8,128)} %bitcast.28), calls=%async_computation | async-start | bytes 2359296 | tf_op jit(solution)/shard_map/all_to_all | solution.py:118
  9.9 27.4 %collective-permute-start.1 = (bf16[2,1,1,64,2240]{4,3,2,1,0:T(8,128)(2,1)S(1)}, bf16[2,1,1,64,2240]{4,3,2,1,0:T(8,128)(2,1)S(1)}, u32[]{:S(2)}, u32[]{:S(2)}) collective-permute-start(bf16[2,1,1,64,2240]{4,3,2,1,0:T(8,128)(2,1)S(1)} %get-tuple-element.39), channel_id=1, source_target_pairs={{1,0},{2,1},{3,2},{4,3},{5,4},{6,5},{7,6},{8,7},{9,8},{10,9},{11,1... | collective-permute-start | bytes 1720328 | tf_op jit(solution)/shard_map/ppermute | solution.py:18
  11.2 26.1 %collective-permute-start = (bf16[2,1,1,64,2240]{4,3,2,1,0:T(8,128)(2,1)S(1)}, bf16[2,1,1,64,2240]{4,3,2,1,0:T(8,128)(2,1)S(1)}, u32[]{:S(2)}, u32[]{:S(2)}) collective-permute-start(bf16[2,1,1,64,2240]{4,3,2,1,0:T(8,128)(2,1)S(1)} %get-tuple-element.40), channel_id=1, source_target_pairs={{0,1},{1,2},{2,3},{3,4},{4,5},{5,6},{6,7},{7,8},{8,9},{9,10},{10,1... | collective-permute-start | bytes 1720328 | tf_op jit(solution)/shard_map/ppermute | solution.py:17
  37.3 23.4 %copy-start.12 = (pred[16]{0:T(512)(128)(4,1)S(1)}, pred[16]{0:T(512)(128)(4,1)}, u32[]{:S(2)}) copy-start(pred[16]{0:T(512)(128)(4,1)} %iota_compare_fusion.3) | copy-start | bytes 52
  60.8 27.6 %copy-start.1 = (bf16[1,2,64,2240]{3,2,1,0:T(8,128)(2,1)S(1)}, bf16[1,2,64,2240]{3,2,1,0:T(8,128)(2,1)}, u32[]{:S(2)}) copy-start(bf16[1,2,64,2240]{3,2,1,0:T(8,128)(2,1)} %param.7) | copy-start | bytes 1720324
  60.8 27.6 %copy-start.3 = (bf16[1,2,64,2240]{3,2,1,0:T(8,128)(2,1)S(1)}, bf16[1,2,64,2240]{3,2,1,0:T(8,128)(2,1)}, u32[]{:S(2)}) copy-start(bf16[1,2,64,2240]{3,2,1,0:T(8,128)(2,1)} %param.9) | copy-start | bytes 1720324
  93.6 4.8 %copy-start.4 = (f32[2240]{0:T(1024)S(1)}, f32[2240]{0:T(1024)}, u32[]{:S(2)}) copy-start(f32[2240]{0:T(1024)} %get-tuple-element.29) | copy-start | bytes 26884
  93.6 4.8 %copy-start.5 = (f32[2240]{0:T(1024)S(1)}, f32[2240]{0:T(1024)}, u32[]{:S(2)}) copy-start(f32[2240]{0:T(1024)} %get-tuple-element.30) | copy-start | bytes 26884
  93.6 4.8 %copy-start.6 = (f32[2240]{0:T(1024)S(1)}, f32[2240]{0:T(1024)}, u32[]{:S(2)}) copy-start(f32[2240]{0:T(1024)} %get-tuple-element.31) | copy-start | bytes 26884
  93.6 4.8 %copy-start.7 = (f32[2240]{0:T(1024)S(1)}, f32[2240]{0:T(1024)}, u32[]{:S(2)}) copy-start(f32[2240]{0:T(1024)} %get-tuple-element.32) | copy-start | bytes 26884
  93.6 4.8 %copy-start.8 = (f32[2240]{0:T(1024)S(1)}, f32[2240]{0:T(1024)}, u32[]{:S(2)}) copy-start(f32[2240]{0:T(1024)} %get-tuple-element.33) | copy-start | bytes 26884
  93.7 4.8 %copy-start.9 = (f32[2240]{0:T(1024)S(1)}, f32[2240]{0:T(1024)}, u32[]{:S(2)}) copy-start(f32[2240]{0:T(1024)} %get-tuple-element.34) | copy-start | bytes 26884
  93.7 4.8 %copy-start.10 = (f32[2240]{0:T(1024)S(1)}, f32[2240]{0:T(1024)}, u32[]{:S(2)}) copy-start(f32[2240]{0:T(1024)} %get-tuple-element.35) | copy-start | bytes 26884
  93.7 4.8 %copy-start.11 = (f32[2240]{0:T(1024)S(1)}, f32[2240]{0:T(1024)}, u32[]{:S(2)}) copy-start(f32[2240]{0:T(1024)} %get-tuple-element.36) | copy-start | bytes 26884
  93.7 19.3 %all-to-all-start.1 = ((f32[16,144,113]{2,1,0:T(8,128)}), f32[16,144,113]{2,1,0:T(8,128)}, u32[]{:S(2)}, u32[]{:S(2)}) async-start(f32[16,144,113]{2,1,0:T(8,128)} %bitcast.27), calls=%async_computation.1 | async-start | bytes 2359296 | tf_op jit(solution)/shard_map/all_to_all | solution.py:118

commit v11 on v10

--- a/solution.py
+++ b/solution.py
@@ -8,7 +8,7 @@
 HD = 112
 
 
-def halo_rows(cells, width):
+def padded_pair(cells, width):
     count = lax.axis_size("space")
     ends = count - 1
     rows = cells.shape[2]
@@ -16,7 +16,7 @@
     tail = cells[:, :, rows - width :]
     above = lax.ppermute(tail, "space", [(i, (i + 1) % count) for i in range(ends)])
     below = lax.ppermute(head, "space", [((i + 1) % count, i) for i in range(ends)])
-    return above, below
+    return jnp.concatenate([above, cells, below], axis=2)
 
 
 ROWS = HEADS * HD
@@ -111,12 +111,11 @@
         gv_ref[:, cols] = (value_grad + c_ref[:, cols]).astype(jnp.bfloat16)
 
 
-def spread_states(packed, reverse, counts, tie=None):
+def spread_states(packed, reverse, counts):
     space = lax.axis_size("space")
     orbit = lax.axis_size("orbit")
     place = lax.axis_index("orbit")
     pieces = lax.all_to_all(packed.reshape(space, -1, WIDTH), "space", 0, 0, tiled=True)
-    pieces, tie = lax.optimization_barrier((pieces, tie))
     whole = jnp.sum(pieces, axis=0)
     views = jnp.arange(orbit)
     if not reverse:
@@ -129,7 +128,7 @@
         gathered = lax.all_gather(whole, "orbit")
         keep = views >= place
         summed = jnp.sum(jnp.where(keep[:, None, None], gathered, 0.0), axis=0)
-    return lax.all_gather(summed.astype(jnp.bfloat16), "space", tiled=True), tie
+    return lax.all_gather(summed.astype(jnp.bfloat16), "space", tiled=True)
 
 
 def on_device_body(queries, keys_in, values, conv_weight, grad_out):
@@ -152,11 +151,9 @@
     q_tiles, q_cross, g_tiles, k_tiles, v_tiles = pl.pallas_call(
         tile_kernel, out_shape=(tile,) * 5
     )(q2, g2, k2, v2)
-    cells = jnp.stack([values, grad_out])
-    halo = halo_rows(cells, 1)
-    state_b, (above, below) = spread_states(packed_part, False, count, halo)
-
-    pair = jnp.concatenate([above, cells, below], axis=2)
+    state_b = spread_states(packed_part, False, count)
+
+    pair = padded_pair(jnp.stack([values, grad_out]), 1)
     pair = jnp.pad(pair, ((0, 0), (0, 0), (0, 0), (1, 1), (0, 0)))
     value_pad, grad_pad = pair[0], pair[1]
     weight_wide = conv_weight.astype(f32)
@@ -183,7 +180,7 @@
             jax.ShapeDtypeStruct(flat_shape, bf),
         ),
     )(q_tiles, g_tiles, conv_flat, state_b)
-    back_state, _ = spread_states(state_grad, True, count)
+    back_state = spread_states(state_grad, True, count)
     grad_key, grad_value = pl.pallas_call(
         backward_kernel,
         out_shape=(

time: 164 us -> 162 us (0.988)
  waiting for transfers between devices: 14.2 us -> 10.6 us
  other arithmetic: 9.18 us -> 10.9 us
    ppermute x2, waiting for transfers between devices: 12.7 us -> 0.01 us  [the longest x1 0.01 us: padded_pair(): lax.ppermute(tail, 'space', [(i, (i + 1) % count) for i in range(ends)])]
    all_to_all x2, waiting for transfers between devices: 1.48 us -> 10.6 us  [spread_states(): lax.all_to_all(packed.reshape(space, -1, WIDTH), 'space', 0, 0, tiled=True)]
    all_to_all x2, starting transfers between devices: 10.2 us -> 13 us  [spread_states(): lax.all_to_all(packed.reshape(space, -1, WIDTH), 'space', 0, 0, tiled=True)]
    ppermute x2, starting transfers between devices: 5.88 us -> 3.1 us  [the longest x1 1.81 us: padded_pair(): lax.ppermute(tail, 'space', [(i, (i + 1) % count) for i in range(ends)])]
  transfers between devices with their start and end apart: 4 -> 4, of which waited for: 2 -> 2; matrix products, arithmetic and copies ran while one was open for 5% -> 5% of each run, Pallas kernels for 9% -> 11%
where the time goes in v11:
time: 162 us; the launch traced here: 160 us
  blocking collectives  92.6 us (57%)
  Pallas kernels  26.4 us (16%)
  starting transfers between devices  16.1 us (10%)
  other arithmetic  10.9 us (7%)
  waiting for transfers between devices  10.6 us (7%)
  local copies, waits for them, and re-layouts  2.04 us (1%)
    all_gather x2, blocking collectives, spread_states(): return lax.all_gather(summed.astype(jnp.bfloat16), 'space', tiled=True)  51 us
    all_gather x2, blocking collectives, spread_states(): gathered = lax.all_gather(whole, 'orbit')  41.6 us
    all_to_all x2, starting transfers between devices, spread_states(): lax.all_to_all(packed.reshape(space, -1, WIDTH), 'space', 0, 0, tiled=True)  13 us
    all_to_all x2, waiting for transfers between devices, spread_states(): lax.all_to_all(packed.reshape(space, -1, WIDTH), 'space', 0, 0, tiled=True)  10.6 us
    pallas_call x1, Pallas kernels, on_device_body(): pl.pallas_call(forward_kernel, out_shape=(jax.ShapeDtypeStruct(flat_shape...  8.91 us
    pallas_call x1, Pallas kernels, on_device_body(): pl.pallas_call(tile_kernel, out_shape=(tile,) * 5)(q2, g2, k2, v2)  5.04 us
    pallas_call x1, Pallas kernels, on_device_body(): pl.pallas_call(backward_kernel, out_shape=(jax.ShapeDtypeStruct(flat_shap...  4.75 us
    pallas_call x1, Pallas kernels, on_device_body(): pl.pallas_call(state_grad_kernel, out_shape=jax.ShapeDtypeStruct((PACKED,...  3.96 us
  transfers between devices with their start and end apart: 4, of which 2 were waited for; matrix products, arithmetic and copies ran while one was open for 5% of the time, Pallas kernels for 11%

profile of v11, /device:TPU:0, one launch (start us, length us, event | category | flops | bytes accessed | tf_op | source)
XLA Modules:
  0.0 159.6 jit_solution(11646857595114642607)
XLA Ops:
  0.6 1.3 fusion.4
  2.0 1.8 %collective-permute-start = (bf16[2,1,1,64,2240]{4,3,2,1,0:T(8,128)(2,1)S(1)}, bf16[2,1,1,64,2240]{4,3,2,1,0:T(8,128)(2,1)S(1)}, u32[]{:S(2)}, u32[]{:S(2)}) collective-permute-start(bf16[2,1,1,64,2240]{4,3,2,1,0:T(8,128)(2,1)S(1)} %get-tuple-element.33), channel_id=1, source_target_pairs={{0,1},{1,2},{2,3},{3,4},{4,5},{5,6},{6,7},{7,8},{8,9},{9,10},{10,1... | collective-permute-start | bytes 1720328 | tf_op jit(solution)/shard_map/ppermute | solution.py:17
  3.8 1.3 collective-permute-start.1
  5.1 3.7 %shard_map.85 = f32[2304,113]{1,0:T(8,128)} custom-call(bf16[128,2240]{1,0:T(8,128)(2,1)} %bitcast.33, bf16[128,2240]{1,0:T(8,128)(2,1)} %bitcast.21), custom_call_target="tpu_custom_call" | custom-call | tf_op jit(solution)/shard_map/pallas_call | solution.py:147
  8.8 0.0 copy-start.10
  8.8 8.2 %all-to-all-start = ((f32[16,144,113]{2,1,0:T(8,128)}), f32[16,144,113]{2,1,0:T(8,128)}, u32[]{:S(2)}, u32[]{:S(2)}) async-start(f32[16,144,113]{2,1,0:T(8,128)} %bitcast.28), calls=%async_computation | async-start | bytes 2359296 | tf_op jit(solution)/shard_map/all_to_all | solution.py:118
  17.1 0.0 copy-done.10
  17.1 0.7 convert_element_type.68
  17.7 0.0 copy-start
  17.7 5.0 %shard_map.84 = (bf16[20,128,128]{2,1,0:T(8,128)(2,1)}, bf16[20,128,128]{2,1,0:T(8,128)(2,1)}, bf16[20,128,128]{2,1,0:T(8,128)(2,1)}, bf16[20,128,128]{2,1,0:T(8,128)(2,1)}, bf16[20,128,128]{2,1,0:T(8,128)(2,1)}) custom-call(bf16[128,2240]{1,0:T(8,128)(2,1)} %bitcast.35, bf16[128,2240]{1,0:T(8,128)(2,1)} %bitcast.25, bf16[128,2240]{1,0:T(8,128)(2,1)} %bitcast.34, ...), custom_call_target="tpu_custom_call" | custom-call | tf_op jit(solution)/shard_map/pallas_call | solution.py:151
  22.8 0.6 iota_compare_fusion.3
  23.4 1.8 %slice_reduce_fusion.8 = (f32[2240]{0:T(1024)S(1)}, f32[2240]{0:T(1024)}, f32[2240]{0:T(1024)}, f32[2240]{0:T(1024)}, f32[2240]{0:T(1024)}, /*index=5*/f32[2240]...) fusion(f32[3,3,2240]{2,1,0:T(4,128)} %convert_element_type.68), kind=kLoop, calls=%fused_computation.28 | loop fusion | bytes 161280 | tf_op jit(solution)/shard_map/slice | solution.py:164
  25.2 0.0 collective-permute-done
  25.2 0.0 collective-permute-done.1
  25.2 0.0 copy-done
  25.2 0.0 copy-done.1
  25.2 1.1 select_maximum_fusion
  26.3 0.2 slice_bitcast_fusion
  26.5 0.0 copy-start.11
  26.5 9.2 %all-to-all-done = f32[16,144,113]{2,1,0:T(8,128)} async-done(((f32[16,144,113]{2,1,0:T(8,128)}), f32[16,144,113]{2,1,0:T(8,128)}, u32[]{:S(2)}, u32[]{:S(2)}) %all-to-all-start) | async-done | bytes 1041440 | tf_op jit(solution)/shard_map/all_to_all | solution.py:118
  35.7 1.4 reduce_sum.36
  37.1 23.3 %all-gather = f32[2304,113]{1,0:T(8,128)S(1)} all-gather(f32[144,113]{1,0:T(8,128)S(1)} %reduce_sum.36), channel_id=2, replica_groups=mesh['orbit'=16,'space'=16] {'orbit'}, dimensions={0}, use_global_device_ids=true | all-gather | bytes 1106496 | tf_op jit(solution)/shard_map/all_gather | solution.py:122
  60.4 0.0 copy-done.11
  60.4 0.2 select_reduce_fusion.1
  60.6 25.9 %all_gather.18.s_ref = bf16[2304,113]{1,0:T(8,128)(2,1)} all-gather(bf16[144,113]{1,0:T(8,128)(2,1)S(1)} %divide_convert_fusion), channel_id=1, replica_groups=mesh['orbit'=16,'space'=16] {'space'}, dimensions={0}, use_global_device_ids=true | all-gather | bytes 553248 | tf_op jit(solution)/shard_map/all_gather | solution.py:131
  86.5 4.0 %shard_map.87 = f32[2304,113]{1,0:T(8,128)} custom-call(bf16[20,128,128]{2,1,0:T(8,128)(2,1)} %get-tuple-element.13.qt_ref, bf16[20,128,128]{2,1,0:T(8,128)(2,1)} %get-tuple-element.19.qx_ref, bf16[20,128,128]{2,1,0:T(8,128)(2,1)} %get-tuple-element.14.gt_ref, bf16[2304,113]{1,0:T(8,128)(2,1)} %all_gather.18.s_ref), custom_call_target="tpu_custom_call" | custom-call | tf_op jit(solution)/shard_map/pallas_call | solution.py:172
  90.4 0.0 copy-start.6
  90.4 0.0 copy-start.7
  90.5 0.0 copy-start.8
  90.5 0.0 copy-start.9
  90.5 4.8 %all-to-all-start.1 = ((f32[16,144,113]{2,1,0:T(8,128)}), f32[16,144,113]{2,1,0:T(8,128)}, u32[]{:S(2)}, u32[]{:S(2)}) async-start(f32[16,144,113]{2,1,0:T(8,128)} %bitcast.27), calls=%async_computation.1 | async-start | bytes 2359296 | tf_op jit(solution)/shard_map/all_to_all | solution.py:118
  95.2 0.0 copy-done.2
  95.3 0.0 copy-done.3
  95.3 0.0 copy-done.4
  95.3 0.0 copy-done.5
  95.3 0.0 copy-done.6
  95.3 0.0 copy-done.7
  95.3 0.0 copy-done.8
  95.3 0.0 copy-done.9
  95.3 2.1 %multiply_add_fusion = f32[1,2,64,2240]{3,2,1,0:T(8,128)} fusion(bf16[1,4,66,2240]{3,2,1,0:T(8,128)(2,1)S(1)} %get-tuple-element.31, f32[2240]{0:T(1024)S(1)} %copy-done.2, f32[2240]{0:T(1024)S(1)} %copy-done.3, f32[2240]{0:T(1024)S(1)} %copy-done.4, f32[2240]{0:T(1024)S(1)} %copy-done.5, f32[2240]{0:T(1024)S(1)} %copy-done.6, f32[2240]{0:T(1024)S(1)} %copy-done.7, ...), kind=kLoop, calls=%fused_computation.13 | loop fusion | flops 7454720 | bytes 6388480 | tf_op jit(solution)/shard_map/add | solution.py:167
  97.4 2.0 %multiply_add_fusion.1 = f32[1,2,64,2240]{3,2,1,0:T(8,128)} fusion(bf16[1,4,66,2240]{3,2,1,0:T(8,128)(2,1)S(1)} %get-tuple-element.32, f32[2240]{0:T(1024)S(1)} %copy-done.2, f32[2240]{0:T(1024)S(1)} %copy-done.3, f32[2240]{0:T(1024)S(1)} %copy-done.4, f32[2240]{0:T(1024)S(1)} %copy-done.5, f32[2240]{0:T(1024)S(1)} %copy-done.6, f32[2240]{0:T(1024)S(1)} %copy-done.7, ...), kind=kLoop, calls=%fused_computation.15 | loop fusion | flops 7454720 | bytes 6388480 | tf_op jit(solution)/shard_map/add | solution.py:164
  99.4 8.9 %shard_map.86 = (bf16[128,2240]{1,0:T(8,128)(2,1)}, bf16[128,2240]{1,0:T(8,128)(2,1)}) custom-call(bf16[20,128,128]{2,1,0:T(8,128)(2,1)} %get-tuple-element.13.qt_ref, bf16[20,128,128]{2,1,0:T(8,128)(2,1)} %get-tuple-element.14.gt_ref, f32[128,2240]{1,0:T(8,128)} %bitcast.30, bf16[2304,113]{1,0:T(8,128)(2,1)} %all_gather.18.s_ref), custom_call_target="tpu_custom_call" | custom-call | tf_op jit(solution)/shard_map/pallas_call | solution.py:176
  108.3 1.4 all-to-all-done.1
  109.8 1.4 reduce_sum.38
  111.2 18.3 %all-gather.1 = f32[2304,113]{1,0:T(8,128)S(1)} all-gather(f32[144,113]{1,0:T(8,128)S(1)} %broadcast_divide_fusion), channel_id=3, replica_groups=mesh['orbit'=16,'space'=16] {'orbit'}, dimensions={0}, use_global_device_ids=true | all-gather | bytes 1106496 | tf_op jit(solution)/shard_map/all_gather | solution.py:128
  129.5 0.2 select_reduce_fusion
  129.7 25.2 %all_gather.20.s_ref = bf16[2304,113]{1,0:T(8,128)(2,1)} all-gather(bf16[144,113]{1,0:T(8,128)(2,1)S(1)} %select_reduce_fusion), channel_id=1, replica_groups=mesh['orbit'=16,'space'=16] {'space'}, dimensions={0}, use_global_device_ids=true | all-gather | bytes 553248 | tf_op jit(solution)/shard_map/all_gather | solution.py:131
  154.8 4.8 %shard_map.88 = (bf16[128,2240]{1,0:T(8,128)(2,1)}, bf16[128,2240]{1,0:T(8,128)(2,1)}) custom-call(bf16[20,128,128]{2,1,0:T(8,128)(2,1)} %get-tuple-element.17.kt_ref, bf16[20,128,128]{2,1,0:T(8,128)(2,1)} %get-tuple-element.18.vt_ref, f32[128,2240]{1,0:T(8,128)} %bitcast.29, bf16[2304,113]{1,0:T(8,128)(2,1)} %all_gather.20.s_ref), custom_call_target="tpu_custom_call" | custom-call | tf_op jit(solution)/shard_map/pallas_call | solution.py:184
  (8 shorter events, 0.0 us)
Async XLA Ops:
  2.0 23.2 %collective-permute-start = (bf16[2,1,1,64,2240]{4,3,2,1,0:T(8,128)(2,1)S(1)}, bf16[2,1,1,64,2240]{4,3,2,1,0:T(8,128)(2,1)S(1)}, u32[]{:S(2)}, u32[]{:S(2)}) collective-permute-start(bf16[2,1,1,64,2240]{4,3,2,1,0:T(8,128)(2,1)S(1)} %get-tuple-element.33), channel_id=1, source_target_pairs={{0,1},{1,2},{2,3},{3,4},{4,5},{5,6},{6,7},{7,8},{8,9},{9,10},{10,1... | collective-permute-start | bytes 1720328 | tf_op jit(solution)/shard_map/ppermute | solution.py:17
  3.8 21.4 %collective-permute-start.1 = (bf16[2,1,1,64,2240]{4,3,2,1,0:T(8,128)(2,1)S(1)}, bf16[2,1,1,64,2240]{4,3,2,1,0:T(8,128)(2,1)S(1)}, u32[]{:S(2)}, u32[]{:S(2)}) collective-permute-start(bf16[2,1,1,64,2240]{4,3,2,1,0:T(8,128)(2,1)S(1)} %get-tuple-element.34), channel_id=1, source_target_pairs={{1,0},{2,1},{3,2},{4,3},{5,4},{6,5},{7,6},{8,7},{9,8},{10,9},{11,1... | collective-permute-start | bytes 1720328 | tf_op jit(solution)/shard_map/ppermute | solution.py:18
  8.8 8.3 %copy-start.10 = (bf16[3,3,2240]{2,1,0:T(4,128)(2,1)S(1)}, bf16[3,3,2240]{2,1,0:T(4,128)(2,1)}, u32[]{:S(2)}) copy-start(bf16[3,3,2240]{2,1,0:T(4,128)(2,1)} %param.8) | copy-start | bytes 120964
  8.8 26.9 %all-to-all-start = ((f32[16,144,113]{2,1,0:T(8,128)}), f32[16,144,113]{2,1,0:T(8,128)}, u32[]{:S(2)}, u32[]{:S(2)}) async-start(f32[16,144,113]{2,1,0:T(8,128)} %bitcast.28), calls=%async_computation | async-start | bytes 2359296 | tf_op jit(solution)/shard_map/all_to_all | solution.py:118
  17.7 7.5 %copy-start = (bf16[1,2,64,2240]{3,2,1,0:T(8,128)(2,1)S(1)}, bf16[1,2,64,2240]{3,2,1,0:T(8,128)(2,1)}, u32[]{:S(2)}) copy-start(bf16[1,2,64,2240]{3,2,1,0:T(8,128)(2,1)} %param.7) | copy-start | bytes 1720324
  17.7 7.5 %copy-start.1 = (bf16[1,2,64,2240]{3,2,1,0:T(8,128)(2,1)S(1)}, bf16[1,2,64,2240]{3,2,1,0:T(8,128)(2,1)}, u32[]{:S(2)}) copy-start(bf16[1,2,64,2240]{3,2,1,0:T(8,128)(2,1)} %param.9) | copy-start | bytes 1720324
  26.5 33.9 %copy-start.11 = (pred[16]{0:T(512)(128)(4,1)S(1)}, pred[16]{0:T(512)(128)(4,1)}, u32[]{:S(2)}) copy-start(pred[16]{0:T(512)(128)(4,1)} %iota_compare_fusion.3) | copy-start | bytes 52
  90.4 4.8 %copy-start.2 = (f32[2240]{0:T(1024)S(1)}, f32[2240]{0:T(1024)}, u32[]{:S(2)}) copy-start(f32[2240]{0:T(1024)} %get-tuple-element.23) | copy-start | bytes 26884
  90.4 4.8 %copy-start.3 = (f32[2240]{0:T(1024)S(1)}, f32[2240]{0:T(1024)}, u32[]{:S(2)}) copy-start(f32[2240]{0:T(1024)} %get-tuple-element.24) | copy-start | bytes 26884
  90.4 4.8 %copy-start.4 = (f32[2240]{0:T(1024)S(1)}, f32[2240]{0:T(1024)}, u32[]{:S(2)}) copy-start(f32[2240]{0:T(1024)} %get-tuple-element.25) | copy-start | bytes 26884
  90.4 4.8 %copy-start.5 = (f32[2240]{0:T(1024)S(1)}, f32[2240]{0:T(1024)}, u32[]{:S(2)}) copy-start(f32[2240]{0:T(1024)} %get-tuple-element.26) | copy-start | bytes 26884
  90.4 4.8 %copy-start.6 = (f32[2240]{0:T(1024)S(1)}, f32[2240]{0:T(1024)}, u32[]{:S(2)}) copy-start(f32[2240]{0:T(1024)} %get-tuple-element.27) | copy-start | bytes 26884
  90.4 4.8 %copy-start.7 = (f32[2240]{0:T(1024)S(1)}, f32[2240]{0:T(1024)}, u32[]{:S(2)}) copy-start(f32[2240]{0:T(1024)} %get-tuple-element.28) | copy-start | bytes 26884
  90.5 4.8 %copy-start.8 = (f32[2240]{0:T(1024)S(1)}, f32[2240]{0:T(1024)}, u32[]{:S(2)}) copy-start(f32[2240]{0:T(1024)} %get-tuple-element.29) | copy-start | bytes 26884
  90.5 4.8 %copy-start.9 = (f32[2240]{0:T(1024)S(1)}, f32[2240]{0:T(1024)}, u32[]{:S(2)}) copy-start(f32[2240]{0:T(1024)} %get-tuple-element.30) | copy-start | bytes 26884
  90.5 19.3 %all-to-all-start.1 = ((f32[16,144,113]{2,1,0:T(8,128)}), f32[16,144,113]{2,1,0:T(8,128)}, u32[]{:S(2)}, u32[]{:S(2)}) async-start(f32[16,144,113]{2,1,0:T(8,128)} %bitcast.27), calls=%async_computation.1 | async-start | bytes 2359296 | tf_op jit(solution)/shard_map/all_to_all | solution.py:118

commit v12 on v11

--- a/solution.py
+++ b/solution.py
@@ -43,7 +43,7 @@
         )
 
 
-def tile_kernel(q_ref, g_ref, k_ref, v_ref, qt_ref, qx_ref, gt_ref, kt_ref, vt_ref):
+def tile_kernel(q_ref, g_ref, k_ref, v_ref, qt_ref, gt_ref, kt_ref, vt_ref):
     tokens = q_ref.shape[0]
     zero = jnp.zeros((tokens, LANES - HD), jnp.bfloat16)
     extra = lane_one(tokens)
@@ -51,13 +51,12 @@
         cols = slice(h * HD, (h + 1) * HD)
         qf = jnp.concatenate([jnp.maximum(q_ref[:, cols], 0), zero], axis=1)
         qt_ref[h] = qf
-        qx_ref[h] = qf.T
         gt_ref[h] = jnp.concatenate([g_ref[:, cols], zero], axis=1)
         kt_ref[h] = jnp.concatenate([jnp.maximum(k_ref[:, cols], 0), zero], axis=1)
         vt_ref[h] = jnp.concatenate([v_ref[:, cols], extra], axis=1)
 
 
-def state_grad_kernel(qt_ref, qx_ref, gt_ref, s_ref, sg_ref):
+def state_grad_kernel(qt_ref, gt_ref, s_ref, sg_ref):
     sg_ref[ROWS:, :] = jnp.zeros((PACKED - ROWS, WIDTH), jnp.float32)
     lanes = lax.broadcasted_iota(jnp.int32, (qt_ref.shape[1], WIDTH), 1)
     for h in range(HEADS):
@@ -71,7 +70,9 @@
             -jnp.sum(gw * wide, axis=1, keepdims=True) / (denominator * denominator)
         ).astype(jnp.bfloat16)
         grads = jnp.where(lanes == NORM, den_grad, num_grad)
-        sg = jnp.dot(qx_ref[h], grads, preferred_element_type=jnp.float32)
+        sg = lax.dot_general(
+            qt_ref[h], grads, (((0,), (0,)), ((), ())), preferred_element_type=jnp.float32
+        )
         sg_ref[h * HD : (h + 1) * HD, :] = sg[:HD]
 
 
@@ -148,8 +149,8 @@
         part_kernel, out_shape=jax.ShapeDtypeStruct((PACKED, WIDTH), f32)
     )(k2, v2)
     tile = jax.ShapeDtypeStruct((HEADS, token_count, LANES), jnp.bfloat16)
-    q_tiles, q_cross, g_tiles, k_tiles, v_tiles = pl.pallas_call(
-        tile_kernel, out_shape=(tile,) * 5
+    q_tiles, g_tiles, k_tiles, v_tiles = pl.pallas_call(
+        tile_kernel, out_shape=(tile,) * 4
     )(q2, g2, k2, v2)
     state_b = spread_states(packed_part, False, count)
 
@@ -171,7 +172,7 @@
     bf = jnp.bfloat16
     state_grad = pl.pallas_call(
         state_grad_kernel, out_shape=jax.ShapeDtypeStruct((PACKED, WIDTH), f32)
-    )(q_tiles, q_cross, g_tiles, state_b)
+    )(q_tiles, g_tiles, state_b)
     conv_flat = conv_term.reshape(flat_shape)
     attended, grad_query = pl.pallas_call(
         forward_kernel,

time: 162 us -> 161 us (level)
  transfers between devices with their start and end apart: 4 -> 4, of which waited for: 2 -> 3; matrix products, arithmetic and copies ran while one was open for 5% -> 5% of each run, Pallas kernels for 11% -> 11%
where the time goes in v12:
time: 161 us; the launch traced here: 159 us
  blocking collectives  92.6 us (58%)
  Pallas kernels  25.6 us (16%)
  starting transfers between devices  16.1 us (10%)
  waiting for transfers between devices  11.4 us (7%)
  other arithmetic  10.8 us (7%)
  local copies, waits for them, and re-layouts  2.04 us (1%)
    all_gather x2, blocking collectives, spread_states(): return lax.all_gather(summed.astype(jnp.bfloat16), 'space', tiled=True)  51 us
    all_gather x2, blocking collectives, spread_states(): gathered = lax.all_gather(whole, 'orbit')  41.6 us
    all_to_all x2, starting transfers between devices, spread_states(): lax.all_to_all(packed.reshape(space, -1, WIDTH), 'space', 0, 0, tiled=True)  13 us
    all_to_all x2, waiting for transfers between devices, spread_states(): lax.all_to_all(packed.reshape(space, -1, WIDTH), 'space', 0, 0, tiled=True)  10.7 us
    pallas_call x1, Pallas kernels, on_device_body(): pl.pallas_call(forward_kernel, out_shape=(jax.ShapeDtypeStruct(flat_shape...  8.91 us
    pallas_call x1, Pallas kernels, on_device_body(): pl.pallas_call(backward_kernel, out_shape=(jax.ShapeDtypeStruct(flat_shap...  4.75 us
    pallas_call x1, Pallas kernels, on_device_body(): pl.pallas_call(tile_kernel, out_shape=(tile,) * 4)(q2, g2, k2, v2)  4.32 us
    pallas_call x1, Pallas kernels, on_device_body(): pl.pallas_call(state_grad_kernel, out_shape=jax.ShapeDtypeStruct((PACKED,...  3.88 us
  transfers between devices with their start and end apart: 4, of which 3 were waited for; matrix products, arithmetic and copies ran while one was open for 5% of the time, Pallas kernels for 11%

profile of v12, /device:TPU:0, one launch (start us, length us, event | category | flops | bytes accessed | tf_op | source)
XLA Modules:
  0.0 159.5 jit_solution(197420344704242519)
XLA Ops:
  0.6 1.3 fusion.4
  2.0 1.8 %collective-permute-start = (bf16[2,1,1,64,2240]{4,3,2,1,0:T(8,128)(2,1)S(1)}, bf16[2,1,1,64,2240]{4,3,2,1,0:T(8,128)(2,1)S(1)}, u32[]{:S(2)}, u32[]{:S(2)}) collective-permute-start(bf16[2,1,1,64,2240]{4,3,2,1,0:T(8,128)(2,1)S(1)} %get-tuple-element.31), channel_id=1, source_target_pairs={{0,1},{1,2},{2,3},{3,4},{4,5},{5,6},{6,7},{7,8},{8,9},{9,10},{10,1... | collective-permute-start | bytes 1720328 | tf_op jit(solution)/shard_map/ppermute | solution.py:17
  3.8 1.3 collective-permute-start.1
  5.1 3.7 %shard_map.85 = f32[2304,113]{1,0:T(8,128)} custom-call(bf16[128,2240]{1,0:T(8,128)(2,1)} %bitcast.33, bf16[128,2240]{1,0:T(8,128)(2,1)} %bitcast.21), custom_call_target="tpu_custom_call" | custom-call | tf_op jit(solution)/shard_map/pallas_call | solution.py:148
  8.8 0.0 copy-start.10
  8.8 8.2 %all-to-all-start = ((f32[16,144,113]{2,1,0:T(8,128)}), f32[16,144,113]{2,1,0:T(8,128)}, u32[]{:S(2)}, u32[]{:S(2)}) async-start(f32[16,144,113]{2,1,0:T(8,128)} %bitcast.28), calls=%async_computation | async-start | bytes 2359296 | tf_op jit(solution)/shard_map/all_to_all | solution.py:119
  17.1 0.0 copy-done.10
  17.1 0.7 convert_element_type.68
  17.7 0.0 copy-start
  17.7 4.3 %shard_map.84 = (bf16[20,128,128]{2,1,0:T(8,128)(2,1)}, bf16[20,128,128]{2,1,0:T(8,128)(2,1)}, bf16[20,128,128]{2,1,0:T(8,128)(2,1)}, bf16[20,128,128]{2,1,0:T(8,128)(2,1)}) custom-call(bf16[128,2240]{1,0:T(8,128)(2,1)} %bitcast.35, bf16[128,2240]{1,0:T(8,128)(2,1)} %bitcast.25, bf16[128,2240]{1,0:T(8,128)(2,1)} %bitcast.34, bf16[128,2240]{1,0:T(8,128)(2,1)} %bitcast.22), custom_call_target="tpu_custom_call" | custom-call | tf_op jit(solution)/shard_map/pallas_call | solution.py:152
  22.1 0.5 iota_compare_fusion.3
  22.6 1.8 %slice_reduce_fusion.8 = (f32[2240]{0:T(1024)S(1)}, f32[2240]{0:T(1024)}, f32[2240]{0:T(1024)}, f32[2240]{0:T(1024)}, f32[2240]{0:T(1024)}, /*index=5*/f32[2240]...) fusion(f32[3,3,2240]{2,1,0:T(4,128)} %convert_element_type.68), kind=kLoop, calls=%fused_computation.28 | loop fusion | bytes 161280 | tf_op jit(solution)/shard_map/slice | solution.py:165
  24.4 0.0 collective-permute-done
  24.4 0.8 collective-permute-done.1
  25.2 0.0 copy-done
  25.2 0.0 copy-done.1
  25.2 1.1 select_maximum_fusion
  26.3 0.2 slice_bitcast_fusion
  26.4 0.0 copy-start.11
  26.5 9.2 %all-to-all-done = f32[16,144,113]{2,1,0:T(8,128)} async-done(((f32[16,144,113]{2,1,0:T(8,128)}), f32[16,144,113]{2,1,0:T(8,128)}, u32[]{:S(2)}, u32[]{:S(2)}) %all-to-all-start) | async-done | bytes 1041440 | tf_op jit(solution)/shard_map/all_to_all | solution.py:119
  35.7 1.4 reduce_sum.36
  37.1 23.3 %all-gather = f32[2304,113]{1,0:T(8,128)S(1)} all-gather(f32[144,113]{1,0:T(8,128)S(1)} %reduce_sum.36), channel_id=2, replica_groups=mesh['orbit'=16,'space'=16] {'orbit'}, dimensions={0}, use_global_device_ids=true | all-gather | bytes 1106496 | tf_op jit(solution)/shard_map/all_gather | solution.py:123
  60.4 0.0 copy-done.11
  60.4 0.2 select_reduce_fusion.1
  60.6 25.9 %all_gather.18.s_ref = bf16[2304,113]{1,0:T(8,128)(2,1)} all-gather(bf16[144,113]{1,0:T(8,128)(2,1)S(1)} %divide_convert_fusion), channel_id=1, replica_groups=mesh['orbit'=16,'space'=16] {'space'}, dimensions={0}, use_global_device_ids=true | all-gather | bytes 553248 | tf_op jit(solution)/shard_map/all_gather | solution.py:132
  86.5 3.9 %shard_map.87 = f32[2304,113]{1,0:T(8,128)} custom-call(bf16[20,128,128]{2,1,0:T(8,128)(2,1)} %get-tuple-element.12.qt_ref, bf16[20,128,128]{2,1,0:T(8,128)(2,1)} %get-tuple-element.13.gt_ref, bf16[2304,113]{1,0:T(8,128)(2,1)} %all_gather.18.s_ref), custom_call_target="tpu_custom_call" | custom-call | tf_op jit(solution)/shard_map/pallas_call | solution.py:173
  90.4 0.0 copy-start.6
  90.4 0.0 copy-start.7
  90.4 0.0 copy-start.8
  90.4 0.0 copy-start.9
  90.4 4.8 %all-to-all-start.1 = ((f32[16,144,113]{2,1,0:T(8,128)}), f32[16,144,113]{2,1,0:T(8,128)}, u32[]{:S(2)}, u32[]{:S(2)}) async-start(f32[16,144,113]{2,1,0:T(8,128)} %bitcast.27), calls=%async_computation.1 | async-start | bytes 2359296 | tf_op jit(solution)/shard_map/all_to_all | solution.py:119
  95.2 0.0 copy-done.2
  95.2 0.0 copy-done.3
  95.2 0.0 copy-done.4
  95.2 0.0 copy-done.5
  95.2 0.0 copy-done.6
  95.2 0.0 copy-done.7
  95.2 0.0 copy-done.8
  95.2 0.0 copy-done.9
  95.2 2.1 %multiply_add_fusion = f32[1,2,64,2240]{3,2,1,0:T(8,128)} fusion(bf16[1,4,66,2240]{3,2,1,0:T(8,128)(2,1)S(1)} %get-tuple-element.29, f32[2240]{0:T(1024)S(1)} %copy-done.2, f32[2240]{0:T(1024)S(1)} %copy-done.3, f32[2240]{0:T(1024)S(1)} %copy-done.4, f32[2240]{0:T(1024)S(1)} %copy-done.5, f32[2240]{0:T(1024)S(1)} %copy-done.6, f32[2240]{0:T(1024)S(1)} %copy-done.7, ...), kind=kLoop, calls=%fused_computation.13 | loop fusion | flops 7454720 | bytes 6388480 | tf_op jit(solution)/shard_map/add | solution.py:168
  97.3 2.0 %multiply_add_fusion.1 = f32[1,2,64,2240]{3,2,1,0:T(8,128)} fusion(bf16[1,4,66,2240]{3,2,1,0:T(8,128)(2,1)S(1)} %get-tuple-element.30, f32[2240]{0:T(1024)S(1)} %copy-done.2, f32[2240]{0:T(1024)S(1)} %copy-done.3, f32[2240]{0:T(1024)S(1)} %copy-done.4, f32[2240]{0:T(1024)S(1)} %copy-done.5, f32[2240]{0:T(1024)S(1)} %copy-done.6, f32[2240]{0:T(1024)S(1)} %copy-done.7, ...), kind=kLoop, calls=%fused_computation.15 | loop fusion | flops 7454720 | bytes 6388480 | tf_op jit(solution)/shard_map/add | solution.py:165
  99.4 8.9 %shard_map.86 = (bf16[128,2240]{1,0:T(8,128)(2,1)}, bf16[128,2240]{1,0:T(8,128)(2,1)}) custom-call(bf16[20,128,128]{2,1,0:T(8,128)(2,1)} %get-tuple-element.12.qt_ref, bf16[20,128,128]{2,1,0:T(8,128)(2,1)} %get-tuple-element.13.gt_ref, f32[128,2240]{1,0:T(8,128)} %bitcast.30, bf16[2304,113]{1,0:T(8,128)(2,1)} %all_gather.18.s_ref), custom_call_target="tpu_custom_call" | custom-call | tf_op jit(solution)/shard_map/pallas_call | solution.py:177
  108.3 1.4 all-to-all-done.1
  109.7 1.4 reduce_sum.38
  111.1 18.3 %all-gather.1 = f32[2304,113]{1,0:T(8,128)S(1)} all-gather(f32[144,113]{1,0:T(8,128)S(1)} %broadcast_divide_fusion), channel_id=3, replica_groups=mesh['orbit'=16,'space'=16] {'orbit'}, dimensions={0}, use_global_device_ids=true | all-gather | bytes 1106496 | tf_op jit(solution)/shard_map/all_gather | solution.py:129
  129.4 0.2 select_reduce_fusion
  129.6 25.1 %all_gather.20.s_ref = bf16[2304,113]{1,0:T(8,128)(2,1)} all-gather(bf16[144,113]{1,0:T(8,128)(2,1)S(1)} %select_reduce_fusion), channel_id=1, replica_groups=mesh['orbit'=16,'space'=16] {'space'}, dimensions={0}, use_global_device_ids=true | all-gather | bytes 553248 | tf_op jit(solution)/shard_map/all_gather | solution.py:132
  154.7 4.8 %shard_map.88 = (bf16[128,2240]{1,0:T(8,128)(2,1)}, bf16[128,2240]{1,0:T(8,128)(2,1)}) custom-call(bf16[20,128,128]{2,1,0:T(8,128)(2,1)} %get-tuple-element.16.kt_ref, bf16[20,128,128]{2,1,0:T(8,128)(2,1)} %get-tuple-element.17.vt_ref, f32[128,2240]{1,0:T(8,128)} %bitcast.29, bf16[2304,113]{1,0:T(8,128)(2,1)} %all_gather.20.s_ref), custom_call_target="tpu_custom_call" | custom-call | tf_op jit(solution)/shard_map/pallas_call | solution.py:185
  (8 shorter events, 0.0 us)
Async XLA Ops:
  2.0 22.4 %collective-permute-start = (bf16[2,1,1,64,2240]{4,3,2,1,0:T(8,128)(2,1)S(1)}, bf16[2,1,1,64,2240]{4,3,2,1,0:T(8,128)(2,1)S(1)}, u32[]{:S(2)}, u32[]{:S(2)}) collective-permute-start(bf16[2,1,1,64,2240]{4,3,2,1,0:T(8,128)(2,1)S(1)} %get-tuple-element.31), channel_id=1, source_target_pairs={{0,1},{1,2},{2,3},{3,4},{4,5},{5,6},{6,7},{7,8},{8,9},{9,10},{10,1... | collective-permute-start | bytes 1720328 | tf_op jit(solution)/shard_map/ppermute | solution.py:17
  3.8 21.4 %collective-permute-start.1 = (bf16[2,1,1,64,2240]{4,3,2,1,0:T(8,128)(2,1)S(1)}, bf16[2,1,1,64,2240]{4,3,2,1,0:T(8,128)(2,1)S(1)}, u32[]{:S(2)}, u32[]{:S(2)}) collective-permute-start(bf16[2,1,1,64,2240]{4,3,2,1,0:T(8,128)(2,1)S(1)} %get-tuple-element.32), channel_id=1, source_target_pairs={{1,0},{2,1},{3,2},{4,3},{5,4},{6,5},{7,6},{8,7},{9,8},{10,9},{11,1... | collective-permute-start | bytes 1720328 | tf_op jit(solution)/shard_map/ppermute | solution.py:18
  8.8 8.3 %copy-start.10 = (bf16[3,3,2240]{2,1,0:T(4,128)(2,1)S(1)}, bf16[3,3,2240]{2,1,0:T(4,128)(2,1)}, u32[]{:S(2)}) copy-start(bf16[3,3,2240]{2,1,0:T(4,128)(2,1)} %param.8) | copy-start | bytes 120964
  8.8 26.9 %all-to-all-start = ((f32[16,144,113]{2,1,0:T(8,128)}), f32[16,144,113]{2,1,0:T(8,128)}, u32[]{:S(2)}, u32[]{:S(2)}) async-start(f32[16,144,113]{2,1,0:T(8,128)} %bitcast.28), calls=%async_computation | async-start | bytes 2359296 | tf_op jit(solution)/shard_map/all_to_all | solution.py:119
  17.7 7.4 %copy-start = (bf16[1,2,64,2240]{3,2,1,0:T(8,128)(2,1)S(1)}, bf16[1,2,64,2240]{3,2,1,0:T(8,128)(2,1)}, u32[]{:S(2)}) copy-start(bf16[1,2,64,2240]{3,2,1,0:T(8,128)(2,1)} %param.7) | copy-start | bytes 1720324
  17.7 7.4 %copy-start.1 = (bf16[1,2,64,2240]{3,2,1,0:T(8,128)(2,1)S(1)}, bf16[1,2,64,2240]{3,2,1,0:T(8,128)(2,1)}, u32[]{:S(2)}) copy-start(bf16[1,2,64,2240]{3,2,1,0:T(8,128)(2,1)} %param.9) | copy-start | bytes 1720324
  26.4 33.9 %copy-start.11 = (pred[16]{0:T(512)(128)(4,1)S(1)}, pred[16]{0:T(512)(128)(4,1)}, u32[]{:S(2)}) copy-start(pred[16]{0:T(512)(128)(4,1)} %iota_compare_fusion.3) | copy-start | bytes 52
  90.3 4.8 %copy-start.2 = (f32[2240]{0:T(1024)S(1)}, f32[2240]{0:T(1024)}, u32[]{:S(2)}) copy-start(f32[2240]{0:T(1024)} %get-tuple-element.21) | copy-start | bytes 26884
  90.3 4.8 %copy-start.3 = (f32[2240]{0:T(1024)S(1)}, f32[2240]{0:T(1024)}, u32[]{:S(2)}) copy-start(f32[2240]{0:T(1024)} %get-tuple-element.22) | copy-start | bytes 26884
  90.4 4.8 %copy-start.4 = (f32[2240]{0:T(1024)S(1)}, f32[2240]{0:T(1024)}, u32[]{:S(2)}) copy-start(f32[2240]{0:T(1024)} %get-tuple-element.23) | copy-start | bytes 26884
  90.4 4.8 %copy-start.5 = (f32[2240]{0:T(1024)S(1)}, f32[2240]{0:T(1024)}, u32[]{:S(2)}) copy-start(f32[2240]{0:T(1024)} %get-tuple-element.24) | copy-start | bytes 26884
  90.4 4.8 %copy-start.6 = (f32[2240]{0:T(1024)S(1)}, f32[2240]{0:T(1024)}, u32[]{:S(2)}) copy-start(f32[2240]{0:T(1024)} %get-tuple-element.25) | copy-start | bytes 26884
  90.4 4.8 %copy-start.7 = (f32[2240]{0:T(1024)S(1)}, f32[2240]{0:T(1024)}, u32[]{:S(2)}) copy-start(f32[2240]{0:T(1024)} %get-tuple-element.26) | copy-start | bytes 26884
  90.4 4.8 %copy-start.8 = (f32[2240]{0:T(1024)S(1)}, f32[2240]{0:T(1024)}, u32[]{:S(2)}) copy-start(f32[2240]{0:T(1024)} %get-tuple-element.27) | copy-start | bytes 26884
  90.4 4.8 %copy-start.9 = (f32[2240]{0:T(1024)S(1)}, f32[2240]{0:T(1024)}, u32[]{:S(2)}) copy-start(f32[2240]{0:T(1024)} %get-tuple-element.28) | copy-start | bytes 26884
  90.4 19.3 %all-to-all-start.1 = ((f32[16,144,113]{2,1,0:T(8,128)}), f32[16,144,113]{2,1,0:T(8,128)}, u32[]{:S(2)}, u32[]{:S(2)}) async-start(f32[16,144,113]{2,1,0:T(8,128)} %bitcast.27), calls=%async_computation.1 | async-start | bytes 2359296 | tf_op jit(solution)/shard_map/all_to_all | solution.py:119

commit v13 on v12

--- a/solution.py
+++ b/solution.py
@@ -108,8 +108,8 @@
         )
         gk_ref[:, cols] = jnp.where(kf[:, :HD] > 0, key_grad, 0.0).astype(jnp.bfloat16)
         state = s_ref[h * HD : h * HD + LANES, :]
-        value_grad = jnp.dot(kf, state, preferred_element_type=jnp.float32)[:, :HD]
-        gv_ref[:, cols] = (value_grad + c_ref[:, cols]).astype(jnp.bfloat16)
+        value_grad = jnp.dot(kf, state, preferred_element_type=jnp.float32) + c_ref[h]
+        gv_ref[:, cols] = value_grad[:, :HD].astype(jnp.bfloat16)
 
 
 def spread_states(packed, reverse, counts):
@@ -170,6 +170,9 @@
             ].astype(f32)
 
     bf = jnp.bfloat16
+    grad_tiles = jnp.pad(
+        conv_grad.reshape(token_count, HEADS, HD), ((0, 0), (0, 0), (0, WIDTH - HD))
+    ).transpose(1, 0, 2)
     state_grad = pl.pallas_call(
         state_grad_kernel, out_shape=jax.ShapeDtypeStruct((PACKED, WIDTH), f32)
     )(q_tiles, g_tiles, state_b)
@@ -188,7 +191,7 @@
             jax.ShapeDtypeStruct(flat_shape, bf),
             jax.ShapeDtypeStruct(flat_shape, bf),
         ),
-    )(k_tiles, v_tiles, conv_grad.reshape(flat_shape), back_state)
+    )(k_tiles, v_tiles, grad_tiles, back_state)
     shape = queries.shape
     return (
         attended.reshape(shape),

time: 161 us -> 164 us (1.019)
  local copies, waits for them, and re-layouts: 2.04 us -> 5.47 us
    reshape x0 -> x2, local copies, waits for them, and re-layouts: none -> 2.26 us  [on_device_body(): conv_grad.reshape(token_count, HEADS, HD)]
  transfers between devices with their start and end apart: 4 -> 4, of which waited for: 3 -> 2; matrix products, arithmetic and copies ran while one was open for 5% -> 7% of each run, Pallas kernels for 11% -> 10%
where the time goes in v13:
time: 164 us; the launch traced here: 162 us
  blocking collectives  94.1 us (57%)
  Pallas kernels  24.5 us (15%)
  starting transfers between devices  16.1 us (10%)
  other arithmetic  10.9 us (7%)
  waiting for transfers between devices  9.9 us (6%)
  local copies, waits for them, and re-layouts  5.47 us (3%)
    all_gather x2, blocking collectives, spread_states(): return lax.all_gather(summed.astype(jnp.bfloat16), 'space', tiled=True)  52.5 us
    all_gather x2, blocking collectives, spread_states(): gathered = lax.all_gather(whole, 'orbit')  41.6 us
    all_to_all x2, starting transfers between devices, spread_states(): lax.all_to_all(packed.reshape(space, -1, WIDTH), 'space', 0, 0, tiled=True)  13 us
    all_to_all x2, waiting for transfers between devices, spread_states(): lax.all_to_all(packed.reshape(space, -1, WIDTH), 'space', 0, 0, tiled=True)  9.23 us
    pallas_call x1, Pallas kernels, on_device_body(): pl.pallas_call(forward_kernel, out_shape=(jax.ShapeDtypeStruct(flat_shape...  8.91 us
    pallas_call x1, Pallas kernels, on_device_body(): pl.pallas_call(tile_kernel, out_shape=(tile,) * 4)(q2, g2, k2, v2)  4.34 us
    pallas_call x1, Pallas kernels, on_device_body(): pl.pallas_call(state_grad_kernel, out_shape=jax.ShapeDtypeStruct((PACKED,...  3.87 us
    pallas_call x1, Pallas kernels, on_device_body(): pl.pallas_call(part_kernel, out_shape=jax.ShapeDtypeStruct((PACKED, WIDTH...  3.73 us
  transfers between devices with their start and end apart: 4, of which 2 were waited for; matrix products, arithmetic and copies ran while one was open for 7% of the time, Pallas kernels for 10%

profile of v13, /device:TPU:0, one launch (start us, length us, event | category | flops | bytes accessed | tf_op | source)
XLA Modules:
  0.0 161.9 jit_solution(16910641803522345920)
XLA Ops:
  0.6 1.3 fusion.4
  2.0 1.8 %collective-permute-start = (bf16[2,1,1,64,2240]{4,3,2,1,0:T(8,128)(2,1)S(1)}, bf16[2,1,1,64,2240]{4,3,2,1,0:T(8,128)(2,1)S(1)}, u32[]{:S(2)}, u32[]{:S(2)}) collective-permute-start(bf16[2,1,1,64,2240]{4,3,2,1,0:T(8,128)(2,1)S(1)} %get-tuple-element.31), channel_id=1, source_target_pairs={{0,1},{1,2},{2,3},{3,4},{4,5},{5,6},{6,7},{7,8},{8,9},{9,10},{10,1... | collective-permute-start | bytes 1720328 | tf_op jit(solution)/shard_map/ppermute | solution.py:17
  3.8 1.3 collective-permute-start.1
  5.1 3.7 %shard_map.85 = f32[2304,113]{1,0:T(8,128)} custom-call(bf16[128,2240]{1,0:T(8,128)(2,1)} %bitcast.35, bf16[128,2240]{1,0:T(8,128)(2,1)} %bitcast.24), custom_call_target="tpu_custom_call" | custom-call | tf_op jit(solution)/shard_map/pallas_call | solution.py:148
  8.8 8.2 %all-to-all-start = ((f32[16,144,113]{2,1,0:T(8,128)}), f32[16,144,113]{2,1,0:T(8,128)}, u32[]{:S(2)}, u32[]{:S(2)}) async-start(f32[16,144,113]{2,1,0:T(8,128)} %bitcast.31), calls=%async_computation | async-start | bytes 2359296 | tf_op jit(solution)/shard_map/all_to_all | solution.py:119
  17.1 0.0 copy-done.10
  17.1 0.7 convert_element_type.70
  17.7 4.3 %shard_map.84 = (bf16[20,128,128]{2,1,0:T(8,128)(2,1)}, bf16[20,128,128]{2,1,0:T(8,128)(2,1)}, bf16[20,128,128]{2,1,0:T(8,128)(2,1)}, bf16[20,128,128]{2,1,0:T(8,128)(2,1)}) custom-call(bf16[128,2240]{1,0:T(8,128)(2,1)} %bitcast.37, bf16[128,2240]{1,0:T(8,128)(2,1)} %bitcast.28, bf16[128,2240]{1,0:T(8,128)(2,1)} %bitcast.36, bf16[128,2240]{1,0:T(8,128)(2,1)} %bitcast.25), custom_call_target="tpu_custom_call" | custom-call | tf_op jit(solution)/shard_map/pallas_call | solution.py:152
  22.1 0.6 iota_compare_fusion.3
  22.7 1.8 %slice_reduce_fusion.8 = (f32[2240]{0:T(1024)S(1)}, f32[2240]{0:T(1024)}, f32[2240]{0:T(1024)}, f32[2240]{0:T(1024)}, f32[2240]{0:T(1024)}, /*index=5*/f32[2240]...) fusion(f32[3,3,2240]{2,1,0:T(4,128)} %convert_element_type.70), kind=kLoop, calls=%fused_computation.29 | loop fusion | bytes 161280 | tf_op jit(solution)/shard_map/slice | solution.py:165
  24.5 0.0 collective-permute-done
  24.5 0.7 collective-permute-done.1
  25.2 0.0 copy-done
  25.2 0.0 copy-done.1
  25.2 1.1 select_maximum_fusion
  26.3 0.2 slice_bitcast_fusion
  26.4 0.0 copy-start.11
  26.5 9.2 %all-to-all-done = f32[16,144,113]{2,1,0:T(8,128)} async-done(((f32[16,144,113]{2,1,0:T(8,128)}), f32[16,144,113]{2,1,0:T(8,128)}, u32[]{:S(2)}, u32[]{:S(2)}) %all-to-all-start) | async-done | bytes 1041440 | tf_op jit(solution)/shard_map/all_to_all | solution.py:119
  35.7 1.4 reduce_sum.36
  37.1 23.3 %all-gather = f32[2304,113]{1,0:T(8,128)S(1)} all-gather(f32[144,113]{1,0:T(8,128)S(1)} %reduce_sum.36), channel_id=2, replica_groups=mesh['orbit'=16,'space'=16] {'orbit'}, dimensions={0}, use_global_device_ids=true | all-gather | bytes 1106496 | tf_op jit(solution)/shard_map/all_gather | solution.py:123
  60.4 0.0 copy-done.11
  60.4 0.2 select_reduce_fusion.1
  60.6 25.9 %all_gather.18.s_ref = bf16[2304,113]{1,0:T(8,128)(2,1)} all-gather(bf16[144,113]{1,0:T(8,128)(2,1)S(1)} %divide_convert_fusion), channel_id=1, replica_groups=mesh['orbit'=16,'space'=16] {'space'}, dimensions={0}, use_global_device_ids=true | all-gather | bytes 553248 | tf_op jit(solution)/shard_map/all_gather | solution.py:132
  86.5 3.9 %shard_map.87 = f32[2304,113]{1,0:T(8,128)} custom-call(bf16[20,128,128]{2,1,0:T(8,128)(2,1)} %get-tuple-element.12.qt_ref, bf16[20,128,128]{2,1,0:T(8,128)(2,1)} %get-tuple-element.13.gt_ref, bf16[2304,113]{1,0:T(8,128)(2,1)} %all_gather.18.s_ref), custom_call_target="tpu_custom_call" | custom-call | tf_op jit(solution)/shard_map/pallas_call | solution.py:176
  90.3 0.0 copy-start.6
  90.4 0.0 copy-start.7
  90.4 0.0 copy-start.8
  90.4 0.0 copy-start.9
  90.4 4.8 %all-to-all-start.1 = ((f32[16,144,113]{2,1,0:T(8,128)}), f32[16,144,113]{2,1,0:T(8,128)}, u32[]{:S(2)}, u32[]{:S(2)}) async-start(f32[16,144,113]{2,1,0:T(8,128)} %bitcast.30), calls=%async_computation.1 | async-start | bytes 2359296 | tf_op jit(solution)/shard_map/all_to_all | solution.py:119
  95.1 0.0 copy-done.2
  95.2 0.0 copy-done.3
  95.2 0.0 copy-done.4
  95.2 0.0 copy-done.5
  95.2 0.0 copy-done.6
  95.2 0.0 copy-done.7
  95.2 0.0 copy-done.8
  95.2 2.1 %multiply_add_fusion = f32[1,2,64,2240]{3,2,1,0:T(8,128)} fusion(bf16[1,4,66,2240]{3,2,1,0:T(8,128)(2,1)S(1)} %get-tuple-element.29, f32[2240]{0:T(1024)S(1)} %copy-done.2, f32[2240]{0:T(1024)S(1)} %copy-done.3, f32[2240]{0:T(1024)S(1)} %copy-done.4, f32[2240]{0:T(1024)S(1)} %copy-done.5, f32[2240]{0:T(1024)S(1)} %copy-done.6, f32[2240]{0:T(1024)S(1)} %copy-done.7, ...), kind=kLoop, calls=%fused_computation.14 | loop fusion | flops 7454720 | bytes 6388480 | tf_op jit(solution)/shard_map/add | solution.py:168
  97.3 2.0 %reshape.96 = f32[128,20,112]{2,1,0:T(8,128)S(1)} reshape(f32[1,2,64,2240]{3,2,1,0:T(8,128)} %multiply_add_fusion) | data formatting | bytes 2293760 | tf_op jit(solution)/shard_map/reshape | solution.py:174
  99.3 0.3 copy.9
  99.6 1.2 pad_bitcast_fusion.c_ref
  100.7 2.1 %multiply_add_fusion.1 = f32[1,2,64,2240]{3,2,1,0:T(8,128)} fusion(bf16[1,4,66,2240]{3,2,1,0:T(8,128)(2,1)S(1)} %get-tuple-element.30, f32[2240]{0:T(1024)S(1)} %copy-done.2, f32[2240]{0:T(1024)S(1)} %copy-done.3, f32[2240]{0:T(1024)S(1)} %copy-done.4, f32[2240]{0:T(1024)S(1)} %copy-done.5, f32[2240]{0:T(1024)S(1)} %copy-done.6, f32[2240]{0:T(1024)S(1)} %copy-done.7, ...), kind=kLoop, calls=%fused_computation.16 | loop fusion | flops 7454720 | bytes 6388480 | tf_op jit(solution)/shard_map/add | solution.py:165
  102.8 8.9 %shard_map.86 = (bf16[128,2240]{1,0:T(8,128)(2,1)}, bf16[128,2240]{1,0:T(8,128)(2,1)}) custom-call(bf16[20,128,128]{2,1,0:T(8,128)(2,1)} %get-tuple-element.12.qt_ref, bf16[20,128,128]{2,1,0:T(8,128)(2,1)} %get-tuple-element.13.gt_ref, f32[128,2240]{1,0:T(8,128)} %bitcast.32, bf16[2304,113]{1,0:T(8,128)(2,1)} %all_gather.18.s_ref), custom_call_target="tpu_custom_call" | custom-call | tf_op jit(solution)/shard_map/pallas_call | solution.py:180
  111.7 0.0 all-to-all-done.1
  111.7 1.4 reduce_sum.38
  113.1 18.3 %all-gather.1 = f32[2304,113]{1,0:T(8,128)S(1)} all-gather(f32[144,113]{1,0:T(8,128)S(1)} %broadcast_divide_fusion), channel_id=3, replica_groups=mesh['orbit'=16,'space'=16] {'orbit'}, dimensions={0}, use_global_device_ids=true | all-gather | bytes 1106496 | tf_op jit(solution)/shard_map/all_gather | solution.py:129
  131.4 0.2 select_reduce_fusion
  131.6 26.6 %all_gather.20.s_ref = bf16[2304,113]{1,0:T(8,128)(2,1)} all-gather(bf16[144,113]{1,0:T(8,128)(2,1)S(1)} %select_reduce_fusion), channel_id=1, replica_groups=mesh['orbit'=16,'space'=16] {'space'}, dimensions={0}, use_global_device_ids=true | all-gather | bytes 553248 | tf_op jit(solution)/shard_map/all_gather | solution.py:132
  158.2 3.7 %shard_map.88 = (bf16[128,2240]{1,0:T(8,128)(2,1)}, bf16[128,2240]{1,0:T(8,128)(2,1)}) custom-call(bf16[20,128,128]{2,1,0:T(8,128)(2,1)} %get-tuple-element.16.kt_ref, bf16[20,128,128]{2,1,0:T(8,128)(2,1)} %get-tuple-element.17.vt_ref, f32[20,128,113]{2,1,0:T(8,128)} %pad_bitcast_fusion.c_ref, bf16[2304,113]{1,0:T(8,128)(2,1)} %all_gather.20.s_ref), custom_call_target="tpu_custom_call" | custom-call | tf_op jit(solution)/shard_map/pallas_call | solution.py:188
  (11 shorter events, 0.0 us)
Async XLA Ops:
  2.0 22.5 %collective-permute-start = (bf16[2,1,1,64,2240]{4,3,2,1,0:T(8,128)(2,1)S(1)}, bf16[2,1,1,64,2240]{4,3,2,1,0:T(8,128)(2,1)S(1)}, u32[]{:S(2)}, u32[]{:S(2)}) collective-permute-start(bf16[2,1,1,64,2240]{4,3,2,1,0:T(8,128)(2,1)S(1)} %get-tuple-element.31), channel_id=1, source_target_pairs={{0,1},{1,2},{2,3},{3,4},{4,5},{5,6},{6,7},{7,8},{8,9},{9,10},{10,1... | collective-permute-start | bytes 1720328 | tf_op jit(solution)/shard_map/ppermute | solution.py:17
  3.8 21.4 %collective-permute-start.1 = (bf16[2,1,1,64,2240]{4,3,2,1,0:T(8,128)(2,1)S(1)}, bf16[2,1,1,64,2240]{4,3,2,1,0:T(8,128)(2,1)S(1)}, u32[]{:S(2)}, u32[]{:S(2)}) collective-permute-start(bf16[2,1,1,64,2240]{4,3,2,1,0:T(8,128)(2,1)S(1)} %get-tuple-element.32), channel_id=1, source_target_pairs={{1,0},{2,1},{3,2},{4,3},{5,4},{6,5},{7,6},{8,7},{9,8},{10,9},{11,1... | collective-permute-start | bytes 1720328 | tf_op jit(solution)/shard_map/ppermute | solution.py:18
  8.8 8.3 %copy-start.10 = (bf16[3,3,2240]{2,1,0:T(4,128)(2,1)S(1)}, bf16[3,3,2240]{2,1,0:T(4,128)(2,1)}, u32[]{:S(2)}) copy-start(bf16[3,3,2240]{2,1,0:T(4,128)(2,1)} %param.8) | copy-start | bytes 120964
  8.8 26.9 %all-to-all-start = ((f32[16,144,113]{2,1,0:T(8,128)}), f32[16,144,113]{2,1,0:T(8,128)}, u32[]{:S(2)}, u32[]{:S(2)}) async-start(f32[16,144,113]{2,1,0:T(8,128)} %bitcast.31), calls=%async_computation | async-start | bytes 2359296 | tf_op jit(solution)/shard_map/all_to_all | solution.py:119
  17.7 7.4 %copy-start = (bf16[1,2,64,2240]{3,2,1,0:T(8,128)(2,1)S(1)}, bf16[1,2,64,2240]{3,2,1,0:T(8,128)(2,1)}, u32[]{:S(2)}) copy-start(bf16[1,2,64,2240]{3,2,1,0:T(8,128)(2,1)} %param.7) | copy-start | bytes 1720324
  17.7 7.4 %copy-start.1 = (bf16[1,2,64,2240]{3,2,1,0:T(8,128)(2,1)S(1)}, bf16[1,2,64,2240]{3,2,1,0:T(8,128)(2,1)}, u32[]{:S(2)}) copy-start(bf16[1,2,64,2240]{3,2,1,0:T(8,128)(2,1)} %param.9) | copy-start | bytes 1720324
  26.4 33.9 %copy-start.11 = (pred[16]{0:T(512)(128)(4,1)S(1)}, pred[16]{0:T(512)(128)(4,1)}, u32[]{:S(2)}) copy-start(pred[16]{0:T(512)(128)(4,1)} %iota_compare_fusion.3) | copy-start | bytes 52
  90.3 4.8 %copy-start.2 = (f32[2240]{0:T(1024)S(1)}, f32[2240]{0:T(1024)}, u32[]{:S(2)}) copy-start(f32[2240]{0:T(1024)} %get-tuple-element.21) | copy-start | bytes 26884
  90.3 4.8 %copy-start.3 = (f32[2240]{0:T(1024)S(1)}, f32[2240]{0:T(1024)}, u32[]{:S(2)}) copy-start(f32[2240]{0:T(1024)} %get-tuple-element.22) | copy-start | bytes 26884
  90.3 4.8 %copy-start.4 = (f32[2240]{0:T(1024)S(1)}, f32[2240]{0:T(1024)}, u32[]{:S(2)}) copy-start(f32[2240]{0:T(1024)} %get-tuple-element.23) | copy-start | bytes 26884
  90.3 4.8 %copy-start.5 = (f32[2240]{0:T(1024)S(1)}, f32[2240]{0:T(1024)}, u32[]{:S(2)}) copy-start(f32[2240]{0:T(1024)} %get-tuple-element.24) | copy-start | bytes 26884
  90.3 4.8 %copy-start.6 = (f32[2240]{0:T(1024)S(1)}, f32[2240]{0:T(1024)}, u32[]{:S(2)}) copy-start(f32[2240]{0:T(1024)} %get-tuple-element.25) | copy-start | bytes 26884
  90.4 4.8 %copy-start.7 = (f32[2240]{0:T(1024)S(1)}, f32[2240]{0:T(1024)}, u32[]{:S(2)}) copy-start(f32[2240]{0:T(1024)} %get-tuple-element.26) | copy-start | bytes 26884
  90.4 4.8 %copy-start.8 = (f32[2240]{0:T(1024)S(1)}, f32[2240]{0:T(1024)}, u32[]{:S(2)}) copy-start(f32[2240]{0:T(1024)} %get-tuple-element.27) | copy-start | bytes 26884
  90.4 4.8 %copy-start.9 = (f32[2240]{0:T(1024)S(1)}, f32[2240]{0:T(1024)}, u32[]{:S(2)}) copy-start(f32[2240]{0:T(1024)} %get-tuple-element.28) | copy-start | bytes 26884
  90.4 21.3 %all-to-all-start.1 = ((f32[16,144,113]{2,1,0:T(8,128)}), f32[16,144,113]{2,1,0:T(8,128)}, u32[]{:S(2)}, u32[]{:S(2)}) async-start(f32[16,144,113]{2,1,0:T(8,128)} %bitcast.30), calls=%async_computation.1 | async-start | bytes 2359296 | tf_op jit(solution)/shard_map/all_to_all | solution.py:119
